TPU v7x, 128 devices: a whole 4x4x4 slice. The times are simulated.
128 devices in a mesh: wide: 64 (over z, y, x), narrow: 2 (over core).
Axes of the slice: x: 4, y: 4, z: 4, core: 2. Of those that a mesh axis runs over, the one named last changes fastest.
Arguments:
- tokens: bfloat16 [65536, 2048], P('wide', 'narrow'), may hold values from -6 to 6
- attn_gain: bfloat16 [2048], replicated, may hold values from 0.5 to 1.5
- q_weight: bfloat16 [2048, 3072], P('wide', 'narrow'), may hold values from -6 to 6
- kva_weight: bfloat16 [2048, 576], P('wide'), may hold values from -0.125 to 0.125
- kv_gain: bfloat16 [512], replicated, may hold values from 0.5 to 1.5
- kvb_weight: bfloat16 [512, 4096], P(None, 'narrow'), may hold values from -0.25 to 0.25
- o_weight: bfloat16 [2048, 2048], P('narrow'), may hold values from -0.125 to 0.125
- adapter_down: bfloat16 [2048, 1024], P(None, 'narrow'), may hold values from -0.125 to 0.125
- adapter_up_weight: bfloat16 [1024, 3072], P(None, 'narrow'), may hold values from -1.5 to 1.5
- lengths: int32 [64, 4], P('wide'), may hold values from 1 to 512, 1024 in all within a row
- adapter_ids: int32 [64, 4], P('wide'), may hold values from 0 to 63
- adapter_slot: int32 [64], replicated, may hold values from 0 to 63, each once
Outputs:
- hidden: bfloat16 [65536, 2048], P('wide', 'narrow')
- latent_cache: bfloat16 [65536, 576], P('wide')
Inputs may be any that keep to these rules, and one draw needn't show every extreme that they name: Each row of lengths sums to 1024, and its longest prompt is exactly 512.
All inputs are finite; a program needn't handle non-finite values.
Results may differ from a plain program's by a relative error of at most 0.0095.
The roundings to bfloat16 on the way count: a program that leaves them out, or rounds other values in their place, can miss the bound.
Values may be sent and summed in bfloat16 or wider, within the bound.
No kernel may reach another device: no remote copies, remote signals or barrier semaphores. Data moves between devices by JAX's collectives and lax.ppermute only.
A program may use at most 192 MiB of HBM per device.

v0:
```python
import jax
import jax.numpy as jnp
from jax import lax
from jax.sharding import PartitionSpec as P

NOPE = 128
ROPE = 64
VDIM = 128
LATENT = 512
RANK = 16


EPS = 1e-06
THETA = 50000.0
ADAPTER_SCALE = 2.0


def rms_scale(values, gain):
    mean_sq = jnp.mean(values * values, axis=-1, keepdims=True)
    return values * lax.rsqrt(mean_sq + EPS) * gain.astype(jnp.float32)


def rotate(values, positions):
    half = values.shape[-1] // 2
    freqs = jnp.exp(-jnp.log(THETA) * 2.0 * jnp.arange(half).astype(jnp.float32) / (2 * half))
    angle = positions.astype(jnp.float32)[:, None] * freqs[None, :]
    cosine = jnp.cos(angle)
    sine = jnp.sin(angle)
    if values.ndim == 3:
        cosine = cosine[:, None, :]
        sine = sine[:, None, :]
    first = values[..., :half]
    second = values[..., half:]
    return jnp.concatenate(
        [first * cosine - second * sine, first * sine + second * cosine], axis=-1
    )


def token_tables(length_row, id_row, adapter_slot, local_pos):
    ends = jnp.cumsum(length_row)
    starts = ends - length_row
    prompt = jnp.sum((ends[None, :] <= local_pos[:, None]).astype(jnp.int32), axis=1)
    onehot = (prompt[:, None] == jnp.arange(length_row.shape[0])[None, :]).astype(jnp.int32)
    position = local_pos - jnp.sum(onehot * starts[None, :], axis=1)
    adapter = jnp.sum(onehot * id_row[None, :], axis=1)
    slot_hot = (adapter[:, None] == jnp.arange(adapter_slot.shape[0])[None, :]).astype(jnp.int32)
    slot = jnp.sum(slot_hot * adapter_slot[None, :], axis=1)
    return (prompt, position, adapter, slot)


def pick_columns(stored, first_slots, prompts_here):
    blocks = [
        lax.dynamic_slice_in_dim(stored, first_slots[prompt_index] * RANK, RANK, 1)
        for prompt_index in range(prompts_here)
    ]
    return jnp.concatenate(blocks, axis=1)


def body(
    tokens,
    attn_gain,
    q_weight,
    kva_weight,
    kv_gain,
    kvb_weight,
    o_weight,
    adapter_down,
    adapter_up_weight,
    lengths,
    adapter_ids,
    adapter_slot,
):
    rows = tokens.shape[0]
    heads_here = o_weight.shape[0] // VDIM
    prompts_here = lengths.shape[1]
    whole = lax.all_gather(tokens, "narrow", axis=1, tiled=True)
    normed = rms_scale(whole.astype(jnp.float32), attn_gain).astype(jnp.bfloat16)
    local_pos = jnp.arange(rows)
    prompt, position, adapter, slot = token_tables(
        lengths[0], adapter_ids[0], adapter_slot, local_pos
    )
    query_vectors = jnp.dot(
        normed,
        lax.all_gather(q_weight, "wide", axis=0, tiled=True),
        preferred_element_type=jnp.float32,
    )
    kv_pre = jnp.dot(
        normed,
        lax.all_gather(kva_weight, "wide", axis=0, tiled=True),
        preferred_element_type=jnp.float32,
    )
    prompt_ids = adapter_ids[0]
    id_hot = (prompt_ids[:, None] == jnp.arange(adapter_slot.shape[0])[None, :]).astype(jnp.int32)
    prompt_position_slot = jnp.sum(id_hot * adapter_slot[None, :], axis=1)
    member = (prompt[:, None] == jnp.arange(prompts_here)[None, :]).astype(jnp.float32)
    stored = lax.all_gather(adapter_down, "narrow", axis=1, tiled=True)
    chosen = pick_columns(stored, prompt_position_slot, prompts_here)
    low = jnp.dot(normed, chosen, preferred_element_type=jnp.float32).reshape(
        rows, prompts_here, RANK
    )
    lowrank = jnp.sum(low * member[:, :, None], axis=1).astype(jnp.bfloat16)
    up_blocks = [
        lax.dynamic_slice_in_dim(adapter_up_weight, prompt_ids[prompt_index] * RANK, RANK, 0)
        for prompt_index in range(prompts_here)
    ]
    up_weight_rows = jnp.concatenate(up_blocks, axis=0)
    spread_rows = (member.astype(jnp.bfloat16)[:, :, None] * lowrank[:, None, :]).reshape(
        rows, prompts_here * RANK
    )
    query_vectors = query_vectors + ADAPTER_SCALE * jnp.dot(
        spread_rows, up_weight_rows, preferred_element_type=jnp.float32
    )
    query_vectors = query_vectors.reshape(rows, heads_here, NOPE + ROPE)
    query_vectors = jnp.concatenate(
        [query_vectors[..., :NOPE], rotate(query_vectors[..., NOPE:], position)], axis=-1
    ).astype(jnp.bfloat16)
    latent = rms_scale(kv_pre[:, :LATENT], kv_gain).astype(jnp.bfloat16)
    key_rope = rotate(kv_pre[:, LATENT:], position).astype(jnp.bfloat16)
    latent_cache = jnp.concatenate([latent, key_rope], axis=1)
    expanded = jnp.dot(latent, kvb_weight, preferred_element_type=jnp.float32).astype(jnp.bfloat16)
    expanded = expanded.reshape(rows, heads_here, NOPE + VDIM)
    key_nope = expanded[..., :NOPE]
    values = expanded[..., NOPE:]
    scale = 1.0 / jnp.sqrt(jnp.float32(NOPE + ROPE))
    scores = jnp.einsum(
        "qhd,khd->hqk", query_vectors[..., :NOPE], key_nope, preferred_element_type=jnp.float32
    )
    scores = scores + jnp.einsum(
        "qhd,kd->hqk", query_vectors[..., NOPE:], key_rope, preferred_element_type=jnp.float32
    )
    scores = scores * scale
    allowed = (prompt[None, :] == prompt[:, None]) & (local_pos[None, :] <= local_pos[:, None])
    scores = jnp.where(allowed[None, :, :], scores, jnp.float32(-1e30))
    top = jnp.max(scores, axis=-1, keepdims=True)
    expo = jnp.exp(scores - top)
    weights = (expo / jnp.sum(expo, axis=-1, keepdims=True)).astype(jnp.bfloat16)
    attended = jnp.einsum(
        "hqk,khd->qhd", weights, values, preferred_element_type=jnp.float32
    ).astype(jnp.bfloat16)
    attended = attended.reshape(rows, heads_here * VDIM)
    partial_out = jnp.dot(attended, o_weight, preferred_element_type=jnp.float32)
    projected = lax.psum_scatter(
        partial_out.astype(jnp.bfloat16), "narrow", scatter_dimension=1, tiled=True
    ).astype(jnp.float32)
    hidden = (tokens.astype(jnp.float32) + projected).astype(jnp.bfloat16)
    return (hidden, latent_cache)


def solution(mesh):
    return jax.shard_map(
        body,
        mesh=mesh,
        in_specs=(
            P("wide", "narrow"),
            P(),
            P("wide", "narrow"),
            P("wide", None),
            P(),
            P(None, "narrow"),
            P("narrow", None),
            P(None, "narrow"),
            P(None, "narrow"),
            P("wide", None),
            P("wide", None),
            P(),
        ),
        out_specs=(P("wide", "narrow"), P("wide", None)),
        check_vma=False,
    )
```

profile of v0, /device:TPU:1, one launch (start us, length us, event | category | flops | bytes accessed | tf_op | source)
XLA Modules:
  0.0 301.0 jit_solution(9721617435012271668)
XLA Ops:
  7.2 0.0 copy-start
  7.2 0.0 copy-start.10
  7.2 0.0 copy-start.14
  7.2 0.0 copy-start.15
  7.2 0.0 copy-start.12
  7.2 0.0 copy-start.11
  7.2 0.0 all-gather.5.cloned.1.call-start
  7.3 0.7 all-gather.5.cloned.1.call-update
  8.0 0.0 all-gather.11.cloned.1.call-start
  8.0 0.7 all-gather.11.cloned.1.call-update
  8.7 0.0 all-gather.7.cloned.1.call-start
  8.8 0.7 all-gather.7.cloned.1.call-update
  9.5 0.0 all-gather.9.cloned.1.call-start
  9.5 0.5 all-gather.9.cloned.1.call-update
  10.0 0.0 reduce-scatter.2.cloned.1.call-start
  10.1 0.0 copy-done.10
  10.1 0.0 copy-done.14
  10.1 0.2 select_reduce_fusion.1
  10.3 0.6 fusion.47
  13.5 0.7 fusion.46
  16.5 0.0 copy-done.15
  16.5 0.2 reduce-window.4
  16.7 0.0 copy-done.12
  16.7 0.0 copy-done.11
  16.8 0.5 multiply_exponential_fusion
  17.3 0.1 convert_reduce_fusion
  17.4 0.1 select_reduce_fusion
  17.5 1.6 constant_dynamic-slice_fusion.3
  19.1 0.6 fusion.7
  19.7 10.1 %all-gather.5.cloned.1.call-done = bf16[1024,2048]{1,0:T(8,128)(2,1)} async-done(((bf16[1024,1024]{1,0:T(8,128)(2,1)}), bf16[1024,2048]{1,0:T(8,128)(2,1)}) %all-gather.5.cloned.1.call-update) | async-done | bytes 4194320 | tf_op jit(solution)/shard_map/all_gather | solution.py:76
  29.8 3.1 %fusion.4 = f32[1024]{0:T(1024)S(1)} fusion(bf16[1024,2048]{1,0:T(8,128)(2,1)} %all-gather.5.cloned.1.call-done), kind=kLoop, calls=%fused_computation.9 | loop fusion | flops 6290432 | bytes 4198400 | tf_op jit(solution)/shard_map/reduce_sum | solution.py:19
  32.9 16.3 %all-gather.11.cloned.1.call-done = bf16[2048,1024]{1,0:T(8,128)(2,1)} async-done(((bf16[2048,512]{1,0:T(8,128)(2,1)}), bf16[2048,1024]{1,0:T(8,128)(2,1)}) %all-gather.11.cloned.1.call-update) | async-done | bytes 4194320 | tf_op jit(solution)/shard_map/all_gather | solution.py:96
  49.2 2.4 constant_dynamic-slice_fusion.7
  51.5 0.5 copy-done.2
  52.0 2.0 fusion.17
  54.2 64.3 %all-gather.7.cloned.1.call-done = bf16[2048,576]{1,0:T(8,128)(2,1)} async-done(((bf16[32,576]{1,0:T(8,128)(2,1)}), bf16[2048,576]{1,0:T(8,128)(2,1)}) %all-gather.7.cloned.1.call-update) | async-done | bytes 2359312 | tf_op jit(solution)/shard_map/all_gather | solution.py:89
  118.5 5.7 %fusion.43 = f32[1024,576]{0,1:T(8,128)S(1)} fusion(bf16[2048,576]{1,0:T(8,128)(2,1)} %all-gather.7.cloned.1.call-done, bf16[1024,2048]{1,0:T(8,128)(2,1)} %all-gather.5.cloned.1.call-done, f32[2048]{0:T(1024)S(1)} %convert_element_type.88, f32[1024]{0:T(1024)S(1)} %add_rsqrt_fusion.1), kind=kOutput, calls=%fused_computation.81 | convolution fusion | flops 2424307712 | bytes 8925184 | tf_op jit(solution)/shard_map/dot_general | solution.py:87
  124.2 0.2 multiply_reduce_fusion
  124.4 0.2 multiply_convert_fusion
  124.6 0.0 copy-done
  124.6 0.0 copy-start.3
  124.6 2.4 convolution_convert_fusion
  127.0 0.0 copy-done.3
  127.0 0.0 copy-start.13
  127.0 1.5 copy.40
  128.5 0.0 copy-done.13
  128.5 1.2 subtract_convert_fusion.1
  129.8 1.6 fusion.45
  131.4 60.1 %all-gather.9.cloned.1.call-done = bf16[2048,1536]{1,0:T(8,128)(2,1)} async-done(((bf16[32,1536]{1,0:T(8,128)(2,1)}), bf16[2048,1536]{1,0:T(8,128)(2,1)}) %all-gather.9.cloned.1.call-update) | async-done | bytes 6291472 | tf_op jit(solution)/shard_map/all_gather | solution.py:84
  191.4 10.1 %fusion.41 = f32[1024,1536]{1,0:T(8,128)S(1)} fusion(bf16[2048,1536]{1,0:T(8,128)(2,1)} %all-gather.9.cloned.1.call-done, bf16[1024,2048]{1,0:T(8,128)(2,1)} %all-gather.5.cloned.1.call-done, f32[2048]{0:T(1024)S(1)} %convert_element_type.88, f32[1024]{0:T(1024)S(1)} %add_rsqrt_fusion.1), kind=kOutput, calls=%fused_computation.80 | convolution fusion | flops 6450839552 | bytes 16789504 | tf_op jit(solution)/shard_map/dot_general | solution.py:82
  201.6 0.0 copy-done.6
  201.6 0.0 copy-done.7
  201.6 3.7 %multiply_add_fusion = f32[1024,1536]{1,0:T(8,128)} fusion(f32[1024,1536]{1,0:T(8,128)S(1)} %fusion.41, bf16[1024,64]{0,1:T(8,128)(2,1)S(1)} %bitcast.47, bf16[16,1536]{1,0:T(8,128)(2,1)S(1)} %copy-done.8, bf16[16,1536]{1,0:T(8,128)(2,1)S(1)} %copy-done.9, bf16[16,1536]{1,0:T(8,128)(2,1)S(1)} %copy-done.7, bf16[16,1536]{1,0:T(8,128)(2,1)S(1)} %copy-done.6), kind=kOutput, calls=%fused_computation.12 | convolution fusion | flops 205258752 | bytes 12910592 | tf_op jit(solution)/shard_map/dot_general | solution.py:110
  205.3 6.7 %copy.32 = f32[1024,1536]{0,1:T(8,128)} copy(f32[1024,1536]{1,0:T(8,128)} %multiply_add_fusion) | data formatting | bytes 12582912 | tf_op jit(solution)/shard_map/add | solution.py:110
  212.0 1.9 subtract_convert_fusion
  213.8 13.4 %fusion.13 = f32[1024,1024,8]{1,0,2:T(8,128)} fusion(bf16[1024,8,32]{0,2,1:T(8,128)(2,1)S(1)} %get-tuple-element.3, bf16[1024,8,32]{0,2,1:T(8,128)(2,1)S(1)} %get-tuple-element.2, bf16[1024,32]{0,1:T(8,128)(2,1)S(1)} %get-tuple-element.15, bf16[1024,32]{0,1:T(8,128)(2,1)S(1)} %get-tuple-element.14), kind=kOutput, calls=%fused_computation.25 | convolution fusion | flops 1076101120 | bytes 34734080 | tf_op jit(solution)/shard_map/qhd,kd->hqk/dot_general | solution.py:128
  227.2 26.8 %fusion.48 = (f32[8,1024]{1,0:T(8,128)S(1)}, f32[8,1024,1024]{1,2,0:T(8,128)}) fusion(f32[1024,1024,8]{1,0,2:T(8,128)} %fusion.13, pred[1024,1024]{0,1:T(8,128)(4,1)S(1)} %fusion.7, f32[1024,8,192]{0,2,1:T(8,128)} %bitcast.44, bf16[1024,8,128]{2,1,0:T(8,128)(2,1)S(1)} %get-tuple-element.5), kind=kOutput, calls=%fused_computation.85 | convolution fusion | flops 2189427712 | bytes 72384512 | tf_op jit(solution)/shard_map/sub | solution.py:135
  254.0 12.7 %fusion.10 = bf16[8,128,1024]{2,1,0:T(8,128)(2,1)S(1)} fusion(f32[8,1024,1024]{1,2,0:T(8,128)} %get-tuple-element.29, f32[8,1024]{1,0:T(8,128)S(1)} %get-tuple-element.28, bf16[1024,8,128]{2,1,0:T(8,128)(2,1)} %get-tuple-element.4), kind=kOutput, calls=%fused_computation.23 | convolution fusion | flops 2165309440 | bytes 37781504 | tf_op jit(solution)/shard_map/hqk,khd->qhd/dot_general | solution.py:137
  266.7 8.3 %convolution_convert_fusion.1 = bf16[1024,2048]{1,0:T(8,128)(2,1)} fusion(bf16[1024,1024]{0,1:T(8,128)(2,1)S(1)} %bitcast.52, bf16[1024,2048]{1,0:T(8,128)(2,1)} %param.18), kind=kOutput, calls=%fused_computation.18 | convolution fusion | flops 4297064448 | bytes 10485760 | tf_op jit(solution)/shard_map/dot_general | solution.py:141
  275.0 0.0 reduce-scatter.2.cloned.1.call-update
  275.1 1.2 copy-done.4
  276.3 1.1 pad_maximum_fusion
  277.4 12.6 %reduce-scatter.2.cloned.1.call-done = bf16[1024,1024]{1,0:T(8,128)(2,1)} async-done(((bf16[1024,2048]{1,0:T(8,128)(2,1)}), bf16[1024,1024]{1,0:T(8,128)(2,1)}) %reduce-scatter.2.cloned.1.call-update) | async-done | bytes 2097168 | tf_op jit(solution)/shard_map/reduce_scatter | solution.py:142
  289.9 4.5 %add_convert_fusion = bf16[1024,1024]{1,0:T(8,128)(2,1)} fusion(bf16[1024,1024]{1,0:T(8,128)(2,1)} %reduce-scatter.2.cloned.1.call-done, bf16[1024,1024]{1,0:T(8,128)(2,1)} %param.12), kind=kLoop, calls=%fused_computation.14 | loop fusion | flops 4194304 | bytes 6291456 | tf_op jit(solution)/shard_map/convert_element_type | solution.py:145
  (21 shorter events, 0.1 us)
Async XLA Ops:
  7.2 117.4 %copy-start = (bf16[512,2048]{1,0:T(8,128)(2,1)S(1)}, bf16[512,2048]{1,0:T(8,128)(2,1)}, u32[]{:S(2)}) copy-start(bf16[512,2048]{1,0:T(8,128)(2,1)} %param.17) | copy-start | bytes 6291460
  7.2 2.9 copy-start.10
  7.2 2.9 copy-start.14
  7.2 9.3 %copy-start.15 = (s32[1,4]{1,0:T(1,128)S(1)}, s32[1,4]{1,0:T(1,128)}, u32[]{:S(2)}) copy-start(s32[1,4]{1,0:T(1,128)} %param.21) | copy-start | bytes 52
  7.2 9.5 %copy-start.12 = (bf16[512]{0:T(512)(128)(2,1)S(1)}, bf16[512]{0:T(512)(128)(2,1)}, u32[]{:S(2)}) copy-start(bf16[512]{0:T(512)(128)(2,1)} %param.16) | copy-start | bytes 3076
  7.2 9.5 %copy-start.11 = (bf16[2048]{0:T(1024)(128)(2,1)S(1)}, bf16[2048]{0:T(1024)(128)(2,1)}, u32[]{:S(2)}) copy-start(bf16[2048]{0:T(1024)(128)(2,1)} %param.13) | copy-start | bytes 12292
  7.2 22.5 %all-gather.5.cloned.1.call-start = ((), (), s32[]{:S(2)}) async-start(), calls=%async_computation.1 | async-start | bytes 6291456 | tf_op jit(solution)/shard_map/all_gather | solution.py:76
  8.0 41.2 %all-gather.11.cloned.1.call-start = ((), (), s32[]{:S(2)}) async-start(), calls=%async_computation.4 | async-start | bytes 6291456 | tf_op jit(solution)/shard_map/all_gather | solution.py:96
  8.7 109.8 %all-gather.7.cloned.1.call-start = ((), (), s32[]{:S(2)}) async-start(), calls=%async_computation.2 | async-start | bytes 2662400 | tf_op jit(solution)/shard_map/all_gather | solution.py:89
  9.5 182.0 %all-gather.9.cloned.1.call-start = ((), (), s32[]{:S(2)}) async-start(), calls=%async_computation.3 | async-start | bytes 6389760 | tf_op jit(solution)/shard_map/all_gather | solution.py:84
  10.0 279.9 %reduce-scatter.2.cloned.1.call-start = ((), (), s32[]{:S(2)}) async-start(), calls=%async_computation.5 | async-start | bytes 6291456 | tf_op jit(solution)/shard_map/reduce_scatter | solution.py:142
  49.2 2.9 copy-start.2
  124.6 2.4 copy-start.3
  127.0 1.5 copy-start.13
  191.4 10.2 %copy-start.6 = (bf16[16,1536]{1,0:T(8,128)(2,1)S(1)}, bf16[16,1536]{1,0:T(8,128)(2,1)}, u32[]{:S(2)}) copy-start(bf16[16,1536]{1,0:T(8,128)(2,1)} %get-tuple-element.10) | copy-start | bytes 147460
  191.4 10.2 %copy-start.7 = (bf16[16,1536]{1,0:T(8,128)(2,1)S(1)}, bf16[16,1536]{1,0:T(8,128)(2,1)}, u32[]{:S(2)}) copy-start(bf16[16,1536]{1,0:T(8,128)(2,1)} %get-tuple-element.11) | copy-start | bytes 147460
  191.4 10.2 %copy-start.8 = (bf16[16,1536]{1,0:T(8,128)(2,1)S(1)}, bf16[16,1536]{1,0:T(8,128)(2,1)}, u32[]{:S(2)}) copy-start(bf16[16,1536]{1,0:T(8,128)(2,1)} %get-tuple-element.12) | copy-start | bytes 147460
  191.4 10.2 %copy-start.9 = (bf16[16,1536]{1,0:T(8,128)(2,1)S(1)}, bf16[16,1536]{1,0:T(8,128)(2,1)}, u32[]{:S(2)}) copy-start(bf16[16,1536]{1,0:T(8,128)(2,1)} %get-tuple-element.13) | copy-start | bytes 147460
  205.3 6.7 %copy-start.5 = (f32[1024,32]{0,1:T(8,128)S(1)}, f32[1024,32]{0,1:T(8,128)}, u32[]{:S(2)}) copy-start(f32[1024,32]{0,1:T(8,128)} %get-tuple-element.17) | copy-start | bytes 393220
  275.0 1.2 copy-start.4
  276.3 18.2 %copy-start.1 = (bf16[512,2048]{1,0:T(8,128)(2,1)S(1)}, bf16[512,2048]{1,0:T(8,128)(2,1)}, u32[]{:S(2)}) copy-start(bf16[512,2048]{1,0:T(8,128)(2,1)} %param.17) | copy-start | bytes 6291460
Sparse Core Ops, SparseCore 0:
  9.7 20.0 all-gather.4
  31.4 17.6 all-gather.10
  52.1 66.3 all-gather.6
  121.1 70.3 all-gather.8
  275.2 14.6 reduce-scatter.1
where the time goes:
time: 301 us
  waiting for transfers between devices  166 us (55%)
  matrix products  85.1 us (28%)
  between operations  19.1 us (6%)
  local copies, waits for them, and re-layouts  16.7 us (6%)
  other arithmetic  13.9 us (5%)
    all_gather x1, waiting for transfers between devices, body(): lax.all_gather(kva_weight, 'wide', axis=0, tiled=True)  64.3 us
    all_gather x1, waiting for transfers between devices, body(): lax.all_gather(q_weight, 'wide', axis=0, tiled=True)  60.1 us
    sub x1, matrix products, body(): expo = jnp.exp(scores - top)  26.8 us
    all_gather x1, waiting for transfers between devices, body(): stored = lax.all_gather(adapter_down, 'narrow', axis=1, tiled=True)  16.3 us
    dot_general x1, matrix products, body(): jnp.einsum('qhd,kd->hqk', query_vectors[..., NOPE:], key_rope, preferred_...  13.4 us
    dot_general x1, matrix products, body(): jnp.einsum('hqk,khd->qhd', weights, values, preferred_element_type=jnp.fl...  12.7 us
    reduce_scatter x1, waiting for transfers between devices, body(): lax.psum_scatter(partial_out.astype(jnp.bfloat16), 'narrow', scatter_dime...  12.6 us
    dot_general x1, matrix products, body(): jnp.dot(normed, lax.all_gather(q_weight, 'wide', axis=0, tiled=True), pre...  10.1 us
  transfers between devices with their start and end apart: 5, of which 5 were waited for; matrix products, arithmetic and copies ran while one was open for 9% of the time, Pallas kernels for 0%

commit v1 on v0

--- a/solution.py
+++ b/solution.py
@@ -48,12 +48,8 @@
     return (prompt, position, adapter, slot)
 
 
-def pick_columns(stored, first_slots, prompts_here):
-    blocks = [
-        lax.dynamic_slice_in_dim(stored, first_slots[prompt_index] * RANK, RANK, 1)
-        for prompt_index in range(prompts_here)
-    ]
-    return jnp.concatenate(blocks, axis=1)
+def swap(values):
+    return lax.ppermute(values, "narrow", perm=[(0, 1), (1, 0)])
 
 
 def body(
@@ -71,30 +67,47 @@
     adapter_slot,
 ):
     rows = tokens.shape[0]
+    half_width = tokens.shape[1]
     heads_here = o_weight.shape[0] // VDIM
     prompts_here = lengths.shape[1]
-    whole = lax.all_gather(tokens, "narrow", axis=1, tiled=True)
+    q_cols = q_weight.shape[1]
+    me = lax.axis_index("narrow")
+    mine_first = me == 0
+
+    joined = jnp.concatenate([q_weight, kva_weight], axis=1)
+    joined = lax.all_gather(joined, "wide", axis=0, tiled=True)
+
+    other = swap(tokens)
+    whole = jnp.concatenate(
+        [jnp.where(mine_first, tokens, other), jnp.where(mine_first, other, tokens)], axis=1
+    )
+
+    slots_here = adapter_down.shape[1] // RANK
+    prompt_ids = adapter_ids[0]
+    id_hot = (prompt_ids[:, None] == jnp.arange(adapter_slot.shape[0])[None, :]).astype(jnp.int32)
+    prompt_slot = jnp.sum(id_hot * adapter_slot[None, :], axis=1)
+    owner = prompt_slot // slots_here
+    local_slot = prompt_slot % slots_here
+    picked = jnp.concatenate(
+        [
+            lax.dynamic_slice_in_dim(adapter_down, local_slot[p] * RANK, RANK, 1)
+            for p in range(prompts_here)
+        ],
+        axis=1,
+    )
+    picked_other = swap(picked)
+    own_block = jnp.repeat(owner == me, RANK)
+    chosen = jnp.where(own_block[None, :], picked, picked_other)
+
     normed = rms_scale(whole.astype(jnp.float32), attn_gain).astype(jnp.bfloat16)
     local_pos = jnp.arange(rows)
     prompt, position, adapter, slot = token_tables(
         lengths[0], adapter_ids[0], adapter_slot, local_pos
     )
-    query_vectors = jnp.dot(
-        normed,
-        lax.all_gather(q_weight, "wide", axis=0, tiled=True),
-        preferred_element_type=jnp.float32,
-    )
-    kv_pre = jnp.dot(
-        normed,
-        lax.all_gather(kva_weight, "wide", axis=0, tiled=True),
-        preferred_element_type=jnp.float32,
-    )
-    prompt_ids = adapter_ids[0]
-    id_hot = (prompt_ids[:, None] == jnp.arange(adapter_slot.shape[0])[None, :]).astype(jnp.int32)
-    prompt_position_slot = jnp.sum(id_hot * adapter_slot[None, :], axis=1)
+    projections = jnp.dot(normed, joined, preferred_element_type=jnp.float32)
+    query_vectors = projections[:, :q_cols]
+    kv_pre = projections[:, q_cols:]
     member = (prompt[:, None] == jnp.arange(prompts_here)[None, :]).astype(jnp.float32)
-    stored = lax.all_gather(adapter_down, "narrow", axis=1, tiled=True)
-    chosen = pick_columns(stored, prompt_position_slot, prompts_here)
     low = jnp.dot(normed, chosen, preferred_element_type=jnp.float32).reshape(
         rows, prompts_here, RANK
     )
@@ -138,10 +151,12 @@
         "hqk,khd->qhd", weights, values, preferred_element_type=jnp.float32
     ).astype(jnp.bfloat16)
     attended = attended.reshape(rows, heads_here * VDIM)
-    partial_out = jnp.dot(attended, o_weight, preferred_element_type=jnp.float32)
-    projected = lax.psum_scatter(
-        partial_out.astype(jnp.bfloat16), "narrow", scatter_dimension=1, tiled=True
-    ).astype(jnp.float32)
+    their_cols = lax.dynamic_slice_in_dim(o_weight, (1 - me) * half_width, half_width, 1)
+    my_cols = lax.dynamic_slice_in_dim(o_weight, me * half_width, half_width, 1)
+    theirs = jnp.dot(attended, their_cols, preferred_element_type=jnp.float32).astype(jnp.bfloat16)
+    received = swap(theirs)
+    mine = jnp.dot(attended, my_cols, preferred_element_type=jnp.float32).astype(jnp.bfloat16)
+    projected = mine.astype(jnp.float32) + received.astype(jnp.float32)
     hidden = (tokens.astype(jnp.float32) + projected).astype(jnp.bfloat16)
     return (hidden, latent_cache)
 

time: 301 us -> 206 us (0.68)
  waiting for transfers between devices: 166 us -> 65.8 us
  matrix products: 85.1 us -> 90.3 us
  local copies, waits for them, and re-layouts: 16.7 us -> 12.5 us
    all_gather x4 -> x1, waiting for transfers between devices: 151 us -> 62.8 us  [body(): joined = lax.all_gather(joined, 'wide', axis=0, tiled=True)]
    reduce_scatter x1 -> x0, waiting for transfers between devices: 12.6 us -> none  [body(): lax.psum_scatter(partial_out.astype(jnp.bfloat16), 'narrow', scatter_dime...]
    add x1 -> x0, local copies, waits for them, and re-layouts: 6.66 us -> none  [body(): query_vectors + ADAPTER_SCALE * jnp.dot(spread_rows, up_weight_rows, pref...]
    dot_general x3, matrix products: 24.2 us -> 29.7 us  [the longest x1 16.1 us: body(): projections = jnp.dot(normed, joined, preferred_element_type=jnp.float32)]
    convert_element_type x1 -> x0, other arithmetic: 4.5 us -> none  [body(): hidden = (tokens.astype(jnp.float32) + projected).astype(jnp.bfloat16)]
    concatenate x0 -> x2, other arithmetic: none -> 3.19 us  [the longest x1 1.71 us: body(): joined = jnp.concatenate([q_weight, kva_weight], axis=1)]
    ppermute x0 -> x3, waiting for transfers between devices: none -> 3.04 us  [swap(): return lax.ppermute(values, 'narrow', perm=[(0, 1), (1, 0)])]
  transfers between devices with their start and end apart: 5 -> 4, of which waited for: 5 -> 2; matrix products, arithmetic and copies ran while one was open for 9% -> 8% of each run, Pallas kernels for 0% -> 0%
where the time goes in v1:
time: 206 us; the launch traced here: 205 us
  matrix products  90.3 us (44%)
  waiting for transfers between devices  65.8 us (32%)
  between operations  19.2 us (9%)
  other arithmetic  15.3 us (7%)
  local copies, waits for them, and re-layouts  12.5 us (6%)
  starting transfers between devices  2.21 us (1%)
    all_gather x1, waiting for transfers between devices, body(): joined = lax.all_gather(joined, 'wide', axis=0, tiled=True)  62.8 us
    sub x1, matrix products, body(): expo = jnp.exp(scores - top)  26.8 us
    dot_general x1, matrix products, body(): projections = jnp.dot(normed, joined, preferred_element_type=jnp.float32)  16.1 us
    dot_general x1, matrix products, body(): jnp.einsum('hqk,khd->qhd', weights, values, preferred_element_type=jnp.fl...  14.1 us
    dot_general x1, matrix products, body(): jnp.einsum('qhd,kd->hqk', query_vectors[..., NOPE:], key_rope, preferred_...  13.2 us
    dot_general x1, matrix products, body(): jnp.dot(attended, my_cols, preferred_element_type=jnp.float32)  7.56 us
    dot_general x1, matrix products, body(): jnp.dot(attended, their_cols, preferred_element_type=jnp.float32)  6.02 us
    unnamed x35, local copies, waits for them, and re-layouts  5.77 us
  transfers between devices with their start and end apart: 4, of which 2 were waited for; matrix products, arithmetic and copies ran while one was open for 8% of the time, Pallas kernels for 0%

profile of v1, /device:TPU:1, one launch (start us, length us, event | category | flops | bytes accessed | tf_op | source)
XLA Modules:
  0.0 205.3 jit_solution(6438729907557349726)
XLA Ops:
  7.2 0.0 copy-start
  7.2 0.0 copy-start.9
  7.2 0.0 copy-start.10
  7.2 0.0 copy-start.13
  7.2 0.0 copy-start.11
  7.2 0.0 all-gather.2.cloned.1.call-start
  7.3 1.7 pad_maximum_fusion.3
  9.0 0.0 all-gather.2.cloned.1.call-update
  9.0 1.5 collective-permute-start
  10.5 0.9 select_reduce_fusion.1
  11.4 0.6 fusion.51
  14.4 2.2 %constant_dynamic-slice_fusion.7 = (bf16[2048,16]{1,0:T(8,128)(2,1)S(1)}, bf16[2048,16]{1,0:T(8,128)(2,1)S(1)}, bf16[2048,16]{1,0:T(8,128)(2,1)S(1)}, bf16[2048,16]{1,0:T(8,128)(2,1)S(1)}) fusion(bf16[2048,512]{1,0:T(8,128)(2,1)} %param.19, s32[]{:T(128)S(6)} %select_n.67, s32[]{:T(128)S(6)} %select_n.68, s32[]{:T(128)S(6)} %select_n.70, s32[]{:T(128)S(6)} %select_n.69), kind=kLoop, calls=%fused_computation.76 | loop fusion | bytes 524304 | tf_op jit(solution)/shard_map/dynamic_slice | solution.py:93
  16.6 1.5 pad_maximum_fusion.2
  18.1 0.0 collective-permute-start.1
  18.1 0.0 copy-done.9
  18.1 0.6 fusion.50
  21.2 0.1 broadcast_in_dim.21
  21.3 0.1 broadcast_in_dim.22
  21.4 0.0 copy-done.10
  21.4 0.0 copy-done.13
  21.4 0.2 reduce-window.4
  21.6 0.0 copy-done.11
  21.6 0.6 multiply_exponential_fusion
  22.1 0.1 convert_reduce_fusion
  22.2 0.1 select_reduce_fusion
  22.3 0.6 subtract_convert_fusion.2
  22.9 1.5 constant_dynamic-slice_fusion.3
  24.4 0.6 fusion.7
  25.0 0.0 collective-permute-done
  25.1 2.5 %broadcast_select_fusion.1 = (bf16[1024,1024]{1,0:T(8,128)(2,1)S(1)}, bf16[1024,1024]{1,0:T(8,128)(2,1)S(1)}) fusion(bf16[1024,1024]{1,0:T(8,128)(2,1)} %param.12, bf16[1024,1024]{1,0:T(8,128)(2,1)} %collective-permute-done, pred[]{:T(512)S(6)} %eq.70), kind=kLoop, calls=%fused_computation.28 | loop fusion | flops 2097152 | bytes 8388609 | tf_op jit(solution)/shard_map/jit(_where)/select_n | solution.py:82
  27.6 0.0 copy-start.3
  27.6 0.0 copy-start.4
  27.6 1.0 fusion.4
  28.6 0.0 collective-permute-done.1
  28.6 3.1 %fusion.26 = f32[1024,64]{0,1:T(8,128)S(1)} fusion(bf16[2048,64]{1,0:T(8,128)(2,1)} %pad_maximum_fusion.2, bf16[2048,64]{1,0:T(8,128)(2,1)} %collective-permute-done.1, pred[64]{0:T(512)(128)(4,1)S(1)} %broadcast_in_dim.22, f32[2048]{0:T(1024)S(1)} %convert_element_type.94, f32[1024]{0:T(1024)S(1)} %add_rsqrt_fusion.1, ...), kind=kOutput, calls=%fused_computation.39 | convolution fusion | flops 283246592 | bytes 4993088 | tf_op jit(solution)/shard_map/dot_general | solution.py:111
  31.7 0.0 copy-done.3
  31.8 62.8 %all-gather.2.cloned.1.call-done = bf16[2048,2112]{1,0:T(8,128)(2,1)} async-done(((bf16[32,2112]{1,0:T(8,128)(2,1)}), bf16[2048,2112]{1,0:T(8,128)(2,1)}) %all-gather.2.cloned.1.call-update) | async-done | bytes 8650768 | tf_op jit(solution)/shard_map/all_gather | solution.py:78
  94.6 16.1 %fusion.47 = f32[1024,2112]{0,1:T(8,128)} fusion(bf16[2048,2112]{1,0:T(8,128)(2,1)} %all-gather.2.cloned.1.call-done, f32[2048]{0:T(1024)S(1)} %convert_element_type.94, f32[1024]{0:T(1024)S(1)} %add_rsqrt_fusion.1, bf16[1024,1024]{1,0:T(8,128)(2,1)} %copy-done.4, bf16[1024,1024]{1,0:T(8,128)(2,1)} %copy-done.3), kind=kOutput, calls=%fused_computation.91 | convolution fusion | flops 8873050112 | bytes 21508096 | tf_op jit(solution)/shard_map/dot_general | solution.py:107
  110.7 1.8 multiply_reduce_fusion
  112.4 1.8 multiply_convert_fusion
  114.3 0.0 copy-start.5
  114.3 2.4 %convolution_convert_fusion = bf16[1024,2048]{1,0:T(8,128)(2,1)S(1)} fusion(bf16[1024,512]{0,1:T(8,128)(2,1)S(1)} %multiply_convert_fusion, bf16[512,2048]{1,0:T(8,128)(2,1)S(1)} %copy-done), kind=kOutput, calls=%fused_computation.18 | convolution fusion | flops 2149580800 | bytes 7340032 | tf_op jit(solution)/shard_map/dot_general | solution.py:133
  116.7 0.0 slice-start
  116.7 0.0 slice-start.1
  116.7 1.5 copy.40
  118.2 0.0 slice-start.2
  118.3 1.6 fusion.49
  119.9 0.0 slice-done.1
  119.9 1.5 slice-done.2
  121.4 0.0 copy-done.8
  121.4 0.6 subtract_convert_fusion.1
  121.9 1.0 slice_add_fusion
  123.0 0.0 copy-start.2
  123.0 2.7 %copy-done.2 = f32[1024,1536]{0,1:T(8,128)} copy-done((f32[1024,1536]{0,1:T(8,128)}, f32[1024,1536]{0,1:T(8,128)S(1)}, u32[]{:S(2)}) %copy-start.2) | copy-done | bytes 6291480
  125.7 0.3 subtract_convert_fusion
  126.0 13.2 %fusion.22 = f32[1024,1024,8]{1,0,2:T(8,128)} fusion(bf16[1024,8,32]{0,2,1:T(8,128)(2,1)S(1)} %get-tuple-element.5, bf16[1024,8,32]{0,2,1:T(8,128)(2,1)S(1)} %get-tuple-element.4, bf16[1024,32]{0,1:T(8,128)(2,1)S(1)} %get-tuple-element.3, bf16[1024,32]{0,1:T(8,128)(2,1)S(1)} %get-tuple-element.2), kind=kOutput, calls=%fused_computation.32 | convolution fusion | flops 1076101120 | bytes 34734080 | tf_op jit(solution)/shard_map/qhd,kd->hqk/dot_general | solution.py:141
  139.2 26.8 %fusion.52 = (f32[8,1024]{1,0:T(8,128)S(1)}, f32[8,1024,1024]{1,2,0:T(8,128)}) fusion(f32[1024,1024,8]{1,0,2:T(8,128)} %fusion.22, pred[1024,1024]{0,1:T(8,128)(4,1)S(1)} %fusion.7, f32[1024,8,192]{0,2,1:T(8,128)} %bitcast.43, bf16[1024,8,128]{2,1,0:T(8,128)(2,1)S(1)} %get-tuple-element.7), kind=kOutput, calls=%fused_computation.95 | convolution fusion | flops 2189427712 | bytes 72384512 | tf_op jit(solution)/shard_map/sub | solution.py:148
  166.0 14.1 %fusion.17 = bf16[8,128,1024]{2,1,0:T(8,128)(2,1)} fusion(f32[8,1024,1024]{1,2,0:T(8,128)} %get-tuple-element.31, f32[8,1024]{1,0:T(8,128)S(1)} %get-tuple-element.30, bf16[1024,8,128]{2,1,0:T(8,128)(2,1)} %get-tuple-element.6), kind=kOutput, calls=%fused_computation.30 | convolution fusion | flops 2165309440 | bytes 37781504 | tf_op jit(solution)/shard_map/hqk,khd->qhd/dot_general | solution.py:150
  180.1 6.0 %fusion.14 = bf16[1024,1024]{1,0:T(8,128)(2,1)} fusion(bf16[1024,1024]{0,1:T(8,128)(2,1)} %bitcast.53, bf16[1024,2048]{1,0:T(8,128)(2,1)} %param.18, s32[]{:T(128)S(6)} %select_n.78), kind=kOutput, calls=%fused_computation.29 | convolution fusion | flops 2148532224 | bytes 6291460 | tf_op jit(solution)/shard_map/dot_general | solution.py:156
  186.1 0.6 collective-permute-start.2
  186.8 1.1 pad_maximum_fusion.1
  187.9 3.0 %collective-permute-done.2 = bf16[1024,1024]{1,0:T(8,128)(2,1)} collective-permute-done((bf16[1024,1024]{1,0:T(8,128)(2,1)}, bf16[1024,1024]{1,0:T(8,128)(2,1)}, u32[]{:S(2)}, u32[]{:S(2)}) %collective-permute-start.2) | collective-permute-done | bytes 2097184 | tf_op jit(solution)/shard_map/ppermute | solution.py:52
  190.9 7.6 %add_convert_fusion = bf16[1024,1024]{1,0:T(8,128)(2,1)} fusion(bf16[1024,1024]{1,0:T(8,128)(2,1)} %collective-permute-done.2, bf16[1024,1024]{1,0:T(8,128)(2,1)} %param.12, bf16[1024,1024]{0,1:T(8,128)(2,1)} %bitcast.54, bf16[1024,2048]{1,0:T(8,128)(2,1)} %param.18, s32[]{:T(128)S(6)} %select_n.77), kind=kOutput, calls=%fused_computation.15 | convolution fusion | flops 2154823680 | bytes 10485764 | tf_op jit(solution)/shard_map/dot_general | solution.py:158
  198.5 0.0 copy-done.1
  (23 shorter events, 0.1 us)
Async XLA Ops:
  7.2 107.1 %copy-start = (bf16[512,2048]{1,0:T(8,128)(2,1)S(1)}, bf16[512,2048]{1,0:T(8,128)(2,1)}, u32[]{:S(2)}) copy-start(bf16[512,2048]{1,0:T(8,128)(2,1)} %param.17) | copy-start | bytes 6291460
  7.2 11.0 %copy-start.9 = (s32[1,4]{1,0:T(1,128)S(1)}, s32[1,4]{1,0:T(1,128)}, u32[]{:S(2)}) copy-start(s32[1,4]{1,0:T(1,128)} %param.22) | copy-start | bytes 52
  7.2 14.2 %copy-start.10 = (bf16[2048]{0:T(1024)(128)(2,1)S(1)}, bf16[2048]{0:T(1024)(128)(2,1)}, u32[]{:S(2)}) copy-start(bf16[2048]{0:T(1024)(128)(2,1)} %param.13) | copy-start | bytes 12292
  7.2 14.2 %copy-start.13 = (s32[1,4]{1,0:T(1,128)S(1)}, s32[1,4]{1,0:T(1,128)}, u32[]{:S(2)}) copy-start(s32[1,4]{1,0:T(1,128)} %param.21) | copy-start | bytes 52
  7.2 14.3 %copy-start.11 = (bf16[512]{0:T(512)(128)(2,1)S(1)}, bf16[512]{0:T(512)(128)(2,1)}, u32[]{:S(2)}) copy-start(bf16[512]{0:T(512)(128)(2,1)} %param.16) | copy-start | bytes 3076
  7.2 87.3 %all-gather.2.cloned.1.call-start = ((), (), s32[]{:S(2)}) async-start(), calls=%async_computation | async-start | bytes 9052160 | tf_op jit(solution)/shard_map/all_gather | solution.py:78
  9.0 16.0 %collective-permute-start = (bf16[1024,1024]{1,0:T(8,128)(2,1)}, bf16[1024,1024]{1,0:T(8,128)(2,1)}, u32[]{:S(2)}, u32[]{:S(2)}) collective-permute-start(bf16[1024,1024]{1,0:T(8,128)(2,1)} %param.12), channel_id=1, source_target_pairs={{0,1},{1,0},{2,3},{3,2},{4,5},{5,4},{6,7},{7,6},{8,9},{9,8},{10,11... | collective-permute-start | bytes 6291464 | tf_op jit(solution)/shard_map/ppermute | solution.py:52
  18.1 10.5 %collective-permute-start.1 = (bf16[2048,64]{1,0:T(8,128)(2,1)}, bf16[2048,64]{1,0:T(8,128)(2,1)}, u32[]{:S(2)}, u32[]{:S(2)}) collective-permute-start(bf16[2048,64]{1,0:T(8,128)(2,1)} %pad_maximum_fusion.2), channel_id=1, source_target_pairs={{0,1},{1,0},{2,3},{3,2},{4,5},{5,4},{6,7},{7,6},{8,9},{9,8},{10,11... | collective-permute-start | bytes 786440 | tf_op jit(solution)/shard_map/ppermute | solution.py:52
  27.6 4.1 %copy-start.3 = (bf16[1024,1024]{1,0:T(8,128)(2,1)}, bf16[1024,1024]{1,0:T(8,128)(2,1)S(1)}, u32[]{:S(2)}) copy-start(bf16[1024,1024]{1,0:T(8,128)(2,1)S(1)} %get-tuple-element.8) | copy-start | bytes 6291460
  27.6 4.1 %copy-start.4 = (bf16[1024,1024]{1,0:T(8,128)(2,1)}, bf16[1024,1024]{1,0:T(8,128)(2,1)S(1)}, u32[]{:S(2)}) copy-start(bf16[1024,1024]{1,0:T(8,128)(2,1)S(1)} %get-tuple-element.9) | copy-start | bytes 6291460
  114.3 2.4 %copy-start.5 = (bf16[1024,512]{0,1:T(8,128)(2,1)}, bf16[1024,512]{0,1:T(8,128)(2,1)S(1)}, u32[]{:S(2)}) copy-start(bf16[1024,512]{0,1:T(8,128)(2,1)S(1)} %multiply_convert_fusion) | copy-start | bytes 3145732
  116.7 3.2 %slice-start = ((s8[8650752]{0:T(1024)(128)(4,1)}), s8[262144]{0:T(1024)(128)(4,1)S(1)}, s32[]{:S(2)}) async-start(s8[8650752]{0:T(1024)(128)(4,1)} %bitcast.44), calls=%async_computation.1 | async-start | bytes 524288
  116.7 3.2 %slice-start.1 = ((s8[8650752]{0:T(1024)(128)(4,1)}), s8[4194304]{0:T(1024)(128)(4,1)S(1)}, s32[]{:S(2)}) async-start(s8[8650752]{0:T(1024)(128)(4,1)} %bitcast.44), calls=%async_computation.2 | async-start | bytes 8388608
  118.2 3.1 %slice-start.2 = ((s8[8650752]{0:T(1024)(128)(4,1)}), s8[4194304]{0:T(1024)(128)(4,1)S(1)}, s32[]{:S(2)}) async-start(s8[8650752]{0:T(1024)(128)(4,1)} %bitcast.44), calls=%async_computation.3 | async-start | bytes 8388608
  118.2 3.1 %copy-start.8 = (f32[1024]{0:T(1024)S(1)}, f32[1024]{0:T(1024)}, u32[]{:S(2)}) copy-start(f32[1024]{0:T(1024)} %subtract_convert_fusion.2) | copy-start | bytes 12292
  118.2 3.1 %copy-start.12 = (f32[32]{0:T(128)S(1)}, f32[32]{0:T(128)}, u32[]{:S(2)}) copy-start(f32[32]{0:T(128)} %multiply_exponential_fusion) | copy-start | bytes 388
  118.3 3.7 %copy-start.7 = (bf16[16,1536]{1,0:T(8,128)(2,1)S(1)}, bf16[16,1536]{1,0:T(8,128)(2,1)}, u32[]{:S(2)}) copy-start(bf16[16,1536]{1,0:T(8,128)(2,1)} %get-tuple-element.13) | copy-start | bytes 147460
  123.0 2.7 %copy-start.2 = (f32[1024,1536]{0,1:T(8,128)}, f32[1024,1536]{0,1:T(8,128)S(1)}, u32[]{:S(2)}) copy-start(f32[1024,1536]{0,1:T(8,128)S(1)} %slice_add_fusion) | copy-start | bytes 18874372
  180.1 6.7 %copy-start.6 = (bf16[1024,512]{0,1:T(8,128)(2,1)S(1)}, bf16[1024,512]{0,1:T(8,128)(2,1)}, u32[]{:S(2)}) copy-start(bf16[1024,512]{0,1:T(8,128)(2,1)} %copy-done.5) | copy-start | bytes 3145732
  186.1 4.8 %collective-permute-start.2 = (bf16[1024,1024]{1,0:T(8,128)(2,1)}, bf16[1024,1024]{1,0:T(8,128)(2,1)}, u32[]{:S(2)}, u32[]{:S(2)}) collective-permute-start(bf16[1024,1024]{1,0:T(8,128)(2,1)} %fusion.14), channel_id=1, source_target_pairs={{0,1},{1,0},{2,3},{3,2},{4,5},{5,4},{6,7},{7,6},{8,9},{9,8},{10,11... | collective-permute-start | bytes 6291464 | tf_op jit(solution)/shard_map/ppermute | solution.py:52
  190.9 7.6 %copy-start.1 = (bf16[512,2048]{1,0:T(8,128)(2,1)S(1)}, bf16[512,2048]{1,0:T(8,128)(2,1)}, u32[]{:S(2)}) copy-start(bf16[512,2048]{1,0:T(8,128)(2,1)} %param.17) | copy-start | bytes 6291460
Sparse Core Ops, SparseCore 0:
  10.8 83.6 all-gather.1

commit v2 on v1

--- a/solution.py
+++ b/solution.py
@@ -2,12 +2,15 @@
 import jax.numpy as jnp
 from jax import lax
 from jax.sharding import PartitionSpec as P
+from jax.experimental import pallas as pl
+from jax.experimental.pallas import tpu as pltpu
 
 NOPE = 128
 ROPE = 64
 VDIM = 128
 LATENT = 512
 RANK = 16
+BLOCK = 128
 
 
 EPS = 1e-06
@@ -46,6 +49,74 @@
     slot_hot = (adapter[:, None] == jnp.arange(adapter_slot.shape[0])[None, :]).astype(jnp.int32)
     slot = jnp.sum(slot_hot * adapter_slot[None, :], axis=1)
     return (prompt, position, adapter, slot)
+
+
+def attention_kernel(first_ref, q_nope_ref, q_rope_ref, kv_ref, kr_ref, kst_ref, o_ref, s_buf):
+    i = pl.program_id(0)
+    heads = q_rope_ref.shape[0]
+    scale = 1.0 / jnp.sqrt(jnp.float32(NOPE + ROPE))
+    lo = first_ref[i]
+    row = i * BLOCK + lax.broadcasted_iota(jnp.int32, (BLOCK, BLOCK), 0)
+    kst = kst_ref[...]
+    for h in range(heads):
+        qn = q_nope_ref[:, h * NOPE:(h + 1) * NOPE]
+        qr = q_rope_ref[h]
+
+        def score_step(c, top):
+            start = pl.multiple_of(c * BLOCK, BLOCK)
+            kn = kv_ref[pl.ds(start, BLOCK), h * (NOPE + VDIM):h * (NOPE + VDIM) + NOPE]
+            kr = kr_ref[pl.ds(start, BLOCK), :]
+            s = lax.dot_general(qn, kn, (((1,), (1,)), ((), ())), preferred_element_type=jnp.float32)
+            s = s + lax.dot_general(qr, kr, (((1,), (1,)), ((), ())), preferred_element_type=jnp.float32)
+            s = s * scale
+            col = start + lax.broadcasted_iota(jnp.int32, (BLOCK, BLOCK), 1)
+            allowed = (col >= kst) & (col <= row)
+            s = jnp.where(allowed, s, jnp.float32(-1e30))
+            s_buf[c] = s
+            return jnp.maximum(top, jnp.max(s, axis=1, keepdims=True))
+
+        top = lax.fori_loop(lo, i + 1, score_step, jnp.full((BLOCK, 1), -jnp.inf, jnp.float32))
+
+        def exp_step(c, total):
+            e = jnp.exp(s_buf[c] - top)
+            s_buf[c] = e
+            return total + jnp.sum(e, axis=1, keepdims=True)
+
+        total = lax.fori_loop(lo, i + 1, exp_step, jnp.zeros((BLOCK, 1), jnp.float32))
+
+        def pv_step(c, acc):
+            start = pl.multiple_of(c * BLOCK, BLOCK)
+            w = (s_buf[c] / total).astype(jnp.bfloat16)
+            v = kv_ref[pl.ds(start, BLOCK), h * (NOPE + VDIM) + NOPE:(h + 1) * (NOPE + VDIM)]
+            return acc + jnp.dot(w, v, preferred_element_type=jnp.float32)
+
+        acc = lax.fori_loop(lo, i + 1, pv_step, jnp.zeros((BLOCK, VDIM), jnp.float32))
+        o_ref[:, h * VDIM:(h + 1) * VDIM] = acc.astype(o_ref.dtype)
+
+
+def attend(q_nope, q_rope, kv, key_rope, key_start):
+    rows = q_nope.shape[0]
+    heads = q_rope.shape[0]
+    blocks = rows // BLOCK
+    first = key_start[::BLOCK] // BLOCK
+    grid_spec = pltpu.PrefetchScalarGridSpec(
+        num_scalar_prefetch=1,
+        grid=(blocks,),
+        in_specs=[
+            pl.BlockSpec((BLOCK, heads * NOPE), lambda i, f: (i, 0)),
+            pl.BlockSpec((heads, BLOCK, ROPE), lambda i, f: (0, i, 0)),
+            pl.BlockSpec((rows, heads * (NOPE + VDIM)), lambda i, f: (0, 0)),
+            pl.BlockSpec((rows, ROPE), lambda i, f: (0, 0)),
+            pl.BlockSpec((BLOCK, 1), lambda i, f: (i, 0)),
+        ],
+        out_specs=pl.BlockSpec((BLOCK, heads * VDIM), lambda i, f: (i, 0)),
+        scratch_shapes=[pltpu.VMEM((blocks, BLOCK, BLOCK), jnp.float32)],
+    )
+    return pl.pallas_call(
+        attention_kernel,
+        grid_spec=grid_spec,
+        out_shape=jax.ShapeDtypeStruct((rows, heads * VDIM), jnp.bfloat16),
+    )(first, q_nope, q_rope, kv, key_rope, key_start[:, None])
 
 
 def swap(values):
@@ -124,33 +195,16 @@
         spread_rows, up_weight_rows, preferred_element_type=jnp.float32
     )
     query_vectors = query_vectors.reshape(rows, heads_here, NOPE + ROPE)
-    query_vectors = jnp.concatenate(
-        [query_vectors[..., :NOPE], rotate(query_vectors[..., NOPE:], position)], axis=-1
-    ).astype(jnp.bfloat16)
+    q_nope = query_vectors[..., :NOPE].astype(jnp.bfloat16).reshape(rows, heads_here * NOPE)
+    q_rope = jnp.transpose(
+        rotate(query_vectors[..., NOPE:], position).astype(jnp.bfloat16), (1, 0, 2)
+    )
     latent = rms_scale(kv_pre[:, :LATENT], kv_gain).astype(jnp.bfloat16)
     key_rope = rotate(kv_pre[:, LATENT:], position).astype(jnp.bfloat16)
     latent_cache = jnp.concatenate([latent, key_rope], axis=1)
     expanded = jnp.dot(latent, kvb_weight, preferred_element_type=jnp.float32).astype(jnp.bfloat16)
-    expanded = expanded.reshape(rows, heads_here, NOPE + VDIM)
-    key_nope = expanded[..., :NOPE]
-    values = expanded[..., NOPE:]
-    scale = 1.0 / jnp.sqrt(jnp.float32(NOPE + ROPE))
-    scores = jnp.einsum(
-        "qhd,khd->hqk", query_vectors[..., :NOPE], key_nope, preferred_element_type=jnp.float32
-    )
-    scores = scores + jnp.einsum(
-        "qhd,kd->hqk", query_vectors[..., NOPE:], key_rope, preferred_element_type=jnp.float32
-    )
-    scores = scores * scale
-    allowed = (prompt[None, :] == prompt[:, None]) & (local_pos[None, :] <= local_pos[:, None])
-    scores = jnp.where(allowed[None, :, :], scores, jnp.float32(-1e30))
-    top = jnp.max(scores, axis=-1, keepdims=True)
-    expo = jnp.exp(scores - top)
-    weights = (expo / jnp.sum(expo, axis=-1, keepdims=True)).astype(jnp.bfloat16)
-    attended = jnp.einsum(
-        "hqk,khd->qhd", weights, values, preferred_element_type=jnp.float32
-    ).astype(jnp.bfloat16)
-    attended = attended.reshape(rows, heads_here * VDIM)
+    key_start = (local_pos - position).astype(jnp.int32)
+    attended = attend(q_nope, q_rope, expanded, key_rope, key_start)
     their_cols = lax.dynamic_slice_in_dim(o_weight, (1 - me) * half_width, half_width, 1)
     my_cols = lax.dynamic_slice_in_dim(o_weight, me * half_width, half_width, 1)
     theirs = jnp.dot(attended, their_cols, preferred_element_type=jnp.float32).astype(jnp.bfloat16)

time: 206 us -> 276 us (1.34)
  the two profiles are of different devices: /device:TPU:1 before, /device:TPU:71 now
where the time goes in v2:
time: 276 us; the launch traced here: 274 us
  Pallas kernels  102 us (37%)
  waiting for transfers between devices  66.2 us (24%)
  matrix products  38.9 us (14%)
  other arithmetic  23.4 us (8%)
  local copies, waits for them, and re-layouts  22.9 us (8%)
  between operations  19.3 us (7%)
    pallas_call x1, Pallas kernels, attend(): pl.pallas_call(attention_kernel, grid_spec=grid_spec, out_shape=jax.Shape...  102 us
    all_gather x1, waiting for transfers between devices, body(): joined = lax.all_gather(joined, 'wide', axis=0, tiled=True)  64.3 us
    dot_general x1, matrix products, body(): projections = jnp.dot(normed, joined, preferred_element_type=jnp.float32)  16.1 us
    unnamed x22, local copies, waits for them, and re-layouts  8.35 us
    another operation x3, other arithmetic  7.65 us
    dot_general x1, matrix products, body(): jnp.dot(attended, my_cols, preferred_element_type=jnp.float32)  7.23 us
    dot_general x1, matrix products, body(): jnp.dot(attended, their_cols, preferred_element_type=jnp.float32)  5.87 us
  transfers between devices with their start and end apart: 4, of which 2 were waited for; matrix products, arithmetic and copies ran while one was open for 6% of the time, Pallas kernels for 0%

profile of v2, /device:TPU:71, one launch (start us, length us, event | category | flops | bytes accessed | tf_op | source)
XLA Modules:
  0.0 274.4 jit_solution(15204015679097052905)
XLA Ops:
  7.2 0.0 copy-start
  7.2 0.0 copy-start.5
  7.2 0.0 copy-start.6
  7.2 0.0 copy-start.8
  7.2 0.0 copy-start.7
  7.2 0.0 all-gather.2.cloned.1.call-start
  7.3 1.7 pad_maximum_fusion.4
  9.0 0.0 all-gather.2.cloned.1.call-update
  9.0 0.8 collective-permute-start
  9.8 0.9 select_reduce_fusion.1
  10.6 0.6 fusion.35
  13.8 2.2 constant_dynamic-slice_fusion.7
  16.0 0.7 pad_maximum_fusion.2
  16.7 0.3 collective-permute-start.1
  17.0 0.0 copy-done.5
  17.0 0.6 fusion.34
  20.1 0.0 copy-done.6
  20.1 0.0 copy-done.8
  20.1 0.2 reduce-window.4
  20.3 0.0 copy-done.7
  20.3 0.1 broadcast_in_dim.12
  20.4 0.1 broadcast_in_dim.13
  20.5 0.1 convert_reduce_fusion
  20.6 0.1 select_reduce_fusion
  20.6 0.1 slice.62
  20.7 1.0 copy.45.kst_ref
  21.8 0.5 and_select_fusion.2.first_ref
  22.3 0.9 constant_dynamic-slice_fusion.3
  23.2 0.0 collective-permute-done
  23.2 2.6 broadcast_select_fusion.1
  25.8 0.0 copy-start.2
  25.8 0.0 copy-start.3
  25.8 1.0 fusion
  26.8 0.0 collective-permute-done.1
  26.9 1.5 fusion.12
  28.4 0.0 copy-done.2
  28.4 0.0 copy-done.3
  28.5 64.3 %all-gather.2.cloned.1.call-done = bf16[2048,2112]{1,0:T(8,128)(2,1)} async-done(((bf16[32,2112]{1,0:T(8,128)(2,1)}), bf16[2048,2112]{1,0:T(8,128)(2,1)}) %all-gather.2.cloned.1.call-update) | async-done | bytes 8650768 | tf_op jit(solution)/shard_map/all_gather | solution.py:149
  92.8 16.1 %fusion.30 = f32[1024,2112]{0,1:T(8,128)} fusion(bf16[2048,2112]{1,0:T(8,128)(2,1)} %all-gather.2.cloned.1.call-done, f32[2048]{0:T(1024)S(1)} %convert_element_type.87, f32[1024]{0:T(1024)S(1)} %add_rsqrt_fusion.1, bf16[1024,1024]{1,0:T(8,128)(2,1)} %copy-done.3, bf16[1024,1024]{1,0:T(8,128)(2,1)} %copy-done.2), kind=kOutput, calls=%fused_computation.77 | convolution fusion | flops 8873050112 | bytes 21508096 | tf_op jit(solution)/shard_map/dot_general | solution.py:178
  108.9 1.0 fusion.32
  109.9 1.8 multiply_reduce_fusion
  111.6 3.8 %slice_add_fusion = f32[1024,1536]{0,1:T(8,128)S(1)} fusion(f32[1024,2112]{0,1:T(8,128)} %fusion.30, bf16[1024,64]{0,1:T(8,128)(2,1)S(1)} %bitcast.33, bf16[16,1536]{1,0:T(8,128)(2,1)S(1)} %get-tuple-element.12, bf16[16,1536]{1,0:T(8,128)(2,1)S(1)} %get-tuple-element.13, bf16[16,1536]{1,0:T(8,128)(2,1)S(1)} %get-tuple-element.11, ...), kind=kOutput, calls=%fused_computation.5 | convolution fusion | flops 205258752 | bytes 12910592 | tf_op jit(solution)/shard_map/dot_general | solution.py:194
  115.5 1.2 fusion.33
  116.6 1.6 slice.89
  118.3 1.0 copy.51
  119.3 1.1 copy.52
  120.3 3.6 %copy.49 = f32[1024,8,32]{2,0,1:T(8,128)} copy(f32[1024,8,32]{0,2,1:T(8,128)} %get-tuple-element.6) | data formatting | bytes 2097152
  123.9 2.6 copy.50
  126.6 3.9 %copy.44.q_nope_ref = bf16[1024,1024]{1,0:T(8,128)(2,1)} copy(bf16[1024,1024]{0,1:T(8,128)(2,1)} %bitcast.32) | data formatting | bytes 4194304 | tf_op jit(solution)/shard_map/reshape | solution.py:198
  130.5 2.0 multiply_convert_fusion
  132.5 3.9 %subtract_convert_fusion.1 = (bf16[1024,32]{1,0:T(8,128)(2,1)S(1)}, bf16[1024,32]{1,0:T(8,128)(2,1)S(1)}, f32[1024,32]{1,0:T(8,128)S(1)}, f32[1024,32]{1,0:T(8,128)S(1)}) fusion(f32[1024,32]{1,0:T(8,128)} %copy.52, f32[1024,32]{1,0:T(8,128)} %copy.51, f32[1024]{0:T(1024)S(1)} %subtract_convert_fusion.2, f32[32]{0:T(128)S(1)} %multiply_exponential_fusion), kind=kLoop, calls=%fused_computation.27 | loop fusion | flops 294912 | bytes 659584 | tf_op jit(solution)/shard_map/convert
  136.5 3.5 %subtract_convert_fusion = (bf16[1024,8,32]{2,0,1:T(8,128)(2,1)S(1)}, bf16[1024,8,32]{2,0,1:T(8,128)(2,1)S(1)}) fusion(f32[1024,8,32]{2,0,1:T(8,128)} %copy.50, f32[1024,8,32]{2,0,1:T(8,128)S(1)} %copy-done.1, f32[1024,32]{1,0:T(8,128)S(1)} %get-tuple-element.20, f32[1024,32]{1,0:T(8,128)S(1)} %get-tuple-element.21), kind=kLoop, calls=%fused_computation.10 | loop fusion | flops 2097152 | bytes 3407872 | tf_op jit(solution)/shard_map/convert.2
  140.0 2.5 maximum_bitcast_fusion.q_rope_ref
  142.5 0.8 pad_maximum_fusion.3.kr_ref
  143.3 0.0 copy-done
  143.3 4.3 %convolution_convert_fusion.kv_ref = bf16[1024,2048]{1,0:T(8,128)(2,1)} fusion(bf16[1024,512]{0,1:T(8,128)(2,1)S(1)} %multiply_convert_fusion, bf16[512,2048]{1,0:T(8,128)(2,1)S(1)} %copy-done), kind=kOutput, calls=%fused_computation.11 | convolution fusion | flops 2149580800 | bytes 7340032 | tf_op jit(solution)/shard_map/dot_general | solution.py:205
  147.6 102.0 %shard_map.131 = bf16[1024,1024]{1,0:T(8,128)(2,1)} custom-call(s32[8]{0:T(128)} %and_select_fusion.2.first_ref, bf16[1024,1024]{1,0:T(8,128)(2,1)} %copy.44.q_nope_ref, bf16[8,1024,64]{2,1,0:T(8,128)(2,1)} %maximum_bitcast_fusion.q_rope_ref, bf16[1024,2048]{1,0:T(8,128)(2,1)} %convolution_convert_fusion.kv_ref, bf16[1024,64]{1,0:T(8,128)(2,1)} %pad_maximum_fusion.3.kr_ref, ...), custom_call_target="tpu_custom_call" | custom-call | tf_op jit(solution)/shard_map/pallas_call | solution.py:115
  249.6 5.9 %fusion.7 = bf16[1024,1024]{1,0:T(8,128)(2,1)} fusion(bf16[1024,1024]{1,0:T(8,128)(2,1)} %shard_map.131, bf16[1024,2048]{1,0:T(8,128)(2,1)} %param.18, s32[]{:T(128)S(6)} %select_n.79), kind=kOutput, calls=%fused_computation.21 | convolution fusion | flops 2148532224 | bytes 6291460 | tf_op jit(solution)/shard_map/dot_general | solution.py:210
  255.5 0.7 collective-permute-start.2
  256.2 1.1 copy.46
  257.2 0.1 copy.47
  257.3 1.1 pad_maximum_fusion.1
  258.4 1.8 collective-permute-done.2
  260.3 7.2 %add_convert_fusion = bf16[1024,1024]{1,0:T(8,128)(2,1)} fusion(bf16[1024,1024]{1,0:T(8,128)(2,1)} %collective-permute-done.2, bf16[1024,1024]{1,0:T(8,128)(2,1)} %param.12, bf16[1024,1024]{1,0:T(8,128)(2,1)} %shard_map.131, bf16[1024,2048]{1,0:T(8,128)(2,1)} %param.18, s32[]{:T(128)S(6)} %select_n.78), kind=kOutput, calls=%fused_computation.8 | convolution fusion | flops 2154823680 | bytes 10485764 | tf_op jit(solution)/shard_map/dot_general | solution.py:212
  (16 shorter events, 0.1 us)
Async XLA Ops:
  7.2 136.2 %copy-start = (bf16[512,2048]{1,0:T(8,128)(2,1)S(1)}, bf16[512,2048]{1,0:T(8,128)(2,1)}, u32[]{:S(2)}) copy-start(bf16[512,2048]{1,0:T(8,128)(2,1)} %param.17) | copy-start | bytes 6291460
  7.2 9.8 %copy-start.5 = (s32[1,4]{1,0:T(1,128)S(1)}, s32[1,4]{1,0:T(1,128)}, u32[]{:S(2)}) copy-start(s32[1,4]{1,0:T(1,128)} %param.22) | copy-start | bytes 52
  7.2 12.9 %copy-start.6 = (bf16[2048]{0:T(1024)(128)(2,1)S(1)}, bf16[2048]{0:T(1024)(128)(2,1)}, u32[]{:S(2)}) copy-start(bf16[2048]{0:T(1024)(128)(2,1)} %param.13) | copy-start | bytes 12292
  7.2 12.9 %copy-start.8 = (s32[1,4]{1,0:T(1,128)S(1)}, s32[1,4]{1,0:T(1,128)}, u32[]{:S(2)}) copy-start(s32[1,4]{1,0:T(1,128)} %param.21) | copy-start | bytes 52
  7.2 13.1 %copy-start.7 = (bf16[512]{0:T(512)(128)(2,1)S(1)}, bf16[512]{0:T(512)(128)(2,1)}, u32[]{:S(2)}) copy-start(bf16[512]{0:T(512)(128)(2,1)} %param.16) | copy-start | bytes 3076
  7.2 85.5 %all-gather.2.cloned.1.call-start = ((), (), s32[]{:S(2)}) async-start(), calls=%async_computation | async-start | bytes 9052160 | tf_op jit(solution)/shard_map/all_gather | solution.py:149
  9.0 14.2 %collective-permute-start = (bf16[1024,1024]{1,0:T(8,128)(2,1)}, bf16[1024,1024]{1,0:T(8,128)(2,1)}, u32[]{:S(2)}, u32[]{:S(2)}) collective-permute-start(bf16[1024,1024]{1,0:T(8,128)(2,1)} %param.12), channel_id=1, source_target_pairs={{0,1},{1,0},{2,3},{3,2},{4,5},{5,4},{6,7},{7,6},{8,9},{9,8},{10,11... | collective-permute-start | bytes 6291464 | tf_op jit(solution)/shard_map/ppermute | solution.py:123
  16.7 10.2 %collective-permute-start.1 = (bf16[2048,64]{1,0:T(8,128)(2,1)S(1)}, bf16[2048,64]{1,0:T(8,128)(2,1)S(1)}, u32[]{:S(2)}, u32[]{:S(2)}) collective-permute-start(bf16[2048,64]{1,0:T(8,128)(2,1)S(1)} %pad_maximum_fusion.2), channel_id=1, source_target_pairs={{0,1},{1,0},{2,3},{3,2},{4,5},{5,4},{6,7},{7,6},{8,9},{9,8},{10,11... | collective-permute-start | bytes 786440 | tf_op jit(solution)/shard_map/ppermute | solution.py:123
  25.8 2.6 copy-start.2
  25.8 2.6 copy-start.3
  130.5 5.9 %copy-start.1 = (f32[1024,8,32]{2,0,1:T(8,128)S(1)}, f32[1024,8,32]{2,0,1:T(8,128)}, u32[]{:S(2)}) copy-start(f32[1024,8,32]{2,0,1:T(8,128)} %copy.49) | copy-start | bytes 3145732
  136.4 6.0 %copy-start.4 = (bf16[1024,32]{1,0:T(8,128)(2,1)}, bf16[1024,32]{1,0:T(8,128)(2,1)S(1)}, u32[]{:S(2)}) copy-start(bf16[1024,32]{1,0:T(8,128)(2,1)S(1)} %get-tuple-element.18) | copy-start | bytes 196612
  255.5 4.8 %collective-permute-start.2 = (bf16[1024,1024]{1,0:T(8,128)(2,1)}, bf16[1024,1024]{1,0:T(8,128)(2,1)}, u32[]{:S(2)}, u32[]{:S(2)}) collective-permute-start(bf16[1024,1024]{1,0:T(8,128)(2,1)} %fusion.7), channel_id=1, source_target_pairs={{0,1},{1,0},{2,3},{3,2},{4,5},{5,4},{6,7},{7,6},{8,9},{9,8},{10,11... | collective-permute-start | bytes 6291464 | tf_op jit(solution)/shard_map/ppermute | solution.py:123
Sparse Core Ops, SparseCore 0:
  11.4 81.3 all-gather.1

commit v3 on v1

--- a/solution.py
+++ b/solution.py
@@ -2,12 +2,17 @@
 import jax.numpy as jnp
 from jax import lax
 from jax.sharding import PartitionSpec as P
+from jax.experimental import pallas as pl
+from jax.experimental.pallas import tpu as pltpu
 
 NOPE = 128
 ROPE = 64
 VDIM = 128
 LATENT = 512
 RANK = 16
+LMAX = 512
+QBLOCK = 256
+WINDOW = QBLOCK + LMAX
 
 
 EPS = 1e-06
@@ -46,6 +51,49 @@
     slot_hot = (adapter[:, None] == jnp.arange(adapter_slot.shape[0])[None, :]).astype(jnp.int32)
     slot = jnp.sum(slot_hot * adapter_slot[None, :], axis=1)
     return (prompt, position, adapter, slot)
+
+
+def attention_kernel(q_nope_ref, q_rope_ref, kv_ref, kr_ref, kst_ref, o_ref):
+    i = pl.program_id(0)
+    heads = q_rope_ref.shape[0]
+    scale = 1.0 / jnp.sqrt(jnp.float32(NOPE + ROPE))
+    start = pl.multiple_of(jnp.maximum(i * QBLOCK - LMAX, 0), 128)
+    row = i * QBLOCK + lax.broadcasted_iota(jnp.int32, (QBLOCK, WINDOW), 0)
+    col = start + lax.broadcasted_iota(jnp.int32, (QBLOCK, WINDOW), 1)
+    allowed = (col >= kst_ref[...]) & (col <= row)
+    kr = kr_ref[pl.ds(start, WINDOW), :]
+    for h in range(heads):
+        qn = q_nope_ref[:, h * NOPE:(h + 1) * NOPE]
+        qr = q_rope_ref[h]
+        kn = kv_ref[pl.ds(start, WINDOW), h * (NOPE + VDIM):h * (NOPE + VDIM) + NOPE]
+        s = lax.dot_general(qn, kn, (((1,), (1,)), ((), ())), preferred_element_type=jnp.float32)
+        s = s + lax.dot_general(qr, kr, (((1,), (1,)), ((), ())), preferred_element_type=jnp.float32)
+        s = jnp.where(allowed, s * scale, jnp.float32(-1e30))
+        top = jnp.max(s, axis=1, keepdims=True)
+        e = jnp.exp(s - top)
+        w = (e / jnp.sum(e, axis=1, keepdims=True)).astype(jnp.bfloat16)
+        v = kv_ref[pl.ds(start, WINDOW), h * (NOPE + VDIM) + NOPE:(h + 1) * (NOPE + VDIM)]
+        o_ref[:, h * VDIM:(h + 1) * VDIM] = jnp.dot(
+            w, v, preferred_element_type=jnp.float32
+        ).astype(o_ref.dtype)
+
+
+def attend(q_nope, q_rope, kv, key_rope, key_start):
+    rows = q_nope.shape[0]
+    heads = q_rope.shape[0]
+    return pl.pallas_call(
+        attention_kernel,
+        grid=(rows // QBLOCK,),
+        in_specs=[
+            pl.BlockSpec((QBLOCK, heads * NOPE), lambda i: (i, 0)),
+            pl.BlockSpec((heads, QBLOCK, ROPE), lambda i: (0, i, 0)),
+            pl.BlockSpec((rows, heads * (NOPE + VDIM)), lambda i: (0, 0)),
+            pl.BlockSpec((rows, ROPE), lambda i: (0, 0)),
+            pl.BlockSpec((QBLOCK, 1), lambda i: (i, 0)),
+        ],
+        out_specs=pl.BlockSpec((QBLOCK, heads * VDIM), lambda i: (i, 0)),
+        out_shape=jax.ShapeDtypeStruct((rows, heads * VDIM), jnp.bfloat16),
+    )(q_nope, q_rope, kv, key_rope, key_start[:, None])
 
 
 def swap(values):
@@ -124,33 +172,16 @@
         spread_rows, up_weight_rows, preferred_element_type=jnp.float32
     )
     query_vectors = query_vectors.reshape(rows, heads_here, NOPE + ROPE)
-    query_vectors = jnp.concatenate(
-        [query_vectors[..., :NOPE], rotate(query_vectors[..., NOPE:], position)], axis=-1
-    ).astype(jnp.bfloat16)
+    q_nope = query_vectors[..., :NOPE].astype(jnp.bfloat16).reshape(rows, heads_here * NOPE)
+    q_rope = jnp.transpose(
+        rotate(query_vectors[..., NOPE:], position).astype(jnp.bfloat16), (1, 0, 2)
+    )
     latent = rms_scale(kv_pre[:, :LATENT], kv_gain).astype(jnp.bfloat16)
     key_rope = rotate(kv_pre[:, LATENT:], position).astype(jnp.bfloat16)
     latent_cache = jnp.concatenate([latent, key_rope], axis=1)
     expanded = jnp.dot(latent, kvb_weight, preferred_element_type=jnp.float32).astype(jnp.bfloat16)
-    expanded = expanded.reshape(rows, heads_here, NOPE + VDIM)
-    key_nope = expanded[..., :NOPE]
-    values = expanded[..., NOPE:]
-    scale = 1.0 / jnp.sqrt(jnp.float32(NOPE + ROPE))
-    scores = jnp.einsum(
-        "qhd,khd->hqk", query_vectors[..., :NOPE], key_nope, preferred_element_type=jnp.float32
-    )
-    scores = scores + jnp.einsum(
-        "qhd,kd->hqk", query_vectors[..., NOPE:], key_rope, preferred_element_type=jnp.float32
-    )
-    scores = scores * scale
-    allowed = (prompt[None, :] == prompt[:, None]) & (local_pos[None, :] <= local_pos[:, None])
-    scores = jnp.where(allowed[None, :, :], scores, jnp.float32(-1e30))
-    top = jnp.max(scores, axis=-1, keepdims=True)
-    expo = jnp.exp(scores - top)
-    weights = (expo / jnp.sum(expo, axis=-1, keepdims=True)).astype(jnp.bfloat16)
-    attended = jnp.einsum(
-        "hqk,khd->qhd", weights, values, preferred_element_type=jnp.float32
-    ).astype(jnp.bfloat16)
-    attended = attended.reshape(rows, heads_here * VDIM)
+    key_start = (local_pos - position).astype(jnp.int32)
+    attended = attend(q_nope, q_rope, expanded, key_rope, key_start)
     their_cols = lax.dynamic_slice_in_dim(o_weight, (1 - me) * half_width, half_width, 1)
     my_cols = lax.dynamic_slice_in_dim(o_weight, me * half_width, half_width, 1)
     theirs = jnp.dot(attended, their_cols, preferred_element_type=jnp.float32).astype(jnp.bfloat16)

time: 206 us -> 204 us (level)
  matrix products: 90.3 us -> 38.9 us
  Pallas kernels: 0 us -> 28.3 us
  local copies, waits for them, and re-layouts: 12.5 us -> 22.8 us
  other arithmetic: 15.3 us -> 22.9 us
  waiting for transfers between devices: 65.8 us -> 68.4 us
    pallas_call x0 -> x1, Pallas kernels: none -> 28.3 us  [attend(): pl.pallas_call(attention_kernel, grid=(rows // QBLOCK,), in_specs=[pl.Blo...]
    dot_general x2 -> x0, matrix products: 27.3 us -> none  [the longest x1 14.1 us: body(): jnp.einsum('hqk,khd->qhd', weights, values, preferred_element_type=jnp.fl...]
    sub x1 -> x0, matrix products: 26.8 us -> none  [body(): expo = jnp.exp(scores - top)]
    another operation x3, other arithmetic: 1.08 us -> 7.65 us
    reshape x0 -> x1, local copies, waits for them, and re-layouts: none -> 3.94 us  [body(): query_vectors[..., :NOPE].astype(jnp.bfloat16)]
    all_gather x1, waiting for transfers between devices: 62.8 us -> 66.6 us  [body(): joined = lax.all_gather(joined, 'wide', axis=0, tiled=True)]
    dot_general x1, matrix products: 1.04 us -> 3.8 us  [body(): jnp.dot(spread_rows, up_weight_rows, preferred_element_type=jnp.float32)]
    unnamed x35 -> x22, local copies, waits for them, and re-layouts: 5.77 us -> 8.35 us
  transfers between devices with their start and end apart: 4 -> 4, of which waited for: 2 -> 2; matrix products, arithmetic and copies ran while one was open for 8% -> 7% of each run, Pallas kernels for 0% -> 0%
where the time goes in v3:
time: 204 us; the launch traced here: 203 us
  waiting for transfers between devices  68.4 us (34%)
  matrix products  38.9 us (19%)
  Pallas kernels  28.3 us (14%)
  other arithmetic  22.9 us (11%)
  local copies, waits for them, and re-layouts  22.8 us (11%)
  between operations  19.3 us (9%)
  starting transfers between devices  2.47 us (1%)
    all_gather x1, waiting for transfers between devices, body(): joined = lax.all_gather(joined, 'wide', axis=0, tiled=True)  66.6 us
    pallas_call x1, Pallas kernels, attend(): pl.pallas_call(attention_kernel, grid=(rows // QBLOCK,), in_specs=[pl.Blo...  28.3 us
    dot_general x1, matrix products, body(): projections = jnp.dot(normed, joined, preferred_element_type=jnp.float32)  16.1 us
    unnamed x22, local copies, waits for them, and re-layouts  8.35 us
    another operation x3, other arithmetic  7.65 us
    dot_general x1, matrix products, body(): jnp.dot(attended, my_cols, preferred_element_type=jnp.float32)  7.23 us
    dot_general x1, matrix products, body(): jnp.dot(attended, their_cols, preferred_element_type=jnp.float32)  5.87 us
    dot_general x1, matrix products, body(): jnp.dot(latent, kvb_weight, preferred_element_type=jnp.float32)  4.32 us
  transfers between devices with their start and end apart: 4, of which 2 were waited for; matrix products, arithmetic and copies ran while one was open for 7% of the time, Pallas kernels for 0%

profile of v3, /device:TPU:1, one launch (start us, length us, event | category | flops | bytes accessed | tf_op | source)
XLA Modules:
  0.0 203.1 jit_solution(12289146228435503708)
XLA Ops:
  7.2 0.0 copy-start
  7.2 0.0 copy-start.5
  7.2 0.0 copy-start.6
  7.2 0.0 copy-start.8
  7.2 0.0 copy-start.7
  7.2 0.0 all-gather.2.cloned.1.call-start
  7.3 1.7 pad_maximum_fusion.4
  9.0 0.0 all-gather.2.cloned.1.call-update
  9.0 1.5 collective-permute-start
  10.5 0.9 select_reduce_fusion.1
  11.4 0.6 fusion.35
  14.5 2.2 %constant_dynamic-slice_fusion.7 = (bf16[2048,16]{1,0:T(8,128)(2,1)S(1)}, bf16[2048,16]{1,0:T(8,128)(2,1)S(1)}, bf16[2048,16]{1,0:T(8,128)(2,1)S(1)}, bf16[2048,16]{1,0:T(8,128)(2,1)S(1)}) fusion(bf16[2048,512]{1,0:T(8,128)(2,1)} %param.19, s32[]{:T(128)S(6)} %select_n.63, s32[]{:T(128)S(6)} %select_n.64, s32[]{:T(128)S(6)} %select_n.66, s32[]{:T(128)S(6)} %select_n.65), kind=kLoop, calls=%fused_computation.59 | loop fusion | bytes 524304 | tf_op jit(solution)/shard_map/dynamic_slice | solution.py:141
  16.8 0.7 pad_maximum_fusion.2
  17.4 0.3 collective-permute-start.1
  17.7 0.0 copy-done.5
  17.7 0.6 fusion.34
  20.8 0.0 copy-done.6
  20.8 0.0 copy-done.8
  20.8 0.2 reduce-window.4
  21.0 0.0 copy-done.7
  21.0 0.1 broadcast_in_dim.12
  21.1 0.1 broadcast_in_dim.13
  21.2 0.1 convert_reduce_fusion
  21.3 0.1 select_reduce_fusion
  21.4 1.0 copy.45.kst_ref
  22.4 0.9 constant_dynamic-slice_fusion.3
  23.3 0.0 collective-permute-done
  23.4 2.6 %broadcast_select_fusion.1 = (bf16[1024,1024]{1,0:T(8,128)(2,1)S(1)}, bf16[1024,1024]{1,0:T(8,128)(2,1)S(1)}) fusion(bf16[1024,1024]{1,0:T(8,128)(2,1)} %param.12, bf16[1024,1024]{1,0:T(8,128)(2,1)} %collective-permute-done, pred[]{:T(512)S(6)} %eq.53), kind=kLoop, calls=%fused_computation.20 | loop fusion | flops 2097152 | bytes 8388609 | tf_op jit(solution)/shard_map/jit(_where)/select_n | solution.py:130
  25.9 0.0 copy-start.2
  25.9 0.0 copy-start.3
  25.9 1.0 fusion
  26.9 0.0 collective-permute-done.1
  27.0 1.5 fusion.12
  28.5 0.0 copy-done.2
  28.5 0.0 copy-done.3
  28.6 66.6 %all-gather.2.cloned.1.call-done = bf16[2048,2112]{1,0:T(8,128)(2,1)} async-done(((bf16[32,2112]{1,0:T(8,128)(2,1)}), bf16[2048,2112]{1,0:T(8,128)(2,1)}) %all-gather.2.cloned.1.call-update) | async-done | bytes 8650768 | tf_op jit(solution)/shard_map/all_gather | solution.py:126
  95.1 16.1 %fusion.30 = f32[1024,2112]{0,1:T(8,128)} fusion(bf16[2048,2112]{1,0:T(8,128)(2,1)} %all-gather.2.cloned.1.call-done, f32[2048]{0:T(1024)S(1)} %convert_element_type.86, f32[1024]{0:T(1024)S(1)} %add_rsqrt_fusion.1, bf16[1024,1024]{1,0:T(8,128)(2,1)} %copy-done.3, bf16[1024,1024]{1,0:T(8,128)(2,1)} %copy-done.2), kind=kOutput, calls=%fused_computation.73 | convolution fusion | flops 8873050112 | bytes 21508096 | tf_op jit(solution)/shard_map/dot_general | solution.py:155
  111.3 1.0 fusion.32
  112.2 1.8 multiply_reduce_fusion
  114.0 3.8 %slice_add_fusion = f32[1024,1536]{0,1:T(8,128)S(1)} fusion(f32[1024,2112]{0,1:T(8,128)} %fusion.30, bf16[1024,64]{0,1:T(8,128)(2,1)S(1)} %bitcast.33, bf16[16,1536]{1,0:T(8,128)(2,1)S(1)} %get-tuple-element.12, bf16[16,1536]{1,0:T(8,128)(2,1)S(1)} %get-tuple-element.13, bf16[16,1536]{1,0:T(8,128)(2,1)S(1)} %get-tuple-element.11, ...), kind=kOutput, calls=%fused_computation.5 | convolution fusion | flops 205258752 | bytes 12910592 | tf_op jit(solution)/shard_map/dot_general | solution.py:171
  117.8 1.2 fusion.33
  119.0 1.6 slice.85
  120.6 1.0 copy.51
  121.6 1.1 copy.52
  122.7 3.6 %copy.49 = f32[1024,8,32]{2,0,1:T(8,128)} copy(f32[1024,8,32]{0,2,1:T(8,128)} %get-tuple-element.6) | data formatting | bytes 2097152
  126.3 2.6 %copy.50 = f32[1024,8,32]{2,0,1:T(8,128)} copy(f32[1024,8,32]{0,2,1:T(8,128)S(1)} %get-tuple-element.7) | data formatting | bytes 2097152
  129.0 3.9 %copy.44.q_nope_ref = bf16[1024,1024]{1,0:T(8,128)(2,1)} copy(bf16[1024,1024]{0,1:T(8,128)(2,1)} %bitcast.32) | data formatting | bytes 4194304 | tf_op jit(solution)/shard_map/reshape | solution.py:175
  132.9 2.0 multiply_convert_fusion
  134.9 3.9 %subtract_convert_fusion.1 = (bf16[1024,32]{1,0:T(8,128)(2,1)S(1)}, bf16[1024,32]{1,0:T(8,128)(2,1)S(1)}, f32[1024,32]{1,0:T(8,128)S(1)}, f32[1024,32]{1,0:T(8,128)S(1)}) fusion(f32[1024,32]{1,0:T(8,128)} %copy.52, f32[1024,32]{1,0:T(8,128)} %copy.51, f32[1024]{0:T(1024)S(1)} %subtract_convert_fusion.2, f32[32]{0:T(128)S(1)} %multiply_exponential_fusion), kind=kLoop, calls=%fused_computation.27 | loop fusion | flops 294912 | bytes 659584 | tf_op jit(solution)/shard_map/convert
  138.8 0.0 copy-start.4
  138.8 0.0 copy-done.1
  138.8 3.5 %subtract_convert_fusion = (bf16[1024,8,32]{2,0,1:T(8,128)(2,1)S(1)}, bf16[1024,8,32]{2,0,1:T(8,128)(2,1)S(1)}) fusion(f32[1024,8,32]{2,0,1:T(8,128)} %copy.50, f32[1024,8,32]{2,0,1:T(8,128)S(1)} %copy-done.1, f32[1024,32]{1,0:T(8,128)S(1)} %get-tuple-element.20, f32[1024,32]{1,0:T(8,128)S(1)} %get-tuple-element.21), kind=kLoop, calls=%fused_computation.10 | loop fusion | flops 2097152 | bytes 3407872 | tf_op jit(solution)/shard_map/convert.2
  142.4 2.5 %maximum_bitcast_fusion.q_rope_ref = bf16[8,1024,64]{2,1,0:T(8,128)(2,1)} fusion(bf16[1024,8,32]{2,0,1:T(8,128)(2,1)S(1)} %get-tuple-element.3, bf16[1024,8,32]{2,0,1:T(8,128)(2,1)S(1)} %get-tuple-element.2), kind=kLoop, calls=%fused_computation.12 | loop fusion | flops 2097152 | bytes 2097152 | tf_op jit(solution)/shard_map/transpose | solution.py:176
  144.8 0.0 copy-done.4
  144.8 0.8 pad_maximum_fusion.3.kr_ref
  145.7 4.3 %convolution_convert_fusion.kv_ref = bf16[1024,2048]{1,0:T(8,128)(2,1)} fusion(bf16[1024,512]{0,1:T(8,128)(2,1)S(1)} %multiply_convert_fusion, bf16[512,2048]{1,0:T(8,128)(2,1)S(1)} %copy-done), kind=kOutput, calls=%fused_computation.11 | convolution fusion | flops 2149580800 | bytes 7340032 | tf_op jit(solution)/shard_map/dot_general | solution.py:182
  150.0 28.3 %shard_map.131 = bf16[1024,1024]{1,0:T(8,128)(2,1)} custom-call(bf16[1024,1024]{1,0:T(8,128)(2,1)} %copy.44.q_nope_ref, bf16[8,1024,64]{2,1,0:T(8,128)(2,1)} %maximum_bitcast_fusion.q_rope_ref, bf16[1024,2048]{1,0:T(8,128)(2,1)} %convolution_convert_fusion.kv_ref, bf16[1024,64]{1,0:T(8,128)(2,1)} %pad_maximum_fusion.3.kr_ref, s32[1024,1]{1,0:T(8,128)} %copy.45.kst_ref), custom_call_target="tpu_custom_call" | custom-call | tf_op jit(solution)/shard_map/pallas_call | solution.py:84
  178.3 5.9 %fusion.7 = bf16[1024,1024]{1,0:T(8,128)(2,1)} fusion(bf16[1024,1024]{1,0:T(8,128)(2,1)} %shard_map.131, bf16[1024,2048]{1,0:T(8,128)(2,1)} %param.18, s32[]{:T(128)S(6)} %select_n.73), kind=kOutput, calls=%fused_computation.21 | convolution fusion | flops 2148532224 | bytes 6291460 | tf_op jit(solution)/shard_map/dot_general | solution.py:187
  184.2 0.7 collective-permute-start.2
  184.8 1.1 copy.46
  185.9 0.1 copy.47
  186.0 1.1 pad_maximum_fusion.1
  187.1 1.8 collective-permute-done.2
  189.0 7.2 %add_convert_fusion = bf16[1024,1024]{1,0:T(8,128)(2,1)} fusion(bf16[1024,1024]{1,0:T(8,128)(2,1)} %collective-permute-done.2, bf16[1024,1024]{1,0:T(8,128)(2,1)} %param.12, bf16[1024,1024]{1,0:T(8,128)(2,1)} %shard_map.131, bf16[1024,2048]{1,0:T(8,128)(2,1)} %param.18, s32[]{:T(128)S(6)} %select_n.72), kind=kOutput, calls=%fused_computation.8 | convolution fusion | flops 2154823680 | bytes 10485764 | tf_op jit(solution)/shard_map/dot_general | solution.py:189
  (14 shorter events, 0.1 us)
Async XLA Ops:
  7.2 138.5 %copy-start = (bf16[512,2048]{1,0:T(8,128)(2,1)S(1)}, bf16[512,2048]{1,0:T(8,128)(2,1)}, u32[]{:S(2)}) copy-start(bf16[512,2048]{1,0:T(8,128)(2,1)} %param.17) | copy-start | bytes 6291460
  7.2 10.5 %copy-start.5 = (s32[1,4]{1,0:T(1,128)S(1)}, s32[1,4]{1,0:T(1,128)}, u32[]{:S(2)}) copy-start(s32[1,4]{1,0:T(1,128)} %param.22) | copy-start | bytes 52
  7.2 13.6 %copy-start.6 = (bf16[2048]{0:T(1024)(128)(2,1)S(1)}, bf16[2048]{0:T(1024)(128)(2,1)}, u32[]{:S(2)}) copy-start(bf16[2048]{0:T(1024)(128)(2,1)} %param.13) | copy-start | bytes 12292
  7.2 13.6 %copy-start.8 = (s32[1,4]{1,0:T(1,128)S(1)}, s32[1,4]{1,0:T(1,128)}, u32[]{:S(2)}) copy-start(s32[1,4]{1,0:T(1,128)} %param.21) | copy-start | bytes 52
  7.2 13.8 %copy-start.7 = (bf16[512]{0:T(512)(128)(2,1)S(1)}, bf16[512]{0:T(512)(128)(2,1)}, u32[]{:S(2)}) copy-start(bf16[512]{0:T(512)(128)(2,1)} %param.16) | copy-start | bytes 3076
  7.2 87.9 %all-gather.2.cloned.1.call-start = ((), (), s32[]{:S(2)}) async-start(), calls=%async_computation | async-start | bytes 9052160 | tf_op jit(solution)/shard_map/all_gather | solution.py:126
  9.0 14.3 %collective-permute-start = (bf16[1024,1024]{1,0:T(8,128)(2,1)}, bf16[1024,1024]{1,0:T(8,128)(2,1)}, u32[]{:S(2)}, u32[]{:S(2)}) collective-permute-start(bf16[1024,1024]{1,0:T(8,128)(2,1)} %param.12), channel_id=1, source_target_pairs={{0,1},{1,0},{2,3},{3,2},{4,5},{5,4},{6,7},{7,6},{8,9},{9,8},{10,11... | collective-permute-start | bytes 6291464 | tf_op jit(solution)/shard_map/ppermute | solution.py:100
  17.4 9.5 %collective-permute-start.1 = (bf16[2048,64]{1,0:T(8,128)(2,1)S(1)}, bf16[2048,64]{1,0:T(8,128)(2,1)S(1)}, u32[]{:S(2)}, u32[]{:S(2)}) collective-permute-start(bf16[2048,64]{1,0:T(8,128)(2,1)S(1)} %pad_maximum_fusion.2), channel_id=1, source_target_pairs={{0,1},{1,0},{2,3},{3,2},{4,5},{5,4},{6,7},{7,6},{8,9},{9,8},{10,11... | collective-permute-start | bytes 786440 | tf_op jit(solution)/shard_map/ppermute | solution.py:100
  25.9 2.6 %copy-start.2 = (bf16[1024,1024]{1,0:T(8,128)(2,1)}, bf16[1024,1024]{1,0:T(8,128)(2,1)S(1)}, u32[]{:S(2)}) copy-start(bf16[1024,1024]{1,0:T(8,128)(2,1)S(1)} %get-tuple-element.8) | copy-start | bytes 6291460
  25.9 2.6 %copy-start.3 = (bf16[1024,1024]{1,0:T(8,128)(2,1)}, bf16[1024,1024]{1,0:T(8,128)(2,1)S(1)}, u32[]{:S(2)}) copy-start(bf16[1024,1024]{1,0:T(8,128)(2,1)S(1)} %get-tuple-element.9) | copy-start | bytes 6291460
  132.9 5.9 %copy-start.1 = (f32[1024,8,32]{2,0,1:T(8,128)S(1)}, f32[1024,8,32]{2,0,1:T(8,128)}, u32[]{:S(2)}) copy-start(f32[1024,8,32]{2,0,1:T(8,128)} %copy.49) | copy-start | bytes 3145732
  138.8 6.0 %copy-start.4 = (bf16[1024,32]{1,0:T(8,128)(2,1)}, bf16[1024,32]{1,0:T(8,128)(2,1)S(1)}, u32[]{:S(2)}) copy-start(bf16[1024,32]{1,0:T(8,128)(2,1)S(1)} %get-tuple-element.18) | copy-start | bytes 196612
  184.2 4.8 %collective-permute-start.2 = (bf16[1024,1024]{1,0:T(8,128)(2,1)}, bf16[1024,1024]{1,0:T(8,128)(2,1)}, u32[]{:S(2)}, u32[]{:S(2)}) collective-permute-start(bf16[1024,1024]{1,0:T(8,128)(2,1)} %fusion.7), channel_id=1, source_target_pairs={{0,1},{1,0},{2,3},{3,2},{4,5},{5,4},{6,7},{7,6},{8,9},{9,8},{10,11... | collective-permute-start | bytes 6291464 | tf_op jit(solution)/shard_map/ppermute | solution.py:100
Sparse Core Ops, SparseCore 0:
  11.4 83.6 all-gather.1

commit v4 on v3

--- a/solution.py
+++ b/solution.py
@@ -11,7 +11,7 @@
 LATENT = 512
 RANK = 16
 LMAX = 512
-QBLOCK = 256
+QBLOCK = 128
 WINDOW = QBLOCK + LMAX
 
 
@@ -71,7 +71,7 @@
         s = jnp.where(allowed, s * scale, jnp.float32(-1e30))
         top = jnp.max(s, axis=1, keepdims=True)
         e = jnp.exp(s - top)
-        w = (e / jnp.sum(e, axis=1, keepdims=True)).astype(jnp.bfloat16)
+        w = (e * (1.0 / jnp.sum(e, axis=1, keepdims=True))).astype(jnp.bfloat16)
         v = kv_ref[pl.ds(start, WINDOW), h * (NOPE + VDIM) + NOPE:(h + 1) * (NOPE + VDIM)]
         o_ref[:, h * VDIM:(h + 1) * VDIM] = jnp.dot(
             w, v, preferred_element_type=jnp.float32
@@ -94,6 +94,19 @@
         out_specs=pl.BlockSpec((QBLOCK, heads * VDIM), lambda i: (i, 0)),
         out_shape=jax.ShapeDtypeStruct((rows, heads * VDIM), jnp.bfloat16),
     )(q_nope, q_rope, kv, key_rope, key_start[:, None])
+
+
+def split_heads(weight, heads):
+    parts = weight.reshape(weight.shape[0], heads, NOPE + ROPE)
+    half = ROPE // 2
+    return jnp.concatenate(
+        [
+            parts[..., :NOPE].reshape(weight.shape[0], heads * NOPE),
+            parts[..., NOPE:NOPE + half].reshape(weight.shape[0], heads * half),
+            parts[..., NOPE + half:].reshape(weight.shape[0], heads * half),
+        ],
+        axis=1,
+    )
 
 
 def swap(values):
@@ -122,7 +135,7 @@
     me = lax.axis_index("narrow")
     mine_first = me == 0
 
-    joined = jnp.concatenate([q_weight, kva_weight], axis=1)
+    joined = jnp.concatenate([split_heads(q_weight, heads_here), kva_weight], axis=1)
     joined = lax.all_gather(joined, "wide", axis=0, tiled=True)
 
     other = swap(tokens)
@@ -164,17 +177,34 @@
         lax.dynamic_slice_in_dim(adapter_up_weight, prompt_ids[prompt_index] * RANK, RANK, 0)
         for prompt_index in range(prompts_here)
     ]
-    up_weight_rows = jnp.concatenate(up_blocks, axis=0)
+    up_weight_rows = split_heads(jnp.concatenate(up_blocks, axis=0), heads_here)
     spread_rows = (member.astype(jnp.bfloat16)[:, :, None] * lowrank[:, None, :]).reshape(
         rows, prompts_here * RANK
     )
     query_vectors = query_vectors + ADAPTER_SCALE * jnp.dot(
         spread_rows, up_weight_rows, preferred_element_type=jnp.float32
     )
-    query_vectors = query_vectors.reshape(rows, heads_here, NOPE + ROPE)
-    q_nope = query_vectors[..., :NOPE].astype(jnp.bfloat16).reshape(rows, heads_here * NOPE)
+    nope_cols = heads_here * NOPE
+    half_cols = heads_here * (ROPE // 2)
+    q_nope = query_vectors[:, :nope_cols].astype(jnp.bfloat16)
+    first = query_vectors[:, nope_cols:nope_cols + half_cols]
+    second = query_vectors[:, nope_cols + half_cols:]
+    half = ROPE // 2
+    freqs = jnp.exp(-jnp.log(THETA) * 2.0 * jnp.arange(half).astype(jnp.float32) / (2 * half))
+    angle = position.astype(jnp.float32)[:, None] * freqs[None, :]
+    cosine = jnp.tile(jnp.cos(angle), (1, heads_here))
+    sine = jnp.tile(jnp.sin(angle), (1, heads_here))
+    turned_first = (first * cosine - second * sine).astype(jnp.bfloat16)
+    turned_second = (first * sine + second * cosine).astype(jnp.bfloat16)
     q_rope = jnp.transpose(
-        rotate(query_vectors[..., NOPE:], position).astype(jnp.bfloat16), (1, 0, 2)
+        jnp.concatenate(
+            [
+                turned_first.reshape(rows, heads_here, half),
+                turned_second.reshape(rows, heads_here, half),
+            ],
+            axis=-1,
+        ),
+        (1, 0, 2),
     )
     latent = rms_scale(kv_pre[:, :LATENT], kv_gain).astype(jnp.bfloat16)
     key_rope = rotate(kv_pre[:, LATENT:], position).astype(jnp.bfloat16)

time: 204 us -> 226 us (1.11)
  local copies, waits for them, and re-layouts: 22.8 us -> 42.1 us
  Pallas kernels: 28.3 us -> 36.3 us
  waiting for transfers between devices: 68.4 us -> 62.5 us
    pallas_call x1, Pallas kernels: 28.3 us -> 36.3 us  [attend(): pl.pallas_call(attention_kernel, grid=(rows // QBLOCK,), in_specs=[pl.Blo...]
    another operation x2 -> x6, local copies, waits for them, and re-layouts: 1.18 us -> 8.38 us  [the longest x2 4.55 us: body(): sine = jnp.tile(jnp.sin(angle), (1, heads_here))]
    slice x1 -> x6, local copies, waits for them, and re-layouts: 1.65 us -> 8.4 us  [the longest x1 6.59 us: body(): query_vectors = projections[:, :q_cols]]
    all_gather x1, waiting for transfers between devices: 66.6 us -> 60.6 us  [body(): joined = lax.all_gather(joined, 'wide', axis=0, tiled=True)]
    another operation x3 -> x2, other arithmetic: 7.65 us -> 3.26 us
    reshape x1 -> x8, local copies, waits for them, and re-layouts: 3.94 us -> 6.58 us  [the longest x1 1.79 us: body(): turned_second.reshape(rows, heads_here, half)]
    unnamed x22 -> x31, local copies, waits for them, and re-layouts: 8.35 us -> 7.61 us
  transfers between devices with their start and end apart: 4 -> 4, of which waited for: 2 -> 2; matrix products, arithmetic and copies ran while one was open for 7% -> 9% of each run, Pallas kernels for 0% -> 0%
where the time goes in v4:
time: 226 us; the launch traced here: 225 us
  waiting for transfers between devices  62.5 us (28%)
  local copies, waits for them, and re-layouts  42.1 us (19%)
  matrix products  40.2 us (18%)
  Pallas kernels  36.3 us (16%)
  other arithmetic  22.5 us (10%)
  between operations  19.4 us (9%)
  starting transfers between devices  2.32 us (1%)
    all_gather x1, waiting for transfers between devices, body(): joined = lax.all_gather(joined, 'wide', axis=0, tiled=True)  60.6 us
    pallas_call x1, Pallas kernels, attend(): pl.pallas_call(attention_kernel, grid=(rows // QBLOCK,), in_specs=[pl.Blo...  36.3 us
    dot_general x1, matrix products, body(): projections = jnp.dot(normed, joined, preferred_element_type=jnp.float32)  16.1 us
    unnamed x31, local copies, waits for them, and re-layouts  7.61 us
    dot_general x1, matrix products, body(): jnp.dot(attended, my_cols, preferred_element_type=jnp.float32)  7.23 us
    slice x1, local copies, waits for them, and re-layouts, body(): query_vectors = projections[:, :q_cols]  6.59 us
    dot_general x1, matrix products, body(): jnp.dot(attended, their_cols, preferred_element_type=jnp.float32)  5.87 us
    another operation x2, local copies, waits for them, and re-layouts, body(): sine = jnp.tile(jnp.sin(angle), (1, heads_here))  4.55 us
  transfers between devices with their start and end apart: 4, of which 2 were waited for; matrix products, arithmetic and copies ran while one was open for 9% of the time, Pallas kernels for 0%

profile of v4, /device:TPU:1, one launch (start us, length us, event | category | flops | bytes accessed | tf_op | source)
XLA Modules:
  0.0 225.4 jit_solution(12065476087550854670)
XLA Ops:
  7.2 1.2 reshape.211
  8.4 0.1 fusion.32
  8.5 0.1 reshape.213
  8.6 0.1 reshape.214
  8.8 1.5 pad_maximum_fusion.5
  10.2 1.5 collective-permute-start
  11.7 0.9 select_reduce_fusion.1
  12.6 0.7 fusion.34
  15.8 2.2 constant_dynamic-slice_fusion.7
  18.1 0.7 pad_maximum_fusion.2
  18.8 0.1 collective-permute-start.1
  18.9 0.7 fusion.33
  22.1 0.2 reduce-window.4
  22.4 0.1 broadcast_in_dim.13
  22.5 0.9 constant_dynamic-slice_fusion.3
  23.4 0.2 reshape.217
  23.6 0.1 fusion.31
  23.7 0.1 copy.82
  23.9 0.7 copy.63
  24.6 0.1 copy.83
  24.7 0.7 copy.64
  25.4 0.1 convert_reduce_fusion
  25.5 0.1 select_reduce_fusion
  25.6 1.0 copy.78.kst_ref
  26.7 0.6 multiply_exponential_fusion
  27.3 2.5 %broadcast_select_fusion.1 = (bf16[1024,1024]{1,0:T(8,128)(2,1)S(1)}, bf16[1024,1024]{1,0:T(8,128)(2,1)S(1)}) fusion(bf16[1024,1024]{1,0:T(8,128)(2,1)} %param.12, bf16[1024,1024]{1,0:T(8,128)(2,1)} %collective-permute-done, pred[]{:T(512)S(6)} %eq.53), kind=kLoop, calls=%fused_computation.18 | loop fusion | flops 2097152 | bytes 8388609 | tf_op jit(solution)/shard_map/jit(_where)/select_n | solution.py:143
  29.8 1.2 fusion
  31.0 2.8 %fusion.12 = f32[1024,64]{0,1:T(8,128)S(1)} fusion(bf16[2048,64]{1,0:T(8,128)(2,1)S(1)} %pad_maximum_fusion.2, bf16[2048,64]{1,0:T(8,128)(2,1)} %collective-permute-done.1, pred[64]{0:T(512)(128)(4,1)S(1)} %broadcast_in_dim.13, f32[2048]{0:T(1024)S(1)} %convert_element_type.91, f32[1024]{0:T(1024)S(1)} %add_rsqrt_fusion.1, ...), kind=kOutput, calls=%fused_computation.28 | convolution fusion | flops 283246592 | bytes 4993088 | tf_op jit(solution)/shard_map/dot_general | solution.py:172
  33.8 0.6 broadcast_multiply_fusion
  34.5 60.6 %all-gather.2.cloned.1.call-done = bf16[2048,2112]{1,0:T(8,128)(2,1)} async-done(((bf16[32,2112]{1,0:T(8,128)(2,1)}), bf16[2048,2112]{1,0:T(8,128)(2,1)}) %all-gather.2.cloned.1.call-update) | async-done | bytes 8650768 | tf_op jit(solution)/shard_map/all_gather | solution.py:139
  95.1 16.1 %fusion.28 = f32[1024,2112]{0,1:T(8,128)} fusion(bf16[2048,2112]{1,0:T(8,128)(2,1)} %all-gather.2.cloned.1.call-done, f32[2048]{0:T(1024)S(1)} %convert_element_type.91, f32[1024]{0:T(1024)S(1)} %add_rsqrt_fusion.1, bf16[1024,1024]{1,0:T(8,128)(2,1)} %copy-done.3, bf16[1024,1024]{1,0:T(8,128)(2,1)} %copy-done.2), kind=kOutput, calls=%fused_computation.74 | convolution fusion | flops 8873050112 | bytes 21508096 | tf_op jit(solution)/shard_map/dot_general | solution.py:168
  111.2 1.0 fusion.30
  112.2 1.8 multiply_reduce_fusion
  114.0 6.6 %slice.98 = f32[1024,1536]{0,1:T(8,128)} slice(f32[1024,2112]{0,1:T(8,128)} %fusion.28), slice={[0:1024], [0:1536]} | slice | bytes 12582912 | tf_op jit(solution)/shard_map/slice | solution.py:169
  120.6 0.2 copy.84
  120.8 0.2 copy.85
  121.0 6.6 %copy.81 = f32[1024,1536]{1,0:T(8,128)} copy(f32[1024,1536]{0,1:T(8,128)} %slice.98) | data formatting | bytes 12582912
  127.6 3.1 %subtract_convert_fusion.1 = (bf16[1024,32]{1,0:T(8,128)(2,1)}, bf16[1024,32]{1,0:T(8,128)(2,1)S(1)}, f32[1024,32]{1,0:T(8,128)}, f32[1024,32]{1,0:T(8,128)}) fusion(f32[1024,32]{1,0:T(8,128)S(1)} %copy.85, f32[1024,32]{1,0:T(8,128)S(1)} %copy.84, f32[1024]{0:T(1024)S(1)} %subtract_convert_fusion.2, f32[32]{0:T(128)S(1)} %copy-done.10), kind=kLoop, calls=%fused_computation.27 | loop fusion | flops 294912 | bytes 659584 | tf_op jit(solution)/shard_map/convert
  130.7 1.2 copy.66
  131.9 1.1 tile.8
  133.0 1.6 copy.67
  134.5 1.9 copy.68
  136.4 2.0 tile.20
  138.4 2.6 %copy.69 = f32[1024,256]{1,0:T(8,128)} copy(f32[1024,256]{0,1:T(8,128)} %bitcast.43) | data formatting | bytes 2097152 | tf_op jit(solution)/shard_map/tile | solution.py:196
  141.0 3.9 %multiply_add_fusion = f32[1024,1536]{1,0:T(8,128)S(1)} fusion(f32[1024,1536]{1,0:T(8,128)} %copy.81, bf16[1024,64]{0,1:T(8,128)(2,1)} %bitcast.47, bf16[64,256]{1,0:T(8,128)(2,1)} %copy.64, bf16[64,256]{1,0:T(8,128)(2,1)} %copy.63, bf16[64,1024]{1,0:T(8,128)(2,1)S(1)} %bitcast.46), kind=kOutput, calls=%fused_computation.5 | convolution fusion | flops 205062144 | bytes 12910592 | tf_op jit(solution)/shard_map/dot_general | solution.py:184
  144.9 1.6 slice.115.q_nope_ref
  146.5 1.3 subtract_convert_fusion
  147.8 1.3 copy.70
  149.1 1.7 copy.74
  150.8 0.2 copy.73
  151.0 1.8 copy.75
  152.8 2.0 multiply_convert_fusion
  154.8 0.2 copy-done.1
  155.0 4.1 %maximum_bitcast_fusion.q_rope_ref = bf16[8,1024,64]{2,1,0:T(8,128)(2,1)} fusion(bf16[1024,8,32]{2,0,1:T(8,128)(2,1)} %copy.75, bf16[1024,8,32]{2,0,1:T(8,128)(2,1)S(1)} %copy-done.1), kind=kLoop, calls=%fused_computation.10 | loop fusion | flops 2097152 | bytes 2097152 | tf_op jit(solution)/shard_map/transpose | solution.py:199
  159.2 0.8 pad_maximum_fusion.3.kr_ref
  160.0 4.3 %convolution_convert_fusion.kv_ref = bf16[1024,2048]{1,0:T(8,128)(2,1)} fusion(bf16[1024,512]{0,1:T(8,128)(2,1)S(1)} %multiply_convert_fusion, bf16[512,2048]{1,0:T(8,128)(2,1)S(1)} %copy-done), kind=kOutput, calls=%fused_computation.9 | convolution fusion | flops 2149580800 | bytes 7340032 | tf_op jit(solution)/shard_map/dot_general | solution.py:212
  164.4 36.3 %shard_map.131 = bf16[1024,1024]{1,0:T(8,128)(2,1)} custom-call(bf16[1024,1024]{1,0:T(8,128)(2,1)} %slice.115.q_nope_ref, bf16[8,1024,64]{2,1,0:T(8,128)(2,1)} %maximum_bitcast_fusion.q_rope_ref, bf16[1024,2048]{1,0:T(8,128)(2,1)} %convolution_convert_fusion.kv_ref, bf16[1024,64]{1,0:T(8,128)(2,1)} %pad_maximum_fusion.3.kr_ref, s32[1024,1]{1,0:T(8,128)} %copy.78.kst_ref), custom_call_target="tpu_custom_call" | custom-call | tf_op jit(solution)/shard_map/pallas_call | solution.py:84
  200.7 5.9 %fusion.7 = bf16[1024,1024]{1,0:T(8,128)(2,1)} fusion(bf16[1024,1024]{1,0:T(8,128)(2,1)} %shard_map.131, bf16[1024,2048]{1,0:T(8,128)(2,1)} %param.18, s32[]{:T(128)S(6)} %select_n.73), kind=kOutput, calls=%fused_computation.19 | convolution fusion | flops 2148532224 | bytes 6291460 | tf_op jit(solution)/shard_map/dot_general | solution.py:217
  206.5 0.7 collective-permute-start.2
  207.2 1.1 copy.79
  208.3 0.1 copy.80
  208.4 1.1 pad_maximum_fusion.1
  209.5 1.8 collective-permute-done.2
  211.4 7.2 %add_convert_fusion = bf16[1024,1024]{1,0:T(8,128)(2,1)} fusion(bf16[1024,1024]{1,0:T(8,128)(2,1)} %collective-permute-done.2, bf16[1024,1024]{1,0:T(8,128)(2,1)} %param.12, bf16[1024,1024]{1,0:T(8,128)(2,1)} %shard_map.131, bf16[1024,2048]{1,0:T(8,128)(2,1)} %param.18, s32[]{:T(128)S(6)} %select_n.72), kind=kOutput, calls=%fused_computation.8 | convolution fusion | flops 2154823680 | bytes 10485764 | tf_op jit(solution)/shard_map/dot_general | solution.py:219
  (43 shorter events, 0.3 us)
Async XLA Ops:
  7.2 152.9 %copy-start = (bf16[512,2048]{1,0:T(8,128)(2,1)S(1)}, bf16[512,2048]{1,0:T(8,128)(2,1)}, u32[]{:S(2)}) copy-start(bf16[512,2048]{1,0:T(8,128)(2,1)} %param.17) | copy-start | bytes 6291460
  7.2 87.9 %all-gather.2.cloned.1.call-start = ((), (), s32[]{:S(2)}) async-start(), calls=%async_computation | async-start | bytes 9052160 | tf_op jit(solution)/shard_map/all_gather | solution.py:139
  10.2 17.0 %collective-permute-start = (bf16[1024,1024]{1,0:T(8,128)(2,1)}, bf16[1024,1024]{1,0:T(8,128)(2,1)}, u32[]{:S(2)}, u32[]{:S(2)}) collective-permute-start(bf16[1024,1024]{1,0:T(8,128)(2,1)} %param.12), channel_id=1, source_target_pairs={{0,1},{1,0},{2,3},{3,2},{4,5},{5,4},{6,7},{7,6},{8,9},{9,8},{10,11... | collective-permute-start | bytes 6291464 | tf_op jit(solution)/shard_map/ppermute | solution.py:113
  15.8 3.1 %copy-start.7 = (s32[1,4]{1,0:T(1,128)S(1)}, s32[1,4]{1,0:T(1,128)}, u32[]{:S(2)}) copy-start(s32[1,4]{1,0:T(1,128)} %param.22) | copy-start | bytes 52
  15.8 6.2 %copy-start.8 = (bf16[2048]{0:T(1024)(128)(2,1)S(1)}, bf16[2048]{0:T(1024)(128)(2,1)}, u32[]{:S(2)}) copy-start(bf16[2048]{0:T(1024)(128)(2,1)} %param.13) | copy-start | bytes 12292
  15.8 6.3 %copy-start.11 = (s32[1,4]{1,0:T(1,128)S(1)}, s32[1,4]{1,0:T(1,128)}, u32[]{:S(2)}) copy-start(s32[1,4]{1,0:T(1,128)} %param.21) | copy-start | bytes 52
  15.8 6.4 %copy-start.9 = (bf16[512]{0:T(512)(128)(2,1)S(1)}, bf16[512]{0:T(512)(128)(2,1)}, u32[]{:S(2)}) copy-start(bf16[512]{0:T(512)(128)(2,1)} %param.16) | copy-start | bytes 3076
  18.8 12.2 %collective-permute-start.1 = (bf16[2048,64]{1,0:T(8,128)(2,1)S(1)}, bf16[2048,64]{1,0:T(8,128)(2,1)}, u32[]{:S(2)}, u32[]{:S(2)}) collective-permute-start(bf16[2048,64]{1,0:T(8,128)(2,1)S(1)} %pad_maximum_fusion.2), channel_id=1, source_target_pairs={{0,1},{1,0},{2,3},{3,2},{4,5},{5,4},{6,7},{7,6},{8,9},{9,8},{10,11... | collective-permute-start | bytes 786440 | tf_op jit(solution)/shard_map/ppermute | solution.py:113
  29.8 4.0 %copy-start.2 = (bf16[1024,1024]{1,0:T(8,128)(2,1)}, bf16[1024,1024]{1,0:T(8,128)(2,1)S(1)}, u32[]{:S(2)}) copy-start(bf16[1024,1024]{1,0:T(8,128)(2,1)S(1)} %get-tuple-element.6) | copy-start | bytes 6291460
  29.8 4.0 %copy-start.3 = (bf16[1024,1024]{1,0:T(8,128)(2,1)}, bf16[1024,1024]{1,0:T(8,128)(2,1)S(1)}, u32[]{:S(2)}) copy-start(bf16[1024,1024]{1,0:T(8,128)(2,1)S(1)} %get-tuple-element.7) | copy-start | bytes 6291460
  121.0 6.6 %copy-start.10 = (f32[32]{0:T(128)S(1)}, f32[32]{0:T(128)}, u32[]{:S(2)}) copy-start(f32[32]{0:T(128)} %multiply_exponential_fusion) | copy-start | bytes 388
  144.9 1.6 copy-start.4
  147.8 3.1 %copy-start.6 = (bf16[1024,256]{1,0:T(8,128)(2,1)S(1)}, bf16[1024,256]{1,0:T(8,128)(2,1)}, u32[]{:S(2)}) copy-start(bf16[1024,256]{1,0:T(8,128)(2,1)} %get-tuple-element.5) | copy-start | bytes 1572868
  152.8 2.2 copy-start.1
  155.0 4.1 %copy-start.5 = (bf16[1024,32]{1,0:T(8,128)(2,1)S(1)}, bf16[1024,32]{1,0:T(8,128)(2,1)}, u32[]{:S(2)}) copy-start(bf16[1024,32]{1,0:T(8,128)(2,1)} %get-tuple-element.16) | copy-start | bytes 196612
  206.5 4.8 %collective-permute-start.2 = (bf16[1024,1024]{1,0:T(8,128)(2,1)}, bf16[1024,1024]{1,0:T(8,128)(2,1)}, u32[]{:S(2)}, u32[]{:S(2)}) collective-permute-start(bf16[1024,1024]{1,0:T(8,128)(2,1)} %fusion.7), channel_id=1, source_target_pairs={{0,1},{1,0},{2,3},{3,2},{4,5},{5,4},{6,7},{7,6},{8,9},{9,8},{10,11... | collective-permute-start | bytes 6291464 | tf_op jit(solution)/shard_map/ppermute | solution.py:113
Sparse Core Ops, SparseCore 0:
  11.4 83.6 all-gather.1

commit v5 on v4

--- a/solution.py
+++ b/solution.py
@@ -11,8 +11,9 @@
 LATENT = 512
 RANK = 16
 LMAX = 512
-QBLOCK = 128
+QBLOCK = 256
 WINDOW = QBLOCK + LMAX
+PBLOCK = 256
 
 
 EPS = 1e-06
@@ -53,22 +54,82 @@
     return (prompt, position, adapter, slot)
 
 
-def attention_kernel(q_nope_ref, q_rope_ref, kv_ref, kr_ref, kst_ref, o_ref):
+def project_kernel(x_ref, w_ref, sp_ref, up_ref, cos_ref, sin_ref, gain_ref, kvb_ref,
+                   qn_ref, qf_ref, qs_ref, lat_ref, kr_ref, kv_ref):
+    x = x_ref[...]
+    sp = sp_ref[...]
+    nope = qn_ref.shape[1]
+    half = qf_ref.shape[1]
+
+    def query_part(lo, hi):
+        base = jnp.dot(x, w_ref[:, lo:hi], preferred_element_type=jnp.float32)
+        return base + ADAPTER_SCALE * jnp.dot(sp, up_ref[:, lo:hi], preferred_element_type=jnp.float32)
+
+    qn_ref[...] = query_part(0, nope).astype(qn_ref.dtype)
+    first = query_part(nope, nope + half)
+    second = query_part(nope + half, nope + 2 * half)
+    cosine = cos_ref[...]
+    sine = sin_ref[...]
+    qf_ref[...] = (first * cosine - second * sine).astype(qf_ref.dtype)
+    qs_ref[...] = (first * sine + second * cosine).astype(qs_ref.dtype)
+    q_end = nope + 2 * half
+    pre = jnp.dot(x, w_ref[:, q_end:q_end + LATENT], preferred_element_type=jnp.float32)
+    mean_sq = jnp.mean(pre * pre, axis=-1, keepdims=True)
+    latent = (pre * lax.rsqrt(mean_sq + EPS) * gain_ref[...]).astype(jnp.bfloat16)
+    lat_ref[...] = latent
+    kr_ref[...] = jnp.dot(x, w_ref[:, q_end + LATENT:], preferred_element_type=jnp.float32)
+    kv_ref[...] = jnp.dot(latent, kvb_ref[...], preferred_element_type=jnp.float32).astype(kv_ref.dtype)
+
+
+def project(normed, joined, spread, up_rows, cosine, sine, kv_gain, kvb_weight, heads):
+    rows, width = normed.shape
+    cols = joined.shape[1]
+    half = heads * ROPE // 2
+    nope = heads * NOPE
+    full = lambda shape: pl.BlockSpec(shape, lambda i: (0, 0))
+    part = lambda c: pl.BlockSpec((PBLOCK, c), lambda i: (i, 0))
+    return pl.pallas_call(
+        project_kernel,
+        grid=(rows // PBLOCK,),
+        in_specs=[
+            part(width), full((width, cols)), part(spread.shape[1]), full(up_rows.shape),
+            part(half), part(half), full((1, LATENT)), full(kvb_weight.shape),
+        ],
+        out_specs=[part(nope), part(half), part(half), part(LATENT), part(ROPE), part(kvb_weight.shape[1])],
+        out_shape=[
+            jax.ShapeDtypeStruct((rows, nope), jnp.bfloat16),
+            jax.ShapeDtypeStruct((rows, half), jnp.bfloat16),
+            jax.ShapeDtypeStruct((rows, half), jnp.bfloat16),
+            jax.ShapeDtypeStruct((rows, LATENT), jnp.bfloat16),
+            jax.ShapeDtypeStruct((rows, ROPE), jnp.float32),
+            jax.ShapeDtypeStruct((rows, kvb_weight.shape[1]), jnp.bfloat16),
+        ],
+    )(normed, joined, spread, up_rows, cosine, sine, kv_gain.astype(jnp.float32)[None, :], kvb_weight)
+
+
+def attention_kernel(q_nope_ref, qf_ref, qs_ref, kv_ref, kr_ref, kst_ref, o_ref):
     i = pl.program_id(0)
-    heads = q_rope_ref.shape[0]
+    heads = qf_ref.shape[1] * 2 // ROPE
+    half = ROPE // 2
     scale = 1.0 / jnp.sqrt(jnp.float32(NOPE + ROPE))
     start = pl.multiple_of(jnp.maximum(i * QBLOCK - LMAX, 0), 128)
     row = i * QBLOCK + lax.broadcasted_iota(jnp.int32, (QBLOCK, WINDOW), 0)
     col = start + lax.broadcasted_iota(jnp.int32, (QBLOCK, WINDOW), 1)
     allowed = (col >= kst_ref[...]) & (col <= row)
     kr = kr_ref[pl.ds(start, WINDOW), :]
+    kf = kr[:, :half]
+    ks = kr[:, half:]
+    qf_all = qf_ref[...]
+    qs_all = qs_ref[...]
     for h in range(heads):
         qn = q_nope_ref[:, h * NOPE:(h + 1) * NOPE]
-        qr = q_rope_ref[h]
+        qf = qf_all[:, h * half:(h + 1) * half]
+        qs = qs_all[:, h * half:(h + 1) * half]
         kn = kv_ref[pl.ds(start, WINDOW), h * (NOPE + VDIM):h * (NOPE + VDIM) + NOPE]
         s = lax.dot_general(qn, kn, (((1,), (1,)), ((), ())), preferred_element_type=jnp.float32)
-        s = s + lax.dot_general(qr, kr, (((1,), (1,)), ((), ())), preferred_element_type=jnp.float32)
-        s = jnp.where(allowed, s * scale, jnp.float32(-1e30))
+        rope = lax.dot_general(qf, kf, (((1,), (1,)), ((), ())), preferred_element_type=jnp.float32)
+        rope = rope + lax.dot_general(qs, ks, (((1,), (1,)), ((), ())), preferred_element_type=jnp.float32)
+        s = jnp.where(allowed, (s + rope) * scale, jnp.float32(-1e30))
         top = jnp.max(s, axis=1, keepdims=True)
         e = jnp.exp(s - top)
         w = (e * (1.0 / jnp.sum(e, axis=1, keepdims=True))).astype(jnp.bfloat16)
@@ -78,22 +139,24 @@
         ).astype(o_ref.dtype)
 
 
-def attend(q_nope, q_rope, kv, key_rope, key_start):
+def attend(q_nope, q_first, q_second, kv, key_rope, key_start):
     rows = q_nope.shape[0]
-    heads = q_rope.shape[0]
+    heads = q_nope.shape[1] // NOPE
+    half = q_first.shape[1]
     return pl.pallas_call(
         attention_kernel,
         grid=(rows // QBLOCK,),
         in_specs=[
             pl.BlockSpec((QBLOCK, heads * NOPE), lambda i: (i, 0)),
-            pl.BlockSpec((heads, QBLOCK, ROPE), lambda i: (0, i, 0)),
+            pl.BlockSpec((QBLOCK, half), lambda i: (i, 0)),
+            pl.BlockSpec((QBLOCK, half), lambda i: (i, 0)),
             pl.BlockSpec((rows, heads * (NOPE + VDIM)), lambda i: (0, 0)),
             pl.BlockSpec((rows, ROPE), lambda i: (0, 0)),
             pl.BlockSpec((QBLOCK, 1), lambda i: (i, 0)),
         ],
         out_specs=pl.BlockSpec((QBLOCK, heads * VDIM), lambda i: (i, 0)),
         out_shape=jax.ShapeDtypeStruct((rows, heads * VDIM), jnp.bfloat16),
-    )(q_nope, q_rope, kv, key_rope, key_start[:, None])
+    )(q_nope, q_first, q_second, kv, key_rope, key_start[:, None])
 
 
 def split_heads(weight, heads):
@@ -165,9 +228,6 @@
     prompt, position, adapter, slot = token_tables(
         lengths[0], adapter_ids[0], adapter_slot, local_pos
     )
-    projections = jnp.dot(normed, joined, preferred_element_type=jnp.float32)
-    query_vectors = projections[:, :q_cols]
-    kv_pre = projections[:, q_cols:]
     member = (prompt[:, None] == jnp.arange(prompts_here)[None, :]).astype(jnp.float32)
     low = jnp.dot(normed, chosen, preferred_element_type=jnp.float32).reshape(
         rows, prompts_here, RANK
@@ -181,37 +241,18 @@
     spread_rows = (member.astype(jnp.bfloat16)[:, :, None] * lowrank[:, None, :]).reshape(
         rows, prompts_here * RANK
     )
-    query_vectors = query_vectors + ADAPTER_SCALE * jnp.dot(
-        spread_rows, up_weight_rows, preferred_element_type=jnp.float32
-    )
-    nope_cols = heads_here * NOPE
-    half_cols = heads_here * (ROPE // 2)
-    q_nope = query_vectors[:, :nope_cols].astype(jnp.bfloat16)
-    first = query_vectors[:, nope_cols:nope_cols + half_cols]
-    second = query_vectors[:, nope_cols + half_cols:]
     half = ROPE // 2
     freqs = jnp.exp(-jnp.log(THETA) * 2.0 * jnp.arange(half).astype(jnp.float32) / (2 * half))
     angle = position.astype(jnp.float32)[:, None] * freqs[None, :]
     cosine = jnp.tile(jnp.cos(angle), (1, heads_here))
     sine = jnp.tile(jnp.sin(angle), (1, heads_here))
-    turned_first = (first * cosine - second * sine).astype(jnp.bfloat16)
-    turned_second = (first * sine + second * cosine).astype(jnp.bfloat16)
-    q_rope = jnp.transpose(
-        jnp.concatenate(
-            [
-                turned_first.reshape(rows, heads_here, half),
-                turned_second.reshape(rows, heads_here, half),
-            ],
-            axis=-1,
-        ),
-        (1, 0, 2),
-    )
-    latent = rms_scale(kv_pre[:, :LATENT], kv_gain).astype(jnp.bfloat16)
-    key_rope = rotate(kv_pre[:, LATENT:], position).astype(jnp.bfloat16)
+    q_nope, q_first, q_second, latent, key_pre, expanded = project(
+        normed, joined, spread_rows, up_weight_rows, cosine, sine, kv_gain, kvb_weight, heads_here
+    )
+    key_rope = rotate(key_pre, position).astype(jnp.bfloat16)
     latent_cache = jnp.concatenate([latent, key_rope], axis=1)
-    expanded = jnp.dot(latent, kvb_weight, preferred_element_type=jnp.float32).astype(jnp.bfloat16)
     key_start = (local_pos - position).astype(jnp.int32)
-    attended = attend(q_nope, q_rope, expanded, key_rope, key_start)
+    attended = attend(q_nope, q_first, q_second, expanded, key_rope, key_start)
     their_cols = lax.dynamic_slice_in_dim(o_weight, (1 - me) * half_width, half_width, 1)
     my_cols = lax.dynamic_slice_in_dim(o_weight, me * half_width, half_width, 1)
     theirs = jnp.dot(attended, their_cols, preferred_element_type=jnp.float32).astype(jnp.bfloat16)

time: 226 us -> 173 us (0.77)
  local copies, waits for them, and re-layouts: 42.1 us -> 13.9 us
  matrix products: 40.2 us -> 14.6 us
  Pallas kernels: 36.3 us -> 48.2 us
  other arithmetic: 22.5 us -> 16.5 us
  waiting for transfers between devices: 62.5 us -> 58 us
    dot_general x3 -> x0, matrix products: 24.3 us -> none  [the longest x1 16.1 us: body(): projections = jnp.dot(normed, joined, preferred_element_type=jnp.float32)]
    pallas_call x0 -> x1, Pallas kernels: none -> 19.4 us  [project(): pl.pallas_call(project_kernel, grid=(rows // PBLOCK,), in_specs=[part(wid...]
    slice x3 -> x0, local copies, waits for them, and re-layouts: 9.16 us -> none  [the longest x1 6.59 us: body(): query_vectors = projections[:, :q_cols]]
    pallas_call x1, Pallas kernels: 36.3 us -> 28.8 us  [attend(): pl.pallas_call(attention_kernel, grid=(rows // QBLOCK,), in_specs=[pl.Blo...]
    unnamed x31 -> x17, local copies, waits for them, and re-layouts: 7.61 us -> 2.26 us
    all_gather x1, waiting for transfers between devices: 60.6 us -> 55.5 us  [body(): joined = lax.all_gather(joined, 'wide', axis=0, tiled=True)]
    transpose x1 -> x0, other arithmetic: 4.14 us -> none  [body(): jnp.transpose(jnp.concatenate([turned_first.reshape(rows, heads_here, hal...]
    reshape x2 -> x0, local copies, waits for them, and re-layouts: 3.53 us -> none  [the longest x1 1.79 us: body(): turned_second.reshape(rows, heads_here, half)]
  transfers between devices with their start and end apart: 4 -> 4, of which waited for: 2 -> 2; matrix products, arithmetic and copies ran while one was open for 9% -> 14% of each run, Pallas kernels for 0% -> 0%
where the time goes in v5:
time: 173 us
  waiting for transfers between devices  58 us (34%)
  Pallas kernels  48.2 us (28%)
  between operations  19.3 us (11%)
  other arithmetic  16.5 us (10%)
  matrix products  14.6 us (8%)
  local copies, waits for them, and re-layouts  13.9 us (8%)
  starting transfers between devices  2.31 us (1%)
    all_gather x1, waiting for transfers between devices, body(): joined = lax.all_gather(joined, 'wide', axis=0, tiled=True)  55.5 us
    pallas_call x1, Pallas kernels, attend(): pl.pallas_call(attention_kernel, grid=(rows // QBLOCK,), in_specs=[pl.Blo...  28.8 us
    pallas_call x1, Pallas kernels, project(): pl.pallas_call(project_kernel, grid=(rows // PBLOCK,), in_specs=[part(wid...  19.4 us
    dot_general x1, matrix products, body(): jnp.dot(attended, my_cols, preferred_element_type=jnp.float32)  7.23 us
    dot_general x1, matrix products, body(): jnp.dot(attended, their_cols, preferred_element_type=jnp.float32)  5.96 us
    another operation x2, other arithmetic  3.98 us
  transfers between devices with their start and end apart: 4, of which 2 were waited for; matrix products, arithmetic and copies ran while one was open for 14% of the time, Pallas kernels for 0%

profile of v5, /device:TPU:1, one launch (start us, length us, event | category | flops | bytes accessed | tf_op | source)
XLA Modules:
  0.0 172.7 jit_solution(11125690584638648872)
XLA Ops:
  7.2 0.0 all-gather.2.cloned.1.call-start
  7.2 1.1 reshape.196
  8.3 0.1 fusion.22
  8.4 0.1 reshape.198
  8.5 0.1 reshape.199
  8.6 1.5 pad_maximum_fusion.6
  10.1 0.0 all-gather.2.cloned.1.call-update
  10.1 0.9 select_reduce_fusion.1
  11.0 0.7 fusion.24
  14.1 0.0 copy-start.2
  14.1 0.0 copy-start.3
  14.1 0.0 copy-start.5
  14.1 2.3 %constant_dynamic-slice_fusion.7 = (bf16[2048,16]{1,0:T(8,128)(2,1)S(1)}, bf16[2048,16]{1,0:T(8,128)(2,1)S(1)}, bf16[2048,16]{1,0:T(8,128)(2,1)S(1)}, bf16[2048,16]{1,0:T(8,128)(2,1)S(1)}) fusion(bf16[2048,512]{1,0:T(8,128)(2,1)} %param.19, s32[]{:T(128)S(6)} %select_n.63, s32[]{:T(128)S(6)} %select_n.64, s32[]{:T(128)S(6)} %select_n.66, s32[]{:T(128)S(6)} %select_n.65), kind=kLoop, calls=%fused_computation.47 | loop fusion | bytes 524304 | tf_op jit(solution)/shard_map/dynamic_slice | solution.py:217
  16.4 0.7 pad_maximum_fusion.2
  17.1 1.5 collective-permute-start.1
  18.6 0.1 collective-permute-start
  18.7 0.0 copy-done.2
  18.7 0.6 fusion.23
  21.9 0.0 copy-done.3
  21.9 0.1 broadcast_in_dim.16
  22.0 0.1 broadcast_in_dim.17
  22.1 0.0 copy-done.5
  22.1 0.2 reduce-window.4
  22.2 0.9 constant_dynamic-slice_fusion.3
  23.1 0.2 reshape.202
  23.4 0.1 fusion.21
  23.5 0.1 copy.50
  23.6 0.1 copy.40
  23.7 0.1 copy.51
  23.9 0.1 copy.41
  24.0 0.1 convert_reduce_fusion
  24.1 0.1 select_reduce_fusion
  24.2 1.9 %multiply_sine_fusion = (f32[1024,32]{1,0:T(8,128)S(1)}, f32[1024,32]{1,0:T(8,128)S(1)}) fusion(f32[1024]{0:T(1024)S(1)} %subtract_convert_fusion.1, f32[32]{0:T(128)S(1)} %multiply_exponential_fusion), kind=kLoop, calls=%fused_computation.15 | loop fusion | flops 32768 | bytes 266368 | tf_op jit(solution)/shard_map/sin | solution.py:248
  26.1 0.2 copy.43
  26.3 0.1 tile.8
  26.4 0.0 copy-start.4
  26.4 1.3 copy.46.cos_ref
  27.7 0.2 copy.44
  27.9 0.1 tile.20
  28.0 1.3 copy.47.sin_ref
  29.3 0.0 copy-done.4
  29.3 0.6 broadcast_in_dim.21
  29.9 1.0 copy.48.kst_ref
  31.0 0.7 pad_maximum_fusion.5.up_ref
  31.7 0.0 collective-permute-done
  31.7 2.5 %broadcast_select_fusion.1 = (bf16[1024,1024]{1,0:T(8,128)(2,1)S(1)}, bf16[1024,1024]{1,0:T(8,128)(2,1)S(1)}) fusion(bf16[1024,1024]{1,0:T(8,128)(2,1)} %param.12, bf16[1024,1024]{1,0:T(8,128)(2,1)} %collective-permute-done, pred[]{:T(512)S(6)} %eq.53), kind=kLoop, calls=%fused_computation.12 | loop fusion | flops 2097152 | bytes 8388609 | tf_op jit(solution)/shard_map/jit(_where)/select_n | solution.py:206
  34.2 1.2 fusion
  35.3 1.4 fusion.2.x_ref
  36.8 0.0 copy-start
  36.8 0.0 collective-permute-done.1
  36.8 1.4 fusion.12
  38.2 0.5 copy-done
  38.7 0.9 copy.45.sp_ref
  39.6 55.5 %all-gather.2.cloned.1.call-done.w_ref = bf16[2048,2112]{1,0:T(8,128)(2,1)} async-done(((bf16[32,2112]{1,0:T(8,128)(2,1)}), bf16[2048,2112]{1,0:T(8,128)(2,1)}) %all-gather.2.cloned.1.call-update) | async-done | bytes 8650768 | tf_op jit(solution)/shard_map/all_gather | solution.py:202
  95.1 19.4 %shard_map.131 = (bf16[1024,1024]{1,0:T(8,128)(2,1)}, bf16[1024,256]{1,0:T(8,128)(2,1)}, bf16[1024,256]{1,0:T(8,128)(2,1)}, bf16[1024,512]{1,0:T(8,128)(2,1)}, f...) custom-call(bf16[1024,2048]{1,0:T(8,128)(2,1)} %copy-done, bf16[2048,2112]{1,0:T(8,128)(2,1)} %all-gather.2.cloned.1.call-done.w_ref, ...), custom_call_target="tpu_custom_call" | custom-call | tf_op jit(solution)/shard_map/pallas_call | solution.py:91
  114.5 3.8 %subtract_convert_fusion = (bf16[1024,32]{1,0:T(8,128)(2,1)S(1)}, bf16[1024,32]{1,0:T(8,128)(2,1)S(1)}) fusion(f32[1024,64]{1,0:T(8,128)} %get-tuple-element.12, f32[1024]{0:T(1024)S(1)} %subtract_convert_fusion.1, f32[32]{0:T(128)S(1)} %multiply_exponential_fusion), kind=kLoop, calls=%fused_computation.19 | loop fusion | flops 294912 | bytes 397440 | tf_op jit(solution)/shard_map/convert.1
  118.3 0.9 pad_maximum_fusion.3.kr_ref
  119.1 28.8 %shard_map.132 = bf16[1024,1024]{1,0:T(8,128)(2,1)} custom-call(bf16[1024,1024]{1,0:T(8,128)(2,1)} %get-tuple-element.8.q_nope_ref, bf16[1024,256]{1,0:T(8,128)(2,1)} %get-tuple-element.9.qf_ref, bf16[1024,256]{1,0:T(8,128)(2,1)} %get-tuple-element.10.qs_ref, bf16[1024,2048]{1,0:T(8,128)(2,1)} %get-tuple-element.11.kv_ref, ...), custom_call_target="tpu_custom_call" | custom-call | tf_op jit(solution)/shard_map/pallas_call | solution.py:146
  147.9 6.0 %fusion.7 = bf16[1024,1024]{1,0:T(8,128)(2,1)} fusion(bf16[1024,1024]{1,0:T(8,128)(2,1)} %shard_map.132, bf16[1024,2048]{1,0:T(8,128)(2,1)} %param.18, s32[]{:T(128)S(6)} %select_n.73), kind=kOutput, calls=%fused_computation.13 | convolution fusion | flops 2148532224 | bytes 6291460 | tf_op jit(solution)/shard_map/dot_general | solution.py:258
  153.9 0.7 collective-permute-start.2
  154.5 0.2 pad_maximum_fusion.1
  154.7 1.4 copy.49
  156.2 2.5 %collective-permute-done.2 = bf16[1024,1024]{1,0:T(8,128)(2,1)} collective-permute-done((bf16[1024,1024]{1,0:T(8,128)(2,1)}, bf16[1024,1024]{1,0:T(8,128)(2,1)}, u32[]{:S(2)}, u32[]{:S(2)}) %collective-permute-start.2) | collective-permute-done | bytes 2097184 | tf_op jit(solution)/shard_map/ppermute | solution.py:176
  158.7 7.2 %add_convert_fusion = bf16[1024,1024]{1,0:T(8,128)(2,1)} fusion(bf16[1024,1024]{1,0:T(8,128)(2,1)} %collective-permute-done.2, bf16[1024,1024]{1,0:T(8,128)(2,1)} %param.12, bf16[1024,1024]{1,0:T(8,128)(2,1)} %shard_map.132, bf16[1024,2048]{1,0:T(8,128)(2,1)} %param.18, s32[]{:T(128)S(6)} %select_n.72), kind=kOutput, calls=%fused_computation.6 | convolution fusion | flops 2154823680 | bytes 10485764 | tf_op jit(solution)/shard_map/dot_general | solution.py:260
  (17 shorter events, 0.2 us)
Async XLA Ops:
  7.2 87.9 %all-gather.2.cloned.1.call-start = ((), (), s32[]{:S(2)}) async-start(), calls=%async_computation | async-start | bytes 9052160 | tf_op jit(solution)/shard_map/all_gather | solution.py:202
  14.1 4.6 %copy-start.2 = (s32[1,4]{1,0:T(1,128)S(1)}, s32[1,4]{1,0:T(1,128)}, u32[]{:S(2)}) copy-start(s32[1,4]{1,0:T(1,128)} %param.22) | copy-start | bytes 52
  14.1 7.7 %copy-start.3 = (bf16[2048]{0:T(1024)(128)(2,1)S(1)}, bf16[2048]{0:T(1024)(128)(2,1)}, u32[]{:S(2)}) copy-start(bf16[2048]{0:T(1024)(128)(2,1)} %param.13) | copy-start | bytes 12292
  14.1 7.9 %copy-start.5 = (s32[1,4]{1,0:T(1,128)S(1)}, s32[1,4]{1,0:T(1,128)}, u32[]{:S(2)}) copy-start(s32[1,4]{1,0:T(1,128)} %param.21) | copy-start | bytes 52
  17.1 19.7 %collective-permute-start.1 = (bf16[2048,64]{1,0:T(8,128)(2,1)S(1)}, bf16[2048,64]{1,0:T(8,128)(2,1)S(1)}, u32[]{:S(2)}, u32[]{:S(2)}) collective-permute-start(bf16[2048,64]{1,0:T(8,128)(2,1)S(1)} %pad_maximum_fusion.2), channel_id=1, source_target_pairs={{0,1},{1,0},{2,3},{3,2},{4,5},{5,4},{6,7},{7,6},{8,9},{9,8},{10,11... | collective-permute-start | bytes 786440 | tf_op jit(solution)/shard_map/ppermute | solution.py:176
  18.6 13.1 %collective-permute-start = (bf16[1024,1024]{1,0:T(8,128)(2,1)}, bf16[1024,1024]{1,0:T(8,128)(2,1)}, u32[]{:S(2)}, u32[]{:S(2)}) collective-permute-start(bf16[1024,1024]{1,0:T(8,128)(2,1)} %param.12), channel_id=1, source_target_pairs={{0,1},{1,0},{2,3},{3,2},{4,5},{5,4},{6,7},{7,6},{8,9},{9,8},{10,11... | collective-permute-start | bytes 6291464 | tf_op jit(solution)/shard_map/ppermute | solution.py:176
  26.4 2.9 %copy-start.4 = (bf16[512]{0:T(512)(128)(2,1)S(1)}, bf16[512]{0:T(512)(128)(2,1)}, u32[]{:S(2)}) copy-start(bf16[512]{0:T(512)(128)(2,1)} %param.16) | copy-start | bytes 3076
  36.8 1.9 %copy-start = (bf16[1024,2048]{1,0:T(8,128)(2,1)}, bf16[1024,2048]{1,0:T(8,128)(2,1)S(1)}, u32[]{:S(2)}) copy-start(bf16[1024,2048]{1,0:T(8,128)(2,1)S(1)} %fusion.2.x_ref) | copy-start | bytes 12582916
  147.9 6.6 %copy-start.1 = (bf16[1024,512]{1,0:T(8,128)(2,1)S(1)}, bf16[1024,512]{1,0:T(8,128)(2,1)}, u32[]{:S(2)}) copy-start(bf16[1024,512]{1,0:T(8,128)(2,1)} %get-tuple-element.13) | copy-start | bytes 3145732
  153.9 4.8 %collective-permute-start.2 = (bf16[1024,1024]{1,0:T(8,128)(2,1)}, bf16[1024,1024]{1,0:T(8,128)(2,1)}, u32[]{:S(2)}, u32[]{:S(2)}) collective-permute-start(bf16[1024,1024]{1,0:T(8,128)(2,1)} %fusion.7), channel_id=1, source_target_pairs={{0,1},{1,0},{2,3},{3,2},{4,5},{5,4},{6,7},{7,6},{8,9},{9,8},{10,11... | collective-permute-start | bytes 6291464 | tf_op jit(solution)/shard_map/ppermute | solution.py:176
Sparse Core Ops, SparseCore 0:
  11.3 83.6 all-gather.1

commit v6 on v5

--- a/solution.py
+++ b/solution.py
@@ -55,7 +55,7 @@
 
 
 def project_kernel(x_ref, w_ref, sp_ref, up_ref, cos_ref, sin_ref, gain_ref, kvb_ref,
-                   qn_ref, qf_ref, qs_ref, lat_ref, kr_ref, kv_ref):
+                   qn_ref, qf_ref, qs_ref, cache_ref, kv_ref):
     x = x_ref[...]
     sp = sp_ref[...]
     nope = qn_ref.shape[1]
@@ -76,8 +76,14 @@
     pre = jnp.dot(x, w_ref[:, q_end:q_end + LATENT], preferred_element_type=jnp.float32)
     mean_sq = jnp.mean(pre * pre, axis=-1, keepdims=True)
     latent = (pre * lax.rsqrt(mean_sq + EPS) * gain_ref[...]).astype(jnp.bfloat16)
-    lat_ref[...] = latent
-    kr_ref[...] = jnp.dot(x, w_ref[:, q_end + LATENT:], preferred_element_type=jnp.float32)
+    cache_ref[:, :LATENT] = latent
+    key = jnp.dot(x, w_ref[:, q_end + LATENT:], preferred_element_type=jnp.float32)
+    key_first = key[:, :ROPE // 2]
+    key_second = key[:, ROPE // 2:]
+    cosine = cosine[:, :ROPE // 2]
+    sine = sine[:, :ROPE // 2]
+    cache_ref[:, LATENT:LATENT + ROPE // 2] = (key_first * cosine - key_second * sine).astype(cache_ref.dtype)
+    cache_ref[:, LATENT + ROPE // 2:] = (key_first * sine + key_second * cosine).astype(cache_ref.dtype)
     kv_ref[...] = jnp.dot(latent, kvb_ref[...], preferred_element_type=jnp.float32).astype(kv_ref.dtype)
 
 
@@ -95,19 +101,19 @@
             part(width), full((width, cols)), part(spread.shape[1]), full(up_rows.shape),
             part(half), part(half), full((1, LATENT)), full(kvb_weight.shape),
         ],
-        out_specs=[part(nope), part(half), part(half), part(LATENT), part(ROPE), part(kvb_weight.shape[1])],
+        out_specs=[part(nope), part(half), part(half), part(LATENT + ROPE), part(kvb_weight.shape[1])],
         out_shape=[
             jax.ShapeDtypeStruct((rows, nope), jnp.bfloat16),
             jax.ShapeDtypeStruct((rows, half), jnp.bfloat16),
             jax.ShapeDtypeStruct((rows, half), jnp.bfloat16),
-            jax.ShapeDtypeStruct((rows, LATENT), jnp.bfloat16),
-            jax.ShapeDtypeStruct((rows, ROPE), jnp.float32),
+            jax.ShapeDtypeStruct((rows, LATENT + ROPE), jnp.bfloat16),
             jax.ShapeDtypeStruct((rows, kvb_weight.shape[1]), jnp.bfloat16),
         ],
     )(normed, joined, spread, up_rows, cosine, sine, kv_gain.astype(jnp.float32)[None, :], kvb_weight)
 
 
-def attention_kernel(q_nope_ref, qf_ref, qs_ref, kv_ref, kr_ref, kst_ref, o_ref):
+def attention_kernel(me_ref, q_nope_ref, qf_ref, qs_ref, kv_ref, cache_ref, kst_ref, wt_ref, wm_ref,
+                     theirs_ref, mine_ref, att_ref):
     i = pl.program_id(0)
     heads = qf_ref.shape[1] * 2 // ROPE
     half = ROPE // 2
@@ -116,7 +122,7 @@
     row = i * QBLOCK + lax.broadcasted_iota(jnp.int32, (QBLOCK, WINDOW), 0)
     col = start + lax.broadcasted_iota(jnp.int32, (QBLOCK, WINDOW), 1)
     allowed = (col >= kst_ref[...]) & (col <= row)
-    kr = kr_ref[pl.ds(start, WINDOW), :]
+    kr = cache_ref[pl.ds(start, WINDOW), LATENT:LATENT + ROPE]
     kf = kr[:, :half]
     ks = kr[:, half:]
     qf_all = qf_ref[...]
@@ -134,29 +140,46 @@
         e = jnp.exp(s - top)
         w = (e * (1.0 / jnp.sum(e, axis=1, keepdims=True))).astype(jnp.bfloat16)
         v = kv_ref[pl.ds(start, WINDOW), h * (NOPE + VDIM) + NOPE:(h + 1) * (NOPE + VDIM)]
-        o_ref[:, h * VDIM:(h + 1) * VDIM] = jnp.dot(
+        att_ref[:, h * VDIM:(h + 1) * VDIM] = jnp.dot(
             w, v, preferred_element_type=jnp.float32
-        ).astype(o_ref.dtype)
-
-
-def attend(q_nope, q_first, q_second, kv, key_rope, key_start):
+        ).astype(att_ref.dtype)
+    att = att_ref[...]
+    theirs_ref[...] = jnp.dot(att, wt_ref[...], preferred_element_type=jnp.float32).astype(theirs_ref.dtype)
+    mine_ref[...] = jnp.dot(att, wm_ref[...], preferred_element_type=jnp.float32).astype(mine_ref.dtype)
+
+
+def attend(me, q_nope, q_first, q_second, kv, latent_cache, key_start, o_weight):
     rows = q_nope.shape[0]
     heads = q_nope.shape[1] // NOPE
     half = q_first.shape[1]
+    out_half = o_weight.shape[1] // 2
+    grid_spec = pltpu.PrefetchScalarGridSpec(
+        num_scalar_prefetch=1,
+        grid=(rows // QBLOCK,),
+        in_specs=[
+            pl.BlockSpec((QBLOCK, heads * NOPE), lambda i, m: (i, 0)),
+            pl.BlockSpec((QBLOCK, half), lambda i, m: (i, 0)),
+            pl.BlockSpec((QBLOCK, half), lambda i, m: (i, 0)),
+            pl.BlockSpec((rows, heads * (NOPE + VDIM)), lambda i, m: (0, 0)),
+            pl.BlockSpec((rows, LATENT + ROPE), lambda i, m: (0, 0)),
+            pl.BlockSpec((QBLOCK, 1), lambda i, m: (i, 0)),
+            pl.BlockSpec((heads * VDIM, out_half), lambda i, m: (0, 1 - m[0])),
+            pl.BlockSpec((heads * VDIM, out_half), lambda i, m: (0, m[0])),
+        ],
+        out_specs=[
+            pl.BlockSpec((QBLOCK, out_half), lambda i, m: (i, 0)),
+            pl.BlockSpec((QBLOCK, out_half), lambda i, m: (i, 0)),
+        ],
+        scratch_shapes=[pltpu.VMEM((QBLOCK, heads * VDIM), jnp.bfloat16)],
+    )
     return pl.pallas_call(
         attention_kernel,
-        grid=(rows // QBLOCK,),
-        in_specs=[
-            pl.BlockSpec((QBLOCK, heads * NOPE), lambda i: (i, 0)),
-            pl.BlockSpec((QBLOCK, half), lambda i: (i, 0)),
-            pl.BlockSpec((QBLOCK, half), lambda i: (i, 0)),
-            pl.BlockSpec((rows, heads * (NOPE + VDIM)), lambda i: (0, 0)),
-            pl.BlockSpec((rows, ROPE), lambda i: (0, 0)),
-            pl.BlockSpec((QBLOCK, 1), lambda i: (i, 0)),
-        ],
-        out_specs=pl.BlockSpec((QBLOCK, heads * VDIM), lambda i: (i, 0)),
-        out_shape=jax.ShapeDtypeStruct((rows, heads * VDIM), jnp.bfloat16),
-    )(q_nope, q_first, q_second, kv, key_rope, key_start[:, None])
+        grid_spec=grid_spec,
+        out_shape=[
+            jax.ShapeDtypeStruct((rows, out_half), jnp.bfloat16),
+            jax.ShapeDtypeStruct((rows, out_half), jnp.bfloat16),
+        ],
+    )(me, q_nope, q_first, q_second, kv, latent_cache, key_start[:, None], o_weight, o_weight)
 
 
 def split_heads(weight, heads):
@@ -246,18 +269,15 @@
     angle = position.astype(jnp.float32)[:, None] * freqs[None, :]
     cosine = jnp.tile(jnp.cos(angle), (1, heads_here))
     sine = jnp.tile(jnp.sin(angle), (1, heads_here))
-    q_nope, q_first, q_second, latent, key_pre, expanded = project(
+    q_nope, q_first, q_second, latent_cache, expanded = project(
         normed, joined, spread_rows, up_weight_rows, cosine, sine, kv_gain, kvb_weight, heads_here
     )
-    key_rope = rotate(key_pre, position).astype(jnp.bfloat16)
-    latent_cache = jnp.concatenate([latent, key_rope], axis=1)
     key_start = (local_pos - position).astype(jnp.int32)
-    attended = attend(q_nope, q_first, q_second, expanded, key_rope, key_start)
-    their_cols = lax.dynamic_slice_in_dim(o_weight, (1 - me) * half_width, half_width, 1)
-    my_cols = lax.dynamic_slice_in_dim(o_weight, me * half_width, half_width, 1)
-    theirs = jnp.dot(attended, their_cols, preferred_element_type=jnp.float32).astype(jnp.bfloat16)
+    theirs, mine = attend(
+        me.astype(jnp.int32).reshape(1), q_nope, q_first, q_second, expanded, latent_cache,
+        key_start, o_weight,
+    )
     received = swap(theirs)
-    mine = jnp.dot(attended, my_cols, preferred_element_type=jnp.float32).astype(jnp.bfloat16)
     projected = mine.astype(jnp.float32) + received.astype(jnp.float32)
     hidden = (tokens.astype(jnp.float32) + projected).astype(jnp.bfloat16)
     return (hidden, latent_cache)

time: 173 us -> 166 us (0.960)
  matrix products: 14.6 us -> 3.41 us
  Pallas kernels: 48.2 us -> 54.5 us
    dot_general x2 -> x0, matrix products: 13.2 us -> none  [the longest x1 7.23 us: body(): jnp.dot(attended, my_cols, preferred_element_type=jnp.float32)]
    pallas_call x1, Pallas kernels: 28.8 us -> 35.1 us  [attend(): pl.pallas_call(attention_kernel, grid_spec=grid_spec, out_shape=[jax.Shap...]
    convert_element_type x0 -> x1, other arithmetic: none -> 5.01 us  [body(): hidden = (tokens.astype(jnp.float32) + projected).astype(jnp.bfloat16)]
    another operation x2 -> x1, other arithmetic: 3.98 us -> 0.18 us
    dot_general x1, matrix products: 1.41 us -> 3.41 us  [body(): jnp.dot(normed, chosen, preferred_element_type=jnp.float32)]
where the time goes in v6:
time: 166 us
  waiting for transfers between devices  57.7 us (35%)
  Pallas kernels  54.5 us (33%)
  between operations  19.4 us (12%)
  other arithmetic  15.5 us (9%)
  local copies, waits for them, and re-layouts  13 us (8%)
  matrix products  3.41 us (2%)
  starting transfers between devices  2.13 us (1%)
    all_gather x1, waiting for transfers between devices, body(): joined = lax.all_gather(joined, 'wide', axis=0, tiled=True)  55 us
    pallas_call x1, Pallas kernels, attend(): pl.pallas_call(attention_kernel, grid_spec=grid_spec, out_shape=[jax.Shap...  35.1 us
    pallas_call x1, Pallas kernels, project(): pl.pallas_call(project_kernel, grid=(rows // PBLOCK,), in_specs=[part(wid...  19.4 us
    convert_element_type x1, other arithmetic, body(): hidden = (tokens.astype(jnp.float32) + projected).astype(jnp.bfloat16)  5.01 us
    dot_general x1, matrix products, body(): jnp.dot(normed, chosen, preferred_element_type=jnp.float32)  3.41 us
  transfers between devices with their start and end apart: 4, of which 2 were waited for; matrix products, arithmetic and copies ran while one was open for 14% of the time, Pallas kernels for 0%

profile of v6, /device:TPU:1, one launch (start us, length us, event | category | flops | bytes accessed | tf_op | source)
XLA Modules:
  0.0 165.7 jit_solution(5917595371256520467)
XLA Ops:
  7.2 0.0 copy-start.3
  7.2 0.0 copy-start.1
  7.2 0.0 copy-start.4
  7.2 0.0 copy-start.6
  7.2 0.0 all-gather.2.cloned.1.call-start
  7.3 1.2 reshape.200
  8.4 0.1 fusion.11
  8.6 0.1 reshape.202
  8.7 0.1 reshape.203
  8.8 1.5 pad_maximum_fusion.4
  10.2 0.0 all-gather.2.cloned.1.call-update
  10.3 0.9 select_reduce_fusion.1
  11.1 0.6 fusion.13
  14.3 2.2 %constant_dynamic-slice_fusion.7 = (bf16[2048,16]{1,0:T(8,128)(2,1)S(1)}, bf16[2048,16]{1,0:T(8,128)(2,1)S(1)}, bf16[2048,16]{1,0:T(8,128)(2,1)S(1)}, bf16[2048,16]{1,0:T(8,128)(2,1)S(1)}) fusion(bf16[2048,512]{1,0:T(8,128)(2,1)} %param.19, s32[]{:T(128)S(6)} %select_n.57, s32[]{:T(128)S(6)} %select_n.58, s32[]{:T(128)S(6)} %select_n.60, s32[]{:T(128)S(6)} %select_n.59), kind=kLoop, calls=%fused_computation.39 | loop fusion | bytes 524304 | tf_op jit(solution)/shard_map/dynamic_slice | solution.py:240
  16.5 1.5 pad_maximum_fusion.1
  18.0 1.4 collective-permute-start.1
  19.4 0.0 copy-done.1
  19.4 0.0 collective-permute-start
  19.4 0.0 copy-done.3
  19.4 0.6 fusion.12
  22.6 0.0 copy-done.4
  22.7 0.1 broadcast_in_dim.16
  22.7 0.1 broadcast_in_dim.17
  22.8 0.0 copy-done.6
  22.8 0.2 reduce-window.4
  23.0 0.9 constant_dynamic-slice_fusion.3
  23.9 0.2 reshape.206
  24.2 0.0 copy-start.5
  24.2 0.1 fusion.10
  24.3 0.1 copy.34
  24.4 0.1 copy.27
  24.5 0.1 copy.35
  24.7 0.1 copy.28
  24.8 0.1 convert_reduce_fusion
  24.9 0.1 select_reduce_fusion
  25.0 0.5 multiply_sine_fusion
  25.6 0.1 tile.8
  25.7 1.3 copy.30.cos_ref
  27.0 0.1 tile.20
  27.1 1.3 copy.31.sin_ref
  28.4 0.0 copy-done.5
  28.4 0.6 broadcast_in_dim.21
  29.0 1.0 copy.32.kst_ref
  30.0 0.7 pad_maximum_fusion.3.up_ref
  30.7 0.0 collective-permute-done
  30.7 1.9 %broadcast_select_fusion.1 = (bf16[1024,1024]{1,0:T(8,128)(2,1)S(1)}, bf16[1024,1024]{1,0:T(8,128)(2,1)S(1)}) fusion(bf16[1024,1024]{1,0:T(8,128)(2,1)S(1)} %copy-done.1, bf16[1024,1024]{1,0:T(8,128)(2,1)} %collective-permute-done, pred[]{:T(512)S(6)} %eq.53), kind=kLoop, calls=%fused_computation.8 | loop fusion | flops 2097152 | bytes 8388609 | tf_op jit(solution)/shard_map/jit(_where)/select_n | solution.py:229
  32.6 1.2 fusion
  33.8 1.4 fusion.2.x_ref
  35.2 0.0 copy-start
  35.2 0.0 collective-permute-done.1
  35.2 3.4 %fusion.3 = f32[1024,64]{0,1:T(8,128)S(1)} fusion(bf16[1024,2048]{1,0:T(8,128)(2,1)S(1)} %fusion.2.x_ref, bf16[2048,64]{1,0:T(8,128)(2,1)} %pad_maximum_fusion.1, bf16[2048,64]{1,0:T(8,128)(2,1)} %collective-permute-done.1, pred[64]{0:T(512)(128)(4,1)S(1)} %broadcast_in_dim.17), kind=kOutput, calls=%fused_computation.10 | convolution fusion | flops 268566528 | bytes 4980800 | tf_op jit(solution)/shard_map/dot_general | solution.py:255
  38.6 0.0 copy-done
  38.7 0.8 copy.29.sp_ref
  39.6 55.0 %all-gather.2.cloned.1.call-done.w_ref = bf16[2048,2112]{1,0:T(8,128)(2,1)} async-done(((bf16[32,2112]{1,0:T(8,128)(2,1)}), bf16[2048,2112]{1,0:T(8,128)(2,1)}) %all-gather.2.cloned.1.call-update) | async-done | bytes 8650768 | tf_op jit(solution)/shard_map/all_gather | solution.py:225
  94.6 19.4 %shard_map.131 = (bf16[1024,1024]{1,0:T(8,128)(2,1)}, bf16[1024,256]{1,0:T(8,128)(2,1)}, bf16[1024,256]{1,0:T(8,128)(2,1)}, bf16[1024,576]{1,0:T(8,128)(2,1)}, bf16[1024,2048]{1,0:T(8,128)(2,1)}) custom-call(bf16[1024,2048]{1,0:T(8,128)(2,1)} %copy-done, bf16[2048,2112]{1,0:T(8,128)(2,1)} %all-gather.2.cloned.1.call-done.w_ref, ...), custom_call_target="tpu_custom_call" | custom-call | tf_op jit(solution)/shard_map/pallas_call | solution.py:97
  113.9 0.0 copy-start.2
  114.0 35.1 %shard_map.132 = (bf16[1024,1024]{1,0:T(8,128)(2,1)}, bf16[1024,1024]{1,0:T(8,128)(2,1)}) custom-call(s32[1]{0:T(128)} %bitcast.me_ref, bf16[1024,1024]{1,0:T(8,128)(2,1)} %get-tuple-element.9.q_nope_ref, bf16[1024,256]{1,0:T(8,128)(2,1)} %get-tuple-element.10.qf_ref, bf16[1024,256]{1,0:T(8,128)(2,1)} %get-tuple-element.11.qs_ref, ...), custom_call_target="tpu_custom_call" | custom-call | tf_op jit(solution)/shard_map/pallas_call | solution.py:175
  149.1 0.7 collective-permute-start.2
  149.7 0.0 copy-done.2
  149.7 1.4 copy.33
  151.2 2.7 %collective-permute-done.2 = bf16[1024,1024]{1,0:T(8,128)(2,1)} collective-permute-done((bf16[1024,1024]{1,0:T(8,128)(2,1)}, bf16[1024,1024]{1,0:T(8,128)(2,1)}, u32[]{:S(2)}, u32[]{:S(2)}) %collective-permute-start.2) | collective-permute-done | bytes 2097184 | tf_op jit(solution)/shard_map/ppermute | solution.py:199
  153.9 5.0 %add_convert_fusion = bf16[1024,1024]{1,0:T(8,128)(2,1)} fusion(bf16[1024,1024]{1,0:T(8,128)(2,1)} %collective-permute-done.2, bf16[1024,1024]{1,0:T(8,128)(2,1)} %get-tuple-element.14, bf16[1024,1024]{1,0:T(8,128)(2,1)S(1)} %copy-done.1), kind=kLoop, calls=%fused_computation.6 | loop fusion | flops 6291456 | bytes 8388608 | tf_op jit(solution)/shard_map/convert_element_type | solution.py:282
  (15 shorter events, 0.2 us)
Async XLA Ops:
  7.2 12.2 %copy-start.3 = (s32[1,4]{1,0:T(1,128)S(1)}, s32[1,4]{1,0:T(1,128)}, u32[]{:S(2)}) copy-start(s32[1,4]{1,0:T(1,128)} %param.22) | copy-start | bytes 52
  7.2 12.2 %copy-start.1 = (bf16[1024,1024]{1,0:T(8,128)(2,1)S(1)}, bf16[1024,1024]{1,0:T(8,128)(2,1)}, u32[]{:S(2)}) copy-start(bf16[1024,1024]{1,0:T(8,128)(2,1)} %param.12) | copy-start | bytes 6291460
  7.2 15.4 %copy-start.4 = (bf16[2048]{0:T(1024)(128)(2,1)S(1)}, bf16[2048]{0:T(1024)(128)(2,1)}, u32[]{:S(2)}) copy-start(bf16[2048]{0:T(1024)(128)(2,1)} %param.13) | copy-start | bytes 12292
  7.2 15.6 %copy-start.6 = (s32[1,4]{1,0:T(1,128)S(1)}, s32[1,4]{1,0:T(1,128)}, u32[]{:S(2)}) copy-start(s32[1,4]{1,0:T(1,128)} %param.21) | copy-start | bytes 52
  7.2 87.4 %all-gather.2.cloned.1.call-start = ((), (), s32[]{:S(2)}) async-start(), calls=%async_computation | async-start | bytes 9052160 | tf_op jit(solution)/shard_map/all_gather | solution.py:225
  18.0 17.3 %collective-permute-start.1 = (bf16[2048,64]{1,0:T(8,128)(2,1)}, bf16[2048,64]{1,0:T(8,128)(2,1)}, u32[]{:S(2)}, u32[]{:S(2)}) collective-permute-start(bf16[2048,64]{1,0:T(8,128)(2,1)} %pad_maximum_fusion.1), channel_id=1, source_target_pairs={{0,1},{1,0},{2,3},{3,2},{4,5},{5,4},{6,7},{7,6},{8,9},{9,8},{10,11... | collective-permute-start | bytes 786440 | tf_op jit(solution)/shard_map/ppermute | solution.py:199
  19.4 11.3 %collective-permute-start = (bf16[1024,1024]{1,0:T(8,128)(2,1)S(1)}, bf16[1024,1024]{1,0:T(8,128)(2,1)}, u32[]{:S(2)}, u32[]{:S(2)}) collective-permute-start(bf16[1024,1024]{1,0:T(8,128)(2,1)S(1)} %copy-done.1), channel_id=1, source_target_pairs={{0,1},{1,0},{2,3},{3,2},{4,5},{5,4},{6,7},{7,6},{8,9},{9,8},{10,11... | collective-permute-start | bytes 6291464 | tf_op jit(solution)/shard_map/ppermute | solution.py:199
  24.2 4.3 %copy-start.5 = (bf16[512]{0:T(512)(128)(2,1)S(1)}, bf16[512]{0:T(512)(128)(2,1)}, u32[]{:S(2)}) copy-start(bf16[512]{0:T(512)(128)(2,1)} %param.16) | copy-start | bytes 3076
  35.2 3.4 %copy-start = (bf16[1024,2048]{1,0:T(8,128)(2,1)}, bf16[1024,2048]{1,0:T(8,128)(2,1)S(1)}, u32[]{:S(2)}) copy-start(bf16[1024,2048]{1,0:T(8,128)(2,1)S(1)} %fusion.2.x_ref) | copy-start | bytes 12582916
  113.9 35.8 %copy-start.2 = (bf16[1024,576]{1,0:T(8,128)(2,1)S(1)}, bf16[1024,576]{1,0:T(8,128)(2,1)}, u32[]{:S(2)}) copy-start(bf16[1024,576]{1,0:T(8,128)(2,1)} %get-tuple-element.21.cache_ref) | copy-start | bytes 3538948
  149.1 4.8 %collective-permute-start.2 = (bf16[1024,1024]{1,0:T(8,128)(2,1)}, bf16[1024,1024]{1,0:T(8,128)(2,1)}, u32[]{:S(2)}, u32[]{:S(2)}) collective-permute-start(bf16[1024,1024]{1,0:T(8,128)(2,1)} %get-tuple-element.15), channel_id=1, source_target_pairs={{0,1},{1,0},{2,3},{3,2},{4,5},{5,4},{6,7},{7,6},{8,9},{9,8},{10,11... | collective-permute-start | bytes 6291464 | tf_op jit(solution)/shard_map/ppermute | solution.py:199
Sparse Core Ops, SparseCore 0:
  10.8 83.7 all-gather.1

commit v7 on v6

--- a/solution.py
+++ b/solution.py
@@ -112,37 +112,57 @@
     )(normed, joined, spread, up_rows, cosine, sine, kv_gain.astype(jnp.float32)[None, :], kvb_weight)
 
 
-def attention_kernel(me_ref, q_nope_ref, qf_ref, qs_ref, kv_ref, cache_ref, kst_ref, wt_ref, wm_ref,
-                     theirs_ref, mine_ref, att_ref):
+def attention_kernel(me_ref, first_ref, q_nope_ref, qf_ref, qs_ref, kv_ref, cache_ref, kst_ref, wt_ref,
+                     wm_ref, theirs_ref, mine_ref, att_ref):
     i = pl.program_id(0)
     heads = qf_ref.shape[1] * 2 // ROPE
     half = ROPE // 2
     scale = 1.0 / jnp.sqrt(jnp.float32(NOPE + ROPE))
-    start = pl.multiple_of(jnp.maximum(i * QBLOCK - LMAX, 0), 128)
-    row = i * QBLOCK + lax.broadcasted_iota(jnp.int32, (QBLOCK, WINDOW), 0)
-    col = start + lax.broadcasted_iota(jnp.int32, (QBLOCK, WINDOW), 1)
-    allowed = (col >= kst_ref[...]) & (col <= row)
-    kr = cache_ref[pl.ds(start, WINDOW), LATENT:LATENT + ROPE]
-    kf = kr[:, :half]
-    ks = kr[:, half:]
     qf_all = qf_ref[...]
     qs_all = qs_ref[...]
-    for h in range(heads):
-        qn = q_nope_ref[:, h * NOPE:(h + 1) * NOPE]
-        qf = qf_all[:, h * half:(h + 1) * half]
-        qs = qs_all[:, h * half:(h + 1) * half]
-        kn = kv_ref[pl.ds(start, WINDOW), h * (NOPE + VDIM):h * (NOPE + VDIM) + NOPE]
-        s = lax.dot_general(qn, kn, (((1,), (1,)), ((), ())), preferred_element_type=jnp.float32)
-        rope = lax.dot_general(qf, kf, (((1,), (1,)), ((), ())), preferred_element_type=jnp.float32)
-        rope = rope + lax.dot_general(qs, ks, (((1,), (1,)), ((), ())), preferred_element_type=jnp.float32)
-        s = jnp.where(allowed, (s + rope) * scale, jnp.float32(-1e30))
-        top = jnp.max(s, axis=1, keepdims=True)
-        e = jnp.exp(s - top)
-        w = (e * (1.0 / jnp.sum(e, axis=1, keepdims=True))).astype(jnp.bfloat16)
-        v = kv_ref[pl.ds(start, WINDOW), h * (NOPE + VDIM) + NOPE:(h + 1) * (NOPE + VDIM)]
-        att_ref[:, h * VDIM:(h + 1) * VDIM] = jnp.dot(
-            w, v, preferred_element_type=jnp.float32
-        ).astype(att_ref.dtype)
+    kst = kst_ref[...]
+
+    def run(start, width):
+        start = pl.multiple_of(start, 128)
+        row = i * QBLOCK + lax.broadcasted_iota(jnp.int32, (QBLOCK, width), 0)
+        col = start + lax.broadcasted_iota(jnp.int32, (QBLOCK, width), 1)
+        allowed = (col >= kst) & (col <= row)
+        kr = cache_ref[pl.ds(start, width), LATENT:LATENT + ROPE]
+        kf = kr[:, :half]
+        ks = kr[:, half:]
+        for h in range(heads):
+            qn = q_nope_ref[:, h * NOPE:(h + 1) * NOPE]
+            qf = qf_all[:, h * half:(h + 1) * half]
+            qs = qs_all[:, h * half:(h + 1) * half]
+            kn = kv_ref[pl.ds(start, width), h * (NOPE + VDIM):h * (NOPE + VDIM) + NOPE]
+            s = lax.dot_general(qn, kn, (((1,), (1,)), ((), ())), preferred_element_type=jnp.float32)
+            rope = lax.dot_general(qf, kf, (((1,), (1,)), ((), ())), preferred_element_type=jnp.float32)
+            rope = rope + lax.dot_general(qs, ks, (((1,), (1,)), ((), ())), preferred_element_type=jnp.float32)
+            s = jnp.where(allowed, (s + rope) * scale, jnp.float32(-1e30))
+            top = jnp.max(s, axis=1, keepdims=True)
+            e = jnp.exp(s - top)
+            w = (e * (1.0 / jnp.sum(e, axis=1, keepdims=True))).astype(jnp.bfloat16)
+            v = kv_ref[pl.ds(start, width), h * (NOPE + VDIM) + NOPE:(h + 1) * (NOPE + VDIM)]
+            att_ref[:, h * VDIM:(h + 1) * VDIM] = jnp.dot(
+                w, v, preferred_element_type=jnp.float32
+            ).astype(att_ref.dtype)
+
+    first = first_ref[i]
+    one = first >= i * QBLOCK
+    two = jnp.logical_and(jnp.logical_not(one), first >= i * QBLOCK - QBLOCK)
+
+    @pl.when(one)
+    def _():
+        run(i * QBLOCK, QBLOCK)
+
+    @pl.when(two)
+    def _():
+        run(jnp.maximum(i * QBLOCK - QBLOCK, 0), 2 * QBLOCK)
+
+    @pl.when(jnp.logical_not(jnp.logical_or(one, two)))
+    def _():
+        run(jnp.maximum(i * QBLOCK - LMAX, 0), WINDOW)
+
     att = att_ref[...]
     theirs_ref[...] = jnp.dot(att, wt_ref[...], preferred_element_type=jnp.float32).astype(theirs_ref.dtype)
     mine_ref[...] = jnp.dot(att, wm_ref[...], preferred_element_type=jnp.float32).astype(mine_ref.dtype)
@@ -154,21 +174,21 @@
     half = q_first.shape[1]
     out_half = o_weight.shape[1] // 2
     grid_spec = pltpu.PrefetchScalarGridSpec(
-        num_scalar_prefetch=1,
+        num_scalar_prefetch=2,
         grid=(rows // QBLOCK,),
         in_specs=[
-            pl.BlockSpec((QBLOCK, heads * NOPE), lambda i, m: (i, 0)),
-            pl.BlockSpec((QBLOCK, half), lambda i, m: (i, 0)),
-            pl.BlockSpec((QBLOCK, half), lambda i, m: (i, 0)),
-            pl.BlockSpec((rows, heads * (NOPE + VDIM)), lambda i, m: (0, 0)),
-            pl.BlockSpec((rows, LATENT + ROPE), lambda i, m: (0, 0)),
-            pl.BlockSpec((QBLOCK, 1), lambda i, m: (i, 0)),
-            pl.BlockSpec((heads * VDIM, out_half), lambda i, m: (0, 1 - m[0])),
-            pl.BlockSpec((heads * VDIM, out_half), lambda i, m: (0, m[0])),
+            pl.BlockSpec((QBLOCK, heads * NOPE), lambda i, m, f: (i, 0)),
+            pl.BlockSpec((QBLOCK, half), lambda i, m, f: (i, 0)),
+            pl.BlockSpec((QBLOCK, half), lambda i, m, f: (i, 0)),
+            pl.BlockSpec((rows, heads * (NOPE + VDIM)), lambda i, m, f: (0, 0)),
+            pl.BlockSpec((rows, LATENT + ROPE), lambda i, m, f: (0, 0)),
+            pl.BlockSpec((QBLOCK, 1), lambda i, m, f: (i, 0)),
+            pl.BlockSpec((heads * VDIM, out_half), lambda i, m, f: (0, 1 - m[0])),
+            pl.BlockSpec((heads * VDIM, out_half), lambda i, m, f: (0, m[0])),
         ],
         out_specs=[
-            pl.BlockSpec((QBLOCK, out_half), lambda i, m: (i, 0)),
-            pl.BlockSpec((QBLOCK, out_half), lambda i, m: (i, 0)),
+            pl.BlockSpec((QBLOCK, out_half), lambda i, m, f: (i, 0)),
+            pl.BlockSpec((QBLOCK, out_half), lambda i, m, f: (i, 0)),
         ],
         scratch_shapes=[pltpu.VMEM((QBLOCK, heads * VDIM), jnp.bfloat16)],
     )
@@ -179,7 +199,7 @@
             jax.ShapeDtypeStruct((rows, out_half), jnp.bfloat16),
             jax.ShapeDtypeStruct((rows, out_half), jnp.bfloat16),
         ],
-    )(me, q_nope, q_first, q_second, kv, latent_cache, key_start[:, None], o_weight, o_weight)
+    )(me, key_start[::QBLOCK], q_nope, q_first, q_second, kv, latent_cache, key_start[:, None], o_weight, o_weight)
 
 
 def split_heads(weight, heads):

time: 166 us -> 162 us (0.976)
  Pallas kernels: 54.5 us -> 50.9 us
    pallas_call x1, Pallas kernels: 35.1 us -> 31.5 us  [attend(): pl.pallas_call(attention_kernel, grid_spec=grid_spec, out_shape=[jax.Shap...]
  transfers between devices with their start and end apart: 4 -> 4, of which waited for: 2 -> 2; matrix products, arithmetic and copies ran while one was open for 14% -> 15% of each run, Pallas kernels for 0% -> 0%
where the time goes in v7:
time: 162 us
  waiting for transfers between devices  57.3 us (35%)
  Pallas kernels  50.9 us (31%)
  between operations  19.4 us (12%)
  other arithmetic  15.3 us (9%)
  local copies, waits for them, and re-layouts  13.7 us (8%)
  matrix products  3.41 us (2%)
  starting transfers between devices  2.14 us (1%)
    all_gather x1, waiting for transfers between devices, body(): joined = lax.all_gather(joined, 'wide', axis=0, tiled=True)  54.5 us
    pallas_call x1, Pallas kernels, attend(): pl.pallas_call(attention_kernel, grid_spec=grid_spec, out_shape=[jax.Shap...  31.5 us
    pallas_call x1, Pallas kernels, project(): pl.pallas_call(project_kernel, grid=(rows // PBLOCK,), in_specs=[part(wid...  19.4 us
    convert_element_type x1, other arithmetic, body(): hidden = (tokens.astype(jnp.float32) + projected).astype(jnp.bfloat16)  5.01 us
    dot_general x1, matrix products, body(): jnp.dot(normed, chosen, preferred_element_type=jnp.float32)  3.41 us
  transfers between devices with their start and end apart: 4, of which 2 were waited for; matrix products, arithmetic and copies ran while one was open for 15% of the time, Pallas kernels for 0%

profile of v7, /device:TPU:1, one launch (start us, length us, event | category | flops | bytes accessed | tf_op | source)
XLA Modules:
  0.0 162.1 jit_solution(1843753606723515790)
XLA Ops:
  7.2 0.0 copy-start.3
  7.2 0.0 copy-start.1
  7.2 0.0 copy-start.4
  7.2 0.0 copy-start.6
  7.2 0.0 all-gather.2.cloned.1.call-start
  7.3 1.2 reshape.201
  8.4 0.1 fusion.11
  8.6 0.1 reshape.203
  8.7 0.1 reshape.204
  8.8 1.5 pad_maximum_fusion.4
  10.2 0.0 all-gather.2.cloned.1.call-update
  10.3 0.9 select_reduce_fusion.1
  11.1 0.6 fusion.13
  14.3 2.2 %constant_dynamic-slice_fusion.6 = (bf16[2048,16]{1,0:T(8,128)(2,1)S(1)}, bf16[2048,16]{1,0:T(8,128)(2,1)S(1)}, bf16[2048,16]{1,0:T(8,128)(2,1)S(1)}, bf16[2048,16]{1,0:T(8,128)(2,1)S(1)}) fusion(bf16[2048,512]{1,0:T(8,128)(2,1)} %param.19, s32[]{:T(128)S(6)} %select_n.57, s32[]{:T(128)S(6)} %select_n.58, s32[]{:T(128)S(6)} %select_n.60, s32[]{:T(128)S(6)} %select_n.59), kind=kLoop, calls=%fused_computation.38 | loop fusion | bytes 524304 | tf_op jit(solution)/shard_map/dynamic_slice | solution.py:260
  16.5 1.5 pad_maximum_fusion.1
  18.0 1.4 collective-permute-start.1
  19.4 0.0 copy-done.1
  19.4 0.0 collective-permute-start
  19.4 0.0 copy-done.3
  19.4 0.6 fusion.12
  22.6 0.0 copy-done.4
  22.7 0.1 broadcast_in_dim.16
  22.7 0.1 broadcast_in_dim.17
  22.8 0.0 copy-done.6
  22.8 0.2 reduce-window.4
  23.0 0.9 constant_dynamic-slice_fusion.2
  23.9 0.2 reshape.206
  24.1 0.0 copy-start.5
  24.2 0.1 fusion.10
  24.3 0.1 copy.34
  24.4 0.1 copy.27
  24.5 0.1 copy.35
  24.7 0.1 copy.28
  24.8 0.1 convert_reduce_fusion
  24.9 0.1 select_reduce_fusion
  25.0 0.7 slice.49.first_ref
  25.7 0.5 multiply_sine_fusion
  26.2 0.1 tile.8
  26.3 1.3 copy.30.cos_ref
  27.6 0.1 tile.20
  27.8 1.3 copy.31.sin_ref
  29.1 0.0 copy-done.5
  29.1 0.6 broadcast_in_dim.21
  29.7 1.0 copy.32.kst_ref
  30.7 0.7 pad_maximum_fusion.3.up_ref
  31.4 0.0 collective-permute-done
  31.4 1.9 %broadcast_select_fusion.1 = (bf16[1024,1024]{1,0:T(8,128)(2,1)S(1)}, bf16[1024,1024]{1,0:T(8,128)(2,1)S(1)}) fusion(bf16[1024,1024]{1,0:T(8,128)(2,1)S(1)} %copy-done.1, bf16[1024,1024]{1,0:T(8,128)(2,1)} %collective-permute-done, pred[]{:T(512)S(6)} %eq.56), kind=kLoop, calls=%fused_computation.8 | loop fusion | flops 2097152 | bytes 8388609 | tf_op jit(solution)/shard_map/jit(_where)/select_n | solution.py:249
  33.3 1.0 fusion
  34.3 1.4 fusion.2.x_ref
  35.7 0.0 copy-start
  35.7 0.0 collective-permute-done.1
  35.7 3.4 %fusion.3 = f32[1024,64]{0,1:T(8,128)S(1)} fusion(bf16[1024,2048]{1,0:T(8,128)(2,1)S(1)} %fusion.2.x_ref, bf16[2048,64]{1,0:T(8,128)(2,1)} %pad_maximum_fusion.1, bf16[2048,64]{1,0:T(8,128)(2,1)} %collective-permute-done.1, pred[64]{0:T(512)(128)(4,1)S(1)} %broadcast_in_dim.17), kind=kOutput, calls=%fused_computation.10 | convolution fusion | flops 268566528 | bytes 4980800 | tf_op jit(solution)/shard_map/dot_general | solution.py:275
  39.1 0.0 copy-done
  39.2 0.8 copy.29.sp_ref
  40.0 54.5 %all-gather.2.cloned.1.call-done.w_ref = bf16[2048,2112]{1,0:T(8,128)(2,1)} async-done(((bf16[32,2112]{1,0:T(8,128)(2,1)}), bf16[2048,2112]{1,0:T(8,128)(2,1)}) %all-gather.2.cloned.1.call-update) | async-done | bytes 8650768 | tf_op jit(solution)/shard_map/all_gather | solution.py:245
  94.6 19.4 %shard_map.131 = (bf16[1024,1024]{1,0:T(8,128)(2,1)}, bf16[1024,256]{1,0:T(8,128)(2,1)}, bf16[1024,256]{1,0:T(8,128)(2,1)}, bf16[1024,576]{1,0:T(8,128)(2,1)}, bf16[1024,2048]{1,0:T(8,128)(2,1)}) custom-call(bf16[1024,2048]{1,0:T(8,128)(2,1)} %copy-done, bf16[2048,2112]{1,0:T(8,128)(2,1)} %all-gather.2.cloned.1.call-done.w_ref, ...), custom_call_target="tpu_custom_call" | custom-call | tf_op jit(solution)/shard_map/pallas_call | solution.py:97
  113.9 0.0 copy-start.2
  113.9 31.5 %shard_map.132 = (bf16[1024,1024]{1,0:T(8,128)(2,1)}, bf16[1024,1024]{1,0:T(8,128)(2,1)}) custom-call(s32[1]{0:T(128)} %bitcast.me_ref, s32[4]{0:T(128)} %slice.49.first_ref, bf16[1024,1024]{1,0:T(8,128)(2,1)} %get-tuple-element.9.q_nope_ref, bf16[1024,256]{1,0:T(8,128)(2,1)} %get-tuple-element.10.qf_ref, bf16[1024,256]{1,0:T(8,128)(2,1)} %get-tuple-element.11.qs_ref, ...), custom_call_target="tpu_custom_call" | custom-call | tf_op jit(solution)/shard_map/pallas_call | solution.py:195
  145.4 0.7 collective-permute-start.2
  146.1 0.0 copy-done.2
  146.1 1.4 copy.33
  147.5 2.7 %collective-permute-done.2 = bf16[1024,1024]{1,0:T(8,128)(2,1)} collective-permute-done((bf16[1024,1024]{1,0:T(8,128)(2,1)}, bf16[1024,1024]{1,0:T(8,128)(2,1)}, u32[]{:S(2)}, u32[]{:S(2)}) %collective-permute-start.2) | collective-permute-done | bytes 2097184 | tf_op jit(solution)/shard_map/ppermute | solution.py:219
  150.3 5.0 %add_convert_fusion = bf16[1024,1024]{1,0:T(8,128)(2,1)} fusion(bf16[1024,1024]{1,0:T(8,128)(2,1)} %collective-permute-done.2, bf16[1024,1024]{1,0:T(8,128)(2,1)} %get-tuple-element.14, bf16[1024,1024]{1,0:T(8,128)(2,1)S(1)} %copy-done.1), kind=kLoop, calls=%fused_computation.6 | loop fusion | flops 6291456 | bytes 8388608 | tf_op jit(solution)/shard_map/convert_element_type | solution.py:302
  (15 shorter events, 0.2 us)
Async XLA Ops:
  7.2 12.2 %copy-start.3 = (s32[1,4]{1,0:T(1,128)S(1)}, s32[1,4]{1,0:T(1,128)}, u32[]{:S(2)}) copy-start(s32[1,4]{1,0:T(1,128)} %param.22) | copy-start | bytes 52
  7.2 12.2 %copy-start.1 = (bf16[1024,1024]{1,0:T(8,128)(2,1)S(1)}, bf16[1024,1024]{1,0:T(8,128)(2,1)}, u32[]{:S(2)}) copy-start(bf16[1024,1024]{1,0:T(8,128)(2,1)} %param.12) | copy-start | bytes 6291460
  7.2 15.4 %copy-start.4 = (bf16[2048]{0:T(1024)(128)(2,1)S(1)}, bf16[2048]{0:T(1024)(128)(2,1)}, u32[]{:S(2)}) copy-start(bf16[2048]{0:T(1024)(128)(2,1)} %param.13) | copy-start | bytes 12292
  7.2 15.6 %copy-start.6 = (s32[1,4]{1,0:T(1,128)S(1)}, s32[1,4]{1,0:T(1,128)}, u32[]{:S(2)}) copy-start(s32[1,4]{1,0:T(1,128)} %param.21) | copy-start | bytes 52
  7.2 87.4 %all-gather.2.cloned.1.call-start = ((), (), s32[]{:S(2)}) async-start(), calls=%async_computation | async-start | bytes 9052160 | tf_op jit(solution)/shard_map/all_gather | solution.py:245
  18.0 17.7 %collective-permute-start.1 = (bf16[2048,64]{1,0:T(8,128)(2,1)}, bf16[2048,64]{1,0:T(8,128)(2,1)}, u32[]{:S(2)}, u32[]{:S(2)}) collective-permute-start(bf16[2048,64]{1,0:T(8,128)(2,1)} %pad_maximum_fusion.1), channel_id=1, source_target_pairs={{0,1},{1,0},{2,3},{3,2},{4,5},{5,4},{6,7},{7,6},{8,9},{9,8},{10,11... | collective-permute-start | bytes 786440 | tf_op jit(solution)/shard_map/ppermute | solution.py:219
  19.4 12.0 %collective-permute-start = (bf16[1024,1024]{1,0:T(8,128)(2,1)S(1)}, bf16[1024,1024]{1,0:T(8,128)(2,1)}, u32[]{:S(2)}, u32[]{:S(2)}) collective-permute-start(bf16[1024,1024]{1,0:T(8,128)(2,1)S(1)} %copy-done.1), channel_id=1, source_target_pairs={{0,1},{1,0},{2,3},{3,2},{4,5},{5,4},{6,7},{7,6},{8,9},{9,8},{10,11... | collective-permute-start | bytes 6291464 | tf_op jit(solution)/shard_map/ppermute | solution.py:219
  24.1 4.9 %copy-start.5 = (bf16[512]{0:T(512)(128)(2,1)S(1)}, bf16[512]{0:T(512)(128)(2,1)}, u32[]{:S(2)}) copy-start(bf16[512]{0:T(512)(128)(2,1)} %param.16) | copy-start | bytes 3076
  35.7 3.4 %copy-start = (bf16[1024,2048]{1,0:T(8,128)(2,1)}, bf16[1024,2048]{1,0:T(8,128)(2,1)S(1)}, u32[]{:S(2)}) copy-start(bf16[1024,2048]{1,0:T(8,128)(2,1)S(1)} %fusion.2.x_ref) | copy-start | bytes 12582916
  113.9 32.2 %copy-start.2 = (bf16[1024,576]{1,0:T(8,128)(2,1)S(1)}, bf16[1024,576]{1,0:T(8,128)(2,1)}, u32[]{:S(2)}) copy-start(bf16[1024,576]{1,0:T(8,128)(2,1)} %get-tuple-element.21.cache_ref) | copy-start | bytes 3538948
  145.4 4.8 %collective-permute-start.2 = (bf16[1024,1024]{1,0:T(8,128)(2,1)}, bf16[1024,1024]{1,0:T(8,128)(2,1)}, u32[]{:S(2)}, u32[]{:S(2)}) collective-permute-start(bf16[1024,1024]{1,0:T(8,128)(2,1)} %get-tuple-element.15), channel_id=1, source_target_pairs={{0,1},{1,0},{2,3},{3,2},{4,5},{5,4},{6,7},{7,6},{8,9},{9,8},{10,11... | collective-permute-start | bytes 6291464 | tf_op jit(solution)/shard_map/ppermute | solution.py:219
Sparse Core Ops, SparseCore 0:
  10.8 83.6 all-gather.1

commit v8 on v7

--- a/solution.py
+++ b/solution.py
@@ -55,11 +55,12 @@
 
 
 def project_kernel(x_ref, w_ref, sp_ref, up_ref, cos_ref, sin_ref, gain_ref, kvb_ref,
-                   qn_ref, qf_ref, qs_ref, cache_ref, kv_ref):
+                   qn_ref, qr_ref, cache_ref, kv_ref):
     x = x_ref[...]
     sp = sp_ref[...]
     nope = qn_ref.shape[1]
-    half = qf_ref.shape[1]
+    heads = qr_ref.shape[0]
+    half = heads * ROPE // 2
 
     def query_part(lo, hi):
         base = jnp.dot(x, w_ref[:, lo:hi], preferred_element_type=jnp.float32)
@@ -70,8 +71,12 @@
     second = query_part(nope + half, nope + 2 * half)
     cosine = cos_ref[...]
     sine = sin_ref[...]
-    qf_ref[...] = (first * cosine - second * sine).astype(qf_ref.dtype)
-    qs_ref[...] = (first * sine + second * cosine).astype(qs_ref.dtype)
+    turned_first = (first * cosine - second * sine).astype(qr_ref.dtype)
+    turned_second = (first * sine + second * cosine).astype(qr_ref.dtype)
+    width = ROPE // 2
+    for h in range(heads):
+        qr_ref[h, :, :width] = turned_first[:, h * width:(h + 1) * width]
+        qr_ref[h, :, width:] = turned_second[:, h * width:(h + 1) * width]
     q_end = nope + 2 * half
     pre = jnp.dot(x, w_ref[:, q_end:q_end + LATENT], preferred_element_type=jnp.float32)
     mean_sq = jnp.mean(pre * pre, axis=-1, keepdims=True)
@@ -101,25 +106,26 @@
             part(width), full((width, cols)), part(spread.shape[1]), full(up_rows.shape),
             part(half), part(half), full((1, LATENT)), full(kvb_weight.shape),
         ],
-        out_specs=[part(nope), part(half), part(half), part(LATENT + ROPE), part(kvb_weight.shape[1])],
+        out_specs=[
+            part(nope),
+            pl.BlockSpec((heads, PBLOCK, ROPE), lambda i: (0, i, 0)),
+            part(LATENT + ROPE),
+            part(kvb_weight.shape[1]),
+        ],
         out_shape=[
             jax.ShapeDtypeStruct((rows, nope), jnp.bfloat16),
-            jax.ShapeDtypeStruct((rows, half), jnp.bfloat16),
-            jax.ShapeDtypeStruct((rows, half), jnp.bfloat16),
+            jax.ShapeDtypeStruct((heads, rows, ROPE), jnp.bfloat16),
             jax.ShapeDtypeStruct((rows, LATENT + ROPE), jnp.bfloat16),
             jax.ShapeDtypeStruct((rows, kvb_weight.shape[1]), jnp.bfloat16),
         ],
     )(normed, joined, spread, up_rows, cosine, sine, kv_gain.astype(jnp.float32)[None, :], kvb_weight)
 
 
-def attention_kernel(me_ref, first_ref, q_nope_ref, qf_ref, qs_ref, kv_ref, cache_ref, kst_ref, wt_ref,
+def attention_kernel(me_ref, first_ref, q_nope_ref, qr_ref, kv_ref, cache_ref, kst_ref, wt_ref,
                      wm_ref, theirs_ref, mine_ref, att_ref):
     i = pl.program_id(0)
-    heads = qf_ref.shape[1] * 2 // ROPE
-    half = ROPE // 2
+    heads = qr_ref.shape[0]
     scale = 1.0 / jnp.sqrt(jnp.float32(NOPE + ROPE))
-    qf_all = qf_ref[...]
-    qs_all = qs_ref[...]
     kst = kst_ref[...]
 
     def run(start, width):
@@ -128,16 +134,12 @@
         col = start + lax.broadcasted_iota(jnp.int32, (QBLOCK, width), 1)
         allowed = (col >= kst) & (col <= row)
         kr = cache_ref[pl.ds(start, width), LATENT:LATENT + ROPE]
-        kf = kr[:, :half]
-        ks = kr[:, half:]
         for h in range(heads):
             qn = q_nope_ref[:, h * NOPE:(h + 1) * NOPE]
-            qf = qf_all[:, h * half:(h + 1) * half]
-            qs = qs_all[:, h * half:(h + 1) * half]
+            qr = qr_ref[h]
             kn = kv_ref[pl.ds(start, width), h * (NOPE + VDIM):h * (NOPE + VDIM) + NOPE]
             s = lax.dot_general(qn, kn, (((1,), (1,)), ((), ())), preferred_element_type=jnp.float32)
-            rope = lax.dot_general(qf, kf, (((1,), (1,)), ((), ())), preferred_element_type=jnp.float32)
-            rope = rope + lax.dot_general(qs, ks, (((1,), (1,)), ((), ())), preferred_element_type=jnp.float32)
+            rope = lax.dot_general(qr, kr, (((1,), (1,)), ((), ())), preferred_element_type=jnp.float32)
             s = jnp.where(allowed, (s + rope) * scale, jnp.float32(-1e30))
             top = jnp.max(s, axis=1, keepdims=True)
             e = jnp.exp(s - top)
@@ -168,18 +170,16 @@
     mine_ref[...] = jnp.dot(att, wm_ref[...], preferred_element_type=jnp.float32).astype(mine_ref.dtype)
 
 
-def attend(me, q_nope, q_first, q_second, kv, latent_cache, key_start, o_weight):
+def attend(me, q_nope, q_rope, kv, latent_cache, key_start, o_weight):
     rows = q_nope.shape[0]
     heads = q_nope.shape[1] // NOPE
-    half = q_first.shape[1]
     out_half = o_weight.shape[1] // 2
     grid_spec = pltpu.PrefetchScalarGridSpec(
         num_scalar_prefetch=2,
         grid=(rows // QBLOCK,),
         in_specs=[
             pl.BlockSpec((QBLOCK, heads * NOPE), lambda i, m, f: (i, 0)),
-            pl.BlockSpec((QBLOCK, half), lambda i, m, f: (i, 0)),
-            pl.BlockSpec((QBLOCK, half), lambda i, m, f: (i, 0)),
+            pl.BlockSpec((heads, QBLOCK, ROPE), lambda i, m, f: (0, i, 0)),
             pl.BlockSpec((rows, heads * (NOPE + VDIM)), lambda i, m, f: (0, 0)),
             pl.BlockSpec((rows, LATENT + ROPE), lambda i, m, f: (0, 0)),
             pl.BlockSpec((QBLOCK, 1), lambda i, m, f: (i, 0)),
@@ -199,7 +199,7 @@
             jax.ShapeDtypeStruct((rows, out_half), jnp.bfloat16),
             jax.ShapeDtypeStruct((rows, out_half), jnp.bfloat16),
         ],
-    )(me, key_start[::QBLOCK], q_nope, q_first, q_second, kv, latent_cache, key_start[:, None], o_weight, o_weight)
+    )(me, key_start[::QBLOCK], q_nope, q_rope, kv, latent_cache, key_start[:, None], o_weight, o_weight)
 
 
 def split_heads(weight, heads):
@@ -289,12 +289,12 @@
     angle = position.astype(jnp.float32)[:, None] * freqs[None, :]
     cosine = jnp.tile(jnp.cos(angle), (1, heads_here))
     sine = jnp.tile(jnp.sin(angle), (1, heads_here))
-    q_nope, q_first, q_second, latent_cache, expanded = project(
+    q_nope, q_rope, latent_cache, expanded = project(
         normed, joined, spread_rows, up_weight_rows, cosine, sine, kv_gain, kvb_weight, heads_here
     )
     key_start = (local_pos - position).astype(jnp.int32)
     theirs, mine = attend(
-        me.astype(jnp.int32).reshape(1), q_nope, q_first, q_second, expanded, latent_cache,
+        me.astype(jnp.int32).reshape(1), q_nope, q_rope, expanded, latent_cache,
         key_start, o_weight,
     )
     received = swap(theirs)

time: 162 us -> 161 us (level)
    pallas_call x1, Pallas kernels: 31.5 us -> 29.6 us  [attend(): pl.pallas_call(attention_kernel, grid_spec=grid_spec, out_shape=[jax.Shap...]
where the time goes in v8:
time: 161 us
  waiting for transfers between devices  57.5 us (36%)
  Pallas kernels  49.3 us (31%)
  between operations  19.3 us (12%)
  other arithmetic  15.4 us (10%)
  local copies, waits for them, and re-layouts  13.6 us (8%)
  matrix products  3.41 us (2%)
  starting transfers between devices  2.14 us (1%)
    all_gather x1, waiting for transfers between devices, body(): joined = lax.all_gather(joined, 'wide', axis=0, tiled=True)  54.7 us
    pallas_call x1, Pallas kernels, attend(): pl.pallas_call(attention_kernel, grid_spec=grid_spec, out_shape=[jax.Shap...  29.6 us
    pallas_call x1, Pallas kernels, project(): pl.pallas_call(project_kernel, grid=(rows // PBLOCK,), in_specs=[part(wid...  19.7 us
    convert_element_type x1, other arithmetic, body(): hidden = (tokens.astype(jnp.float32) + projected).astype(jnp.bfloat16)  5.01 us
    dot_general x1, matrix products, body(): jnp.dot(normed, chosen, preferred_element_type=jnp.float32)  3.41 us
  transfers between devices with their start and end apart: 4, of which 2 were waited for; matrix products, arithmetic and copies ran while one was open for 15% of the time, Pallas kernels for 0%

profile of v8, /device:TPU:1, one launch (start us, length us, event | category | flops | bytes accessed | tf_op | source)
XLA Modules:
  0.0 160.5 jit_solution(17670649574874094494)
XLA Ops:
  7.2 0.0 copy-start.3
  7.2 0.0 copy-start.1
  7.2 0.0 copy-start.4
  7.2 0.0 copy-start.6
  7.2 0.0 all-gather.2.cloned.1.call-start
  7.3 1.2 reshape.201
  8.4 0.1 fusion.11
  8.6 0.1 reshape.203
  8.7 0.1 reshape.204
  8.8 1.5 pad_maximum_fusion.4
  10.2 0.0 all-gather.2.cloned.1.call-update
  10.3 0.9 select_reduce_fusion.1
  11.1 0.6 fusion.13
  14.3 2.2 %constant_dynamic-slice_fusion.6 = (bf16[2048,16]{1,0:T(8,128)(2,1)S(1)}, bf16[2048,16]{1,0:T(8,128)(2,1)S(1)}, bf16[2048,16]{1,0:T(8,128)(2,1)S(1)}, bf16[2048,16]{1,0:T(8,128)(2,1)S(1)}) fusion(bf16[2048,512]{1,0:T(8,128)(2,1)} %param.19, s32[]{:T(128)S(6)} %select_n.57, s32[]{:T(128)S(6)} %select_n.58, s32[]{:T(128)S(6)} %select_n.60, s32[]{:T(128)S(6)} %select_n.59), kind=kLoop, calls=%fused_computation.38 | loop fusion | bytes 524304 | tf_op jit(solution)/shard_map/dynamic_slice | solution.py:260
  16.5 1.5 pad_maximum_fusion.1
  18.0 1.4 collective-permute-start.1
  19.4 0.0 copy-done.1
  19.4 0.0 collective-permute-start
  19.4 0.0 copy-done.3
  19.4 0.6 fusion.12
  22.5 0.0 copy-done.4
  22.5 0.1 broadcast_in_dim.16
  22.6 0.1 broadcast_in_dim.17
  22.7 0.0 copy-done.6
  22.7 0.2 reduce-window.4
  22.9 0.9 constant_dynamic-slice_fusion.2
  23.8 0.2 reshape.206
  24.0 0.0 copy-start.5
  24.1 0.1 fusion.10
  24.2 0.1 copy.34
  24.3 0.1 copy.27
  24.4 0.1 copy.35
  24.6 0.1 copy.28
  24.7 0.1 convert_reduce_fusion
  24.8 0.1 select_reduce_fusion
  24.9 0.6 slice.49.first_ref
  25.5 0.5 multiply_sine_fusion
  26.0 0.1 tile.8
  26.2 1.3 copy.30.cos_ref
  27.5 0.1 tile.20
  27.6 1.3 copy.31.sin_ref
  28.9 0.0 copy-done.5
  28.9 0.6 broadcast_in_dim.21
  29.5 1.0 copy.32.kst_ref
  30.5 0.7 pad_maximum_fusion.3.up_ref
  31.2 0.0 collective-permute-done
  31.2 1.9 %broadcast_select_fusion.1 = (bf16[1024,1024]{1,0:T(8,128)(2,1)S(1)}, bf16[1024,1024]{1,0:T(8,128)(2,1)S(1)}) fusion(bf16[1024,1024]{1,0:T(8,128)(2,1)S(1)} %copy-done.1, bf16[1024,1024]{1,0:T(8,128)(2,1)} %collective-permute-done, pred[]{:T(512)S(6)} %eq.56), kind=kLoop, calls=%fused_computation.8 | loop fusion | flops 2097152 | bytes 8388609 | tf_op jit(solution)/shard_map/jit(_where)/select_n | solution.py:249
  33.1 1.0 fusion
  34.1 1.4 fusion.2.x_ref
  35.5 0.0 copy-start
  35.5 0.0 collective-permute-done.1
  35.5 3.4 %fusion.3 = f32[1024,64]{0,1:T(8,128)S(1)} fusion(bf16[1024,2048]{1,0:T(8,128)(2,1)S(1)} %fusion.2.x_ref, bf16[2048,64]{1,0:T(8,128)(2,1)} %pad_maximum_fusion.1, bf16[2048,64]{1,0:T(8,128)(2,1)} %collective-permute-done.1, pred[64]{0:T(512)(128)(4,1)S(1)} %broadcast_in_dim.17), kind=kOutput, calls=%fused_computation.10 | convolution fusion | flops 268566528 | bytes 4980800 | tf_op jit(solution)/shard_map/dot_general | solution.py:275
  38.9 0.0 copy-done
  39.0 0.8 copy.29.sp_ref
  39.9 54.7 %all-gather.2.cloned.1.call-done.w_ref = bf16[2048,2112]{1,0:T(8,128)(2,1)} async-done(((bf16[32,2112]{1,0:T(8,128)(2,1)}), bf16[2048,2112]{1,0:T(8,128)(2,1)}) %all-gather.2.cloned.1.call-update) | async-done | bytes 8650768 | tf_op jit(solution)/shard_map/all_gather | solution.py:245
  94.6 19.7 %shard_map.131 = (bf16[1024,1024]{1,0:T(8,128)(2,1)}, bf16[8,1024,64]{2,1,0:T(8,128)(2,1)}, bf16[1024,576]{1,0:T(8,128)(2,1)}, bf16[1024,2048]{1,0:T(8,128)(2,1)}) custom-call(bf16[1024,2048]{1,0:T(8,128)(2,1)} %copy-done, bf16[2048,2112]{1,0:T(8,128)(2,1)} %all-gather.2.cloned.1.call-done.w_ref, bf16[1024,64]{1,0:T(8,128)(2,1)} %copy.29.sp_ref, ...), custom_call_target="tpu_custom_call" | custom-call | tf_op jit(solution)/shard_map/pallas_call | solution.py:102
  114.3 0.0 copy-start.2
  114.3 29.6 %shard_map.132 = (bf16[1024,1024]{1,0:T(8,128)(2,1)}, bf16[1024,1024]{1,0:T(8,128)(2,1)}) custom-call(s32[1]{0:T(128)} %bitcast.me_ref, s32[4]{0:T(128)} %slice.49.first_ref, bf16[1024,1024]{1,0:T(8,128)(2,1)} %get-tuple-element.8.q_nope_ref, bf16[8,1024,64]{2,1,0:T(8,128)(2,1)} %get-tuple-element.9.qr_ref, bf16[1024,2048]{1,0:T(8,128)(2,1)} %get-tuple-element.10.kv_ref, ...), custom_call_target="tpu_custom_call" | custom-call | tf_op jit(solution)/shard_map/pallas_call | solution.py:195
  143.9 0.7 collective-permute-start.2
  144.6 0.0 copy-done.2
  144.6 1.4 copy.33
  146.0 2.7 %collective-permute-done.2 = bf16[1024,1024]{1,0:T(8,128)(2,1)} collective-permute-done((bf16[1024,1024]{1,0:T(8,128)(2,1)}, bf16[1024,1024]{1,0:T(8,128)(2,1)}, u32[]{:S(2)}, u32[]{:S(2)}) %collective-permute-start.2) | collective-permute-done | bytes 2097184 | tf_op jit(solution)/shard_map/ppermute | solution.py:219
  148.7 5.0 %add_convert_fusion = bf16[1024,1024]{1,0:T(8,128)(2,1)} fusion(bf16[1024,1024]{1,0:T(8,128)(2,1)} %collective-permute-done.2, bf16[1024,1024]{1,0:T(8,128)(2,1)} %get-tuple-element.12, bf16[1024,1024]{1,0:T(8,128)(2,1)S(1)} %copy-done.1), kind=kLoop, calls=%fused_computation.6 | loop fusion | flops 6291456 | bytes 8388608 | tf_op jit(solution)/shard_map/convert_element_type | solution.py:302
  (15 shorter events, 0.2 us)
Async XLA Ops:
  7.2 12.2 %copy-start.3 = (s32[1,4]{1,0:T(1,128)S(1)}, s32[1,4]{1,0:T(1,128)}, u32[]{:S(2)}) copy-start(s32[1,4]{1,0:T(1,128)} %param.22) | copy-start | bytes 52
  7.2 12.2 %copy-start.1 = (bf16[1024,1024]{1,0:T(8,128)(2,1)S(1)}, bf16[1024,1024]{1,0:T(8,128)(2,1)}, u32[]{:S(2)}) copy-start(bf16[1024,1024]{1,0:T(8,128)(2,1)} %param.12) | copy-start | bytes 6291460
  7.2 15.3 %copy-start.4 = (bf16[2048]{0:T(1024)(128)(2,1)S(1)}, bf16[2048]{0:T(1024)(128)(2,1)}, u32[]{:S(2)}) copy-start(bf16[2048]{0:T(1024)(128)(2,1)} %param.13) | copy-start | bytes 12292
  7.2 15.5 %copy-start.6 = (s32[1,4]{1,0:T(1,128)S(1)}, s32[1,4]{1,0:T(1,128)}, u32[]{:S(2)}) copy-start(s32[1,4]{1,0:T(1,128)} %param.21) | copy-start | bytes 52
  7.2 87.4 %all-gather.2.cloned.1.call-start = ((), (), s32[]{:S(2)}) async-start(), calls=%async_computation | async-start | bytes 9052160 | tf_op jit(solution)/shard_map/all_gather | solution.py:245
  18.0 17.6 %collective-permute-start.1 = (bf16[2048,64]{1,0:T(8,128)(2,1)}, bf16[2048,64]{1,0:T(8,128)(2,1)}, u32[]{:S(2)}, u32[]{:S(2)}) collective-permute-start(bf16[2048,64]{1,0:T(8,128)(2,1)} %pad_maximum_fusion.1), channel_id=1, source_target_pairs={{0,1},{1,0},{2,3},{3,2},{4,5},{5,4},{6,7},{7,6},{8,9},{9,8},{10,11... | collective-permute-start | bytes 786440 | tf_op jit(solution)/shard_map/ppermute | solution.py:219
  19.4 11.9 %collective-permute-start = (bf16[1024,1024]{1,0:T(8,128)(2,1)S(1)}, bf16[1024,1024]{1,0:T(8,128)(2,1)}, u32[]{:S(2)}, u32[]{:S(2)}) collective-permute-start(bf16[1024,1024]{1,0:T(8,128)(2,1)S(1)} %copy-done.1), channel_id=1, source_target_pairs={{0,1},{1,0},{2,3},{3,2},{4,5},{5,4},{6,7},{7,6},{8,9},{9,8},{10,11... | collective-permute-start | bytes 6291464 | tf_op jit(solution)/shard_map/ppermute | solution.py:219
  24.0 4.9 %copy-start.5 = (bf16[512]{0:T(512)(128)(2,1)S(1)}, bf16[512]{0:T(512)(128)(2,1)}, u32[]{:S(2)}) copy-start(bf16[512]{0:T(512)(128)(2,1)} %param.16) | copy-start | bytes 3076
  35.5 3.4 %copy-start = (bf16[1024,2048]{1,0:T(8,128)(2,1)}, bf16[1024,2048]{1,0:T(8,128)(2,1)S(1)}, u32[]{:S(2)}) copy-start(bf16[1024,2048]{1,0:T(8,128)(2,1)S(1)} %fusion.2.x_ref) | copy-start | bytes 12582916
  114.3 30.3 %copy-start.2 = (bf16[1024,576]{1,0:T(8,128)(2,1)S(1)}, bf16[1024,576]{1,0:T(8,128)(2,1)}, u32[]{:S(2)}) copy-start(bf16[1024,576]{1,0:T(8,128)(2,1)} %get-tuple-element.19.cache_ref) | copy-start | bytes 3538948
  143.9 4.8 %collective-permute-start.2 = (bf16[1024,1024]{1,0:T(8,128)(2,1)}, bf16[1024,1024]{1,0:T(8,128)(2,1)}, u32[]{:S(2)}, u32[]{:S(2)}) collective-permute-start(bf16[1024,1024]{1,0:T(8,128)(2,1)} %get-tuple-element.13), channel_id=1, source_target_pairs={{0,1},{1,0},{2,3},{3,2},{4,5},{5,4},{6,7},{7,6},{8,9},{9,8},{10,11... | collective-permute-start | bytes 6291464 | tf_op jit(solution)/shard_map/ppermute | solution.py:219
Sparse Core Ops, SparseCore 0:
  10.8 83.7 all-gather.1

commit v9 on v8

--- a/solution.py
+++ b/solution.py
@@ -202,6 +202,23 @@
     )(me, key_start[::QBLOCK], q_nope, q_rope, kv, latent_cache, key_start[:, None], o_weight, o_weight)
 
 
+def finish_kernel(tok_ref, mine_ref, rec_ref, out_ref):
+    projected = mine_ref[...].astype(jnp.float32) + rec_ref[...].astype(jnp.float32)
+    out_ref[...] = (tok_ref[...].astype(jnp.float32) + projected).astype(out_ref.dtype)
+
+
+def finish(tokens, mine, received):
+    rows, cols = tokens.shape
+    spec = pl.BlockSpec((QBLOCK, cols), lambda i: (i, 0))
+    return pl.pallas_call(
+        finish_kernel,
+        grid=(rows // QBLOCK,),
+        in_specs=[spec, spec, spec],
+        out_specs=spec,
+        out_shape=jax.ShapeDtypeStruct((rows, cols), tokens.dtype),
+    )(tokens, mine, received)
+
+
 def split_heads(weight, heads):
     parts = weight.reshape(weight.shape[0], heads, NOPE + ROPE)
     half = ROPE // 2
@@ -298,8 +315,7 @@
         key_start, o_weight,
     )
     received = swap(theirs)
-    projected = mine.astype(jnp.float32) + received.astype(jnp.float32)
-    hidden = (tokens.astype(jnp.float32) + projected).astype(jnp.bfloat16)
+    hidden = finish(tokens, mine, received)
     return (hidden, latent_cache)
 
 

time: 161 us -> 160 us (level); the launches traced: 161 us -> 158 us
  other arithmetic: 15.4 us -> 10.3 us
  Pallas kernels: 49.3 us -> 51.4 us
    convert_element_type x1 -> x0, other arithmetic: 5.01 us -> none  [body(): hidden = (tokens.astype(jnp.float32) + projected).astype(jnp.bfloat16)]
    pallas_call x0 -> x1, Pallas kernels: none -> 4.83 us  [finish(): pl.pallas_call(finish_kernel, grid=(rows // QBLOCK,), in_specs=[spec, spe...]
    pallas_call x1, Pallas kernels: 29.6 us -> 26.9 us  [attend(): pl.pallas_call(attention_kernel, grid_spec=grid_spec, out_shape=[jax.Shap...]
where the time goes in v9:
time: 160 us; the launch traced here: 158 us
  waiting for transfers between devices  57.5 us (36%)
  Pallas kernels  51.4 us (32%)
  between operations  19.3 us (12%)
  local copies, waits for them, and re-layouts  13.6 us (8%)
  other arithmetic  10.3 us (6%)
  matrix products  3.41 us (2%)
  starting transfers between devices  2.14 us (1%)
    all_gather x1, waiting for transfers between devices, body(): joined = lax.all_gather(joined, 'wide', axis=0, tiled=True)  54.7 us
    pallas_call x1, Pallas kernels, attend(): pl.pallas_call(attention_kernel, grid_spec=grid_spec, out_shape=[jax.Shap...  26.9 us
    pallas_call x1, Pallas kernels, project(): pl.pallas_call(project_kernel, grid=(rows // PBLOCK,), in_specs=[part(wid...  19.7 us
    pallas_call x1, Pallas kernels, finish(): pl.pallas_call(finish_kernel, grid=(rows // QBLOCK,), in_specs=[spec, spe...  4.83 us
    dot_general x1, matrix products, body(): jnp.dot(normed, chosen, preferred_element_type=jnp.float32)  3.41 us
  transfers between devices with their start and end apart: 4, of which 2 were waited for; matrix products, arithmetic and copies ran while one was open for 15% of the time, Pallas kernels for 0%

profile of v9, /device:TPU:1, one launch (start us, length us, event | category | flops | bytes accessed | tf_op | source)
XLA Modules:
  0.0 157.7 jit_solution(3201497077344627462)
XLA Ops:
  7.2 0.0 copy-start.3
  7.2 0.0 copy-start.1
  7.2 0.0 copy-start.4
  7.2 0.0 copy-start.6
  7.2 0.0 all-gather.2.cloned.1.call-start
  7.3 1.2 reshape.201
  8.4 0.1 fusion.11
  8.6 0.1 reshape.203
  8.7 0.1 reshape.204
  8.8 1.5 pad_maximum_fusion.4
  10.2 0.0 all-gather.2.cloned.1.call-update
  10.3 0.9 select_reduce_fusion.1
  11.1 0.6 fusion.13
  14.3 2.2 %constant_dynamic-slice_fusion.6 = (bf16[2048,16]{1,0:T(8,128)(2,1)S(1)}, bf16[2048,16]{1,0:T(8,128)(2,1)S(1)}, bf16[2048,16]{1,0:T(8,128)(2,1)S(1)}, bf16[2048,16]{1,0:T(8,128)(2,1)S(1)}) fusion(bf16[2048,512]{1,0:T(8,128)(2,1)} %param.19, s32[]{:T(128)S(6)} %select_n.57, s32[]{:T(128)S(6)} %select_n.58, s32[]{:T(128)S(6)} %select_n.60, s32[]{:T(128)S(6)} %select_n.59), kind=kLoop, calls=%fused_computation.37 | loop fusion | bytes 524304 | tf_op jit(solution)/shard_map/dynamic_slice | solution.py:277
  16.5 1.5 pad_maximum_fusion.1
  18.0 1.4 collective-permute-start.1
  19.4 0.0 copy-done.1
  19.4 0.0 collective-permute-start
  19.4 0.0 copy-done.3
  19.4 0.6 fusion.12
  22.5 0.0 copy-done.4
  22.6 0.1 broadcast_in_dim.16
  22.6 0.1 broadcast_in_dim.17
  22.7 0.0 copy-done.6
  22.7 0.2 reduce-window.4
  22.9 0.9 constant_dynamic-slice_fusion.2
  23.8 0.2 reshape.206
  24.0 0.0 copy-start.5
  24.1 0.1 fusion.10
  24.2 0.1 copy.34
  24.3 0.1 copy.27
  24.4 0.1 copy.35
  24.6 0.1 copy.28
  24.7 0.1 convert_reduce_fusion
  24.8 0.1 select_reduce_fusion
  24.9 0.6 slice.49.first_ref
  25.5 0.5 multiply_sine_fusion
  26.0 0.1 tile.8
  26.2 1.3 copy.30.cos_ref
  27.5 0.1 tile.20
  27.6 1.3 copy.31.sin_ref
  28.9 0.0 copy-done.5
  28.9 0.6 broadcast_in_dim.21
  29.5 1.0 copy.32.kst_ref
  30.5 0.7 pad_maximum_fusion.3.up_ref
  31.2 0.0 collective-permute-done
  31.2 1.9 %broadcast_select_fusion.1 = (bf16[1024,1024]{1,0:T(8,128)(2,1)S(1)}, bf16[1024,1024]{1,0:T(8,128)(2,1)S(1)}) fusion(bf16[1024,1024]{1,0:T(8,128)(2,1)S(1)} %copy-done.1, bf16[1024,1024]{1,0:T(8,128)(2,1)} %collective-permute-done, pred[]{:T(512)S(6)} %eq.56), kind=kLoop, calls=%fused_computation.7 | loop fusion | flops 2097152 | bytes 8388609 | tf_op jit(solution)/shard_map/jit(_where)/select_n | solution.py:266
  33.1 1.0 fusion
  34.1 1.4 fusion.2.x_ref
  35.5 0.0 copy-start
  35.5 0.0 collective-permute-done.1
  35.5 3.4 %fusion.3 = f32[1024,64]{0,1:T(8,128)S(1)} fusion(bf16[1024,2048]{1,0:T(8,128)(2,1)S(1)} %fusion.2.x_ref, bf16[2048,64]{1,0:T(8,128)(2,1)} %pad_maximum_fusion.1, bf16[2048,64]{1,0:T(8,128)(2,1)} %collective-permute-done.1, pred[64]{0:T(512)(128)(4,1)S(1)} %broadcast_in_dim.17), kind=kOutput, calls=%fused_computation.9 | convolution fusion | flops 268566528 | bytes 4980800 | tf_op jit(solution)/shard_map/dot_general | solution.py:292
  39.0 0.0 copy-done
  39.0 0.8 copy.29.sp_ref
  39.9 54.7 %all-gather.2.cloned.1.call-done.w_ref = bf16[2048,2112]{1,0:T(8,128)(2,1)} async-done(((bf16[32,2112]{1,0:T(8,128)(2,1)}), bf16[2048,2112]{1,0:T(8,128)(2,1)}) %all-gather.2.cloned.1.call-update) | async-done | bytes 8650768 | tf_op jit(solution)/shard_map/all_gather | solution.py:262
  94.6 19.7 %shard_map.131 = (bf16[1024,1024]{1,0:T(8,128)(2,1)}, bf16[8,1024,64]{2,1,0:T(8,128)(2,1)}, bf16[1024,576]{1,0:T(8,128)(2,1)}, bf16[1024,2048]{1,0:T(8,128)(2,1)}) custom-call(bf16[1024,2048]{1,0:T(8,128)(2,1)} %copy-done, bf16[2048,2112]{1,0:T(8,128)(2,1)} %all-gather.2.cloned.1.call-done.w_ref, bf16[1024,64]{1,0:T(8,128)(2,1)} %copy.29.sp_ref, ...), custom_call_target="tpu_custom_call" | custom-call | tf_op jit(solution)/shard_map/pallas_call | solution.py:102
  114.3 0.0 copy-start.2
  114.3 26.9 %shard_map.132 = (bf16[1024,1024]{1,0:T(8,128)(2,1)}, bf16[1024,1024]{1,0:T(8,128)(2,1)}) custom-call(s32[1]{0:T(128)} %bitcast.me_ref, s32[4]{0:T(128)} %slice.49.first_ref, bf16[1024,1024]{1,0:T(8,128)(2,1)} %get-tuple-element.8.q_nope_ref, bf16[8,1024,64]{2,1,0:T(8,128)(2,1)} %get-tuple-element.9.qr_ref, bf16[1024,2048]{1,0:T(8,128)(2,1)} %get-tuple-element.10.kv_ref, ...), custom_call_target="tpu_custom_call" | custom-call | tf_op jit(solution)/shard_map/pallas_call | solution.py:195
  141.2 0.7 collective-permute-start.2
  141.8 0.0 copy-done.2
  141.8 1.4 copy.33
  143.3 2.7 %collective-permute-done.2.rec_ref = bf16[1024,1024]{1,0:T(8,128)(2,1)} collective-permute-done((bf16[1024,1024]{1,0:T(8,128)(2,1)}, bf16[1024,1024]{1,0:T(8,128)(2,1)}, u32[]{:S(2)}, u32[]{:S(2)}) %collective-permute-start.2) | collective-permute-done | bytes 2097184 | tf_op jit(solution)/shard_map/ppermute | solution.py:236
  146.0 4.8 %shard_map.133 = bf16[1024,1024]{1,0:T(8,128)(2,1)} custom-call(bf16[1024,1024]{1,0:T(8,128)(2,1)} %tok_ref.1, bf16[1024,1024]{1,0:T(8,128)(2,1)} %get-tuple-element.12.mine_ref, bf16[1024,1024]{1,0:T(8,128)(2,1)} %collective-permute-done.2.rec_ref), custom_call_target="tpu_custom_call" | custom-call | tf_op jit(solution)/shard_map/pallas_call | solution.py:213
  (15 shorter events, 0.2 us)
Async XLA Ops:
  7.2 12.2 %copy-start.3 = (s32[1,4]{1,0:T(1,128)S(1)}, s32[1,4]{1,0:T(1,128)}, u32[]{:S(2)}) copy-start(s32[1,4]{1,0:T(1,128)} %param.22) | copy-start | bytes 52
  7.2 12.2 %copy-start.1 = (bf16[1024,1024]{1,0:T(8,128)(2,1)S(1)}, bf16[1024,1024]{1,0:T(8,128)(2,1)}, u32[]{:S(2)}) copy-start(bf16[1024,1024]{1,0:T(8,128)(2,1)} %tok_ref.1) | copy-start | bytes 6291460
  7.2 15.3 %copy-start.4 = (bf16[2048]{0:T(1024)(128)(2,1)S(1)}, bf16[2048]{0:T(1024)(128)(2,1)}, u32[]{:S(2)}) copy-start(bf16[2048]{0:T(1024)(128)(2,1)} %param.13) | copy-start | bytes 12292
  7.2 15.5 %copy-start.6 = (s32[1,4]{1,0:T(1,128)S(1)}, s32[1,4]{1,0:T(1,128)}, u32[]{:S(2)}) copy-start(s32[1,4]{1,0:T(1,128)} %param.21) | copy-start | bytes 52
  7.2 87.4 %all-gather.2.cloned.1.call-start = ((), (), s32[]{:S(2)}) async-start(), calls=%async_computation | async-start | bytes 9052160 | tf_op jit(solution)/shard_map/all_gather | solution.py:262
  18.0 17.6 %collective-permute-start.1 = (bf16[2048,64]{1,0:T(8,128)(2,1)}, bf16[2048,64]{1,0:T(8,128)(2,1)}, u32[]{:S(2)}, u32[]{:S(2)}) collective-permute-start(bf16[2048,64]{1,0:T(8,128)(2,1)} %pad_maximum_fusion.1), channel_id=1, source_target_pairs={{0,1},{1,0},{2,3},{3,2},{4,5},{5,4},{6,7},{7,6},{8,9},{9,8},{10,11... | collective-permute-start | bytes 786440 | tf_op jit(solution)/shard_map/ppermute | solution.py:236
  19.4 11.9 %collective-permute-start = (bf16[1024,1024]{1,0:T(8,128)(2,1)S(1)}, bf16[1024,1024]{1,0:T(8,128)(2,1)}, u32[]{:S(2)}, u32[]{:S(2)}) collective-permute-start(bf16[1024,1024]{1,0:T(8,128)(2,1)S(1)} %copy-done.1), channel_id=1, source_target_pairs={{0,1},{1,0},{2,3},{3,2},{4,5},{5,4},{6,7},{7,6},{8,9},{9,8},{10,11... | collective-permute-start | bytes 6291464 | tf_op jit(solution)/shard_map/ppermute | solution.py:236
  24.0 4.9 %copy-start.5 = (bf16[512]{0:T(512)(128)(2,1)S(1)}, bf16[512]{0:T(512)(128)(2,1)}, u32[]{:S(2)}) copy-start(bf16[512]{0:T(512)(128)(2,1)} %param.16) | copy-start | bytes 3076
  35.5 3.4 %copy-start = (bf16[1024,2048]{1,0:T(8,128)(2,1)}, bf16[1024,2048]{1,0:T(8,128)(2,1)S(1)}, u32[]{:S(2)}) copy-start(bf16[1024,2048]{1,0:T(8,128)(2,1)S(1)} %fusion.2.x_ref) | copy-start | bytes 12582916
  114.3 27.6 %copy-start.2 = (bf16[1024,576]{1,0:T(8,128)(2,1)S(1)}, bf16[1024,576]{1,0:T(8,128)(2,1)}, u32[]{:S(2)}) copy-start(bf16[1024,576]{1,0:T(8,128)(2,1)} %get-tuple-element.19.cache_ref) | copy-start | bytes 3538948
  141.2 4.8 %collective-permute-start.2 = (bf16[1024,1024]{1,0:T(8,128)(2,1)}, bf16[1024,1024]{1,0:T(8,128)(2,1)}, u32[]{:S(2)}, u32[]{:S(2)}) collective-permute-start(bf16[1024,1024]{1,0:T(8,128)(2,1)} %get-tuple-element.13), channel_id=1, source_target_pairs={{0,1},{1,0},{2,3},{3,2},{4,5},{5,4},{6,7},{7,6},{8,9},{9,8},{10,11... | collective-permute-start | bytes 6291464 | tf_op jit(solution)/shard_map/ppermute | solution.py:236
Sparse Core Ops, SparseCore 0:
  10.8 83.7 all-gather.1

commit v10 on v9

--- a/solution.py
+++ b/solution.py
@@ -150,20 +150,13 @@
             ).astype(att_ref.dtype)
 
     first = first_ref[i]
-    one = first >= i * QBLOCK
-    two = jnp.logical_and(jnp.logical_not(one), first >= i * QBLOCK - QBLOCK)
-
-    @pl.when(one)
-    def _():
-        run(i * QBLOCK, QBLOCK)
-
-    @pl.when(two)
-    def _():
-        run(jnp.maximum(i * QBLOCK - QBLOCK, 0), 2 * QBLOCK)
-
-    @pl.when(jnp.logical_not(jnp.logical_or(one, two)))
-    def _():
-        run(jnp.maximum(i * QBLOCK - LMAX, 0), WINDOW)
+    steps = LMAX // 128
+    extra = jnp.clip((i * QBLOCK - first + 127) // 128, 0, steps)
+    for k in range(steps + 1):
+
+        @pl.when(extra == k)
+        def _():
+            run(jnp.maximum(i * QBLOCK - 128 * k, 0), QBLOCK + 128 * k)
 
     att = att_ref[...]
     theirs_ref[...] = jnp.dot(att, wt_ref[...], preferred_element_type=jnp.float32).astype(theirs_ref.dtype)

time: 160 us -> 160 us (level); the launches traced: 158 us -> 160 us
  Pallas kernels: 51.4 us -> 54.2 us
    pallas_call x1, Pallas kernels: 26.9 us -> 29.6 us  [attend(): pl.pallas_call(attention_kernel, grid_spec=grid_spec, out_shape=[jax.Shap...]
where the time goes in v10:
time: 160 us
  waiting for transfers between devices  57.5 us (36%)
  Pallas kernels  54.2 us (34%)
  between operations  19.3 us (12%)
  local copies, waits for them, and re-layouts  13.6 us (8%)
  other arithmetic  10.3 us (6%)
  matrix products  3.41 us (2%)
  starting transfers between devices  2.1 us (1%)
    all_gather x1, waiting for transfers between devices, body(): joined = lax.all_gather(joined, 'wide', axis=0, tiled=True)  54.7 us
    pallas_call x1, Pallas kernels, attend(): pl.pallas_call(attention_kernel, grid_spec=grid_spec, out_shape=[jax.Shap...  29.6 us
    pallas_call x1, Pallas kernels, project(): pl.pallas_call(project_kernel, grid=(rows // PBLOCK,), in_specs=[part(wid...  19.7 us
    pallas_call x1, Pallas kernels, finish(): pl.pallas_call(finish_kernel, grid=(rows // QBLOCK,), in_specs=[spec, spe...  4.83 us
    dot_general x1, matrix products, body(): jnp.dot(normed, chosen, preferred_element_type=jnp.float32)  3.41 us
  transfers between devices with their start and end apart: 4, of which 2 were waited for; matrix products, arithmetic and copies ran while one was open for 15% of the time, Pallas kernels for 0%

profile of v10, /device:TPU:1, one launch (start us, length us, event | category | flops | bytes accessed | tf_op | source)
XLA Modules:
  0.0 160.4 jit_solution(10030069889010227760)
XLA Ops:
  7.2 0.0 copy-start.3
  7.2 0.0 copy-start.1
  7.2 0.0 copy-start.4
  7.2 0.0 copy-start.6
  7.2 0.0 all-gather.2.cloned.1.call-start
  7.3 1.2 reshape.201
  8.4 0.1 fusion.11
  8.6 0.1 reshape.203
  8.7 0.1 reshape.204
  8.8 1.5 pad_maximum_fusion.4
  10.2 0.0 all-gather.2.cloned.1.call-update
  10.3 0.9 select_reduce_fusion.1
  11.1 0.6 fusion.13
  14.3 2.2 %constant_dynamic-slice_fusion.6 = (bf16[2048,16]{1,0:T(8,128)(2,1)S(1)}, bf16[2048,16]{1,0:T(8,128)(2,1)S(1)}, bf16[2048,16]{1,0:T(8,128)(2,1)S(1)}, bf16[2048,16]{1,0:T(8,128)(2,1)S(1)}) fusion(bf16[2048,512]{1,0:T(8,128)(2,1)} %param.19, s32[]{:T(128)S(6)} %select_n.57, s32[]{:T(128)S(6)} %select_n.58, s32[]{:T(128)S(6)} %select_n.60, s32[]{:T(128)S(6)} %select_n.59), kind=kLoop, calls=%fused_computation.37 | loop fusion | bytes 524304 | tf_op jit(solution)/shard_map/dynamic_slice | solution.py:270
  16.5 1.5 pad_maximum_fusion.1
  18.0 1.4 collective-permute-start.1
  19.4 0.0 copy-done.1
  19.4 0.0 collective-permute-start
  19.4 0.0 copy-done.3
  19.4 0.6 fusion.12
  22.5 0.0 copy-done.4
  22.6 0.1 broadcast_in_dim.16
  22.6 0.1 broadcast_in_dim.17
  22.7 0.0 copy-done.6
  22.7 0.2 reduce-window.4
  22.9 0.9 constant_dynamic-slice_fusion.2
  23.8 0.2 reshape.206
  24.0 0.0 copy-start.5
  24.1 0.1 fusion.10
  24.2 0.1 copy.34
  24.3 0.1 copy.27
  24.4 0.1 copy.35
  24.6 0.1 copy.28
  24.7 0.1 convert_reduce_fusion
  24.8 0.1 select_reduce_fusion
  24.9 0.6 slice.49.first_ref
  25.5 0.5 multiply_sine_fusion
  26.0 0.1 tile.8
  26.2 1.3 copy.30.cos_ref
  27.5 0.1 tile.20
  27.6 1.3 copy.31.sin_ref
  28.9 0.0 copy-done.5
  28.9 0.6 broadcast_in_dim.21
  29.5 1.0 copy.32.kst_ref
  30.5 0.7 pad_maximum_fusion.3.up_ref
  31.2 0.0 collective-permute-done
  31.2 1.9 %broadcast_select_fusion.1 = (bf16[1024,1024]{1,0:T(8,128)(2,1)S(1)}, bf16[1024,1024]{1,0:T(8,128)(2,1)S(1)}) fusion(bf16[1024,1024]{1,0:T(8,128)(2,1)S(1)} %copy-done.1, bf16[1024,1024]{1,0:T(8,128)(2,1)} %collective-permute-done, pred[]{:T(512)S(6)} %eq.56), kind=kLoop, calls=%fused_computation.7 | loop fusion | flops 2097152 | bytes 8388609 | tf_op jit(solution)/shard_map/jit(_where)/select_n | solution.py:259
  33.1 1.0 fusion
  34.1 1.4 fusion.2.x_ref
  35.5 0.0 copy-start
  35.5 0.0 collective-permute-done.1
  35.5 3.4 %fusion.3 = f32[1024,64]{0,1:T(8,128)S(1)} fusion(bf16[1024,2048]{1,0:T(8,128)(2,1)S(1)} %fusion.2.x_ref, bf16[2048,64]{1,0:T(8,128)(2,1)} %pad_maximum_fusion.1, bf16[2048,64]{1,0:T(8,128)(2,1)} %collective-permute-done.1, pred[64]{0:T(512)(128)(4,1)S(1)} %broadcast_in_dim.17), kind=kOutput, calls=%fused_computation.9 | convolution fusion | flops 268566528 | bytes 4980800 | tf_op jit(solution)/shard_map/dot_general | solution.py:285
  39.0 0.0 copy-done
  39.0 0.8 copy.29.sp_ref
  39.9 54.7 %all-gather.2.cloned.1.call-done.w_ref = bf16[2048,2112]{1,0:T(8,128)(2,1)} async-done(((bf16[32,2112]{1,0:T(8,128)(2,1)}), bf16[2048,2112]{1,0:T(8,128)(2,1)}) %all-gather.2.cloned.1.call-update) | async-done | bytes 8650768 | tf_op jit(solution)/shard_map/all_gather | solution.py:255
  94.6 19.7 %shard_map.131 = (bf16[1024,1024]{1,0:T(8,128)(2,1)}, bf16[8,1024,64]{2,1,0:T(8,128)(2,1)}, bf16[1024,576]{1,0:T(8,128)(2,1)}, bf16[1024,2048]{1,0:T(8,128)(2,1)}) custom-call(bf16[1024,2048]{1,0:T(8,128)(2,1)} %copy-done, bf16[2048,2112]{1,0:T(8,128)(2,1)} %all-gather.2.cloned.1.call-done.w_ref, bf16[1024,64]{1,0:T(8,128)(2,1)} %copy.29.sp_ref, ...), custom_call_target="tpu_custom_call" | custom-call | tf_op jit(solution)/shard_map/pallas_call | solution.py:102
  114.3 0.0 copy-start.2
  114.3 29.6 %shard_map.132 = (bf16[1024,1024]{1,0:T(8,128)(2,1)}, bf16[1024,1024]{1,0:T(8,128)(2,1)}) custom-call(s32[1]{0:T(128)} %bitcast.me_ref, s32[4]{0:T(128)} %slice.49.first_ref, bf16[1024,1024]{1,0:T(8,128)(2,1)} %get-tuple-element.8.q_nope_ref, bf16[8,1024,64]{2,1,0:T(8,128)(2,1)} %get-tuple-element.9.qr_ref, bf16[1024,2048]{1,0:T(8,128)(2,1)} %get-tuple-element.10.kv_ref, ...), custom_call_target="tpu_custom_call" | custom-call | tf_op jit(solution)/shard_map/pallas_call | solution.py:188
  144.0 0.6 collective-permute-start.2
  144.6 0.0 copy-done.2
  144.6 1.4 copy.33
  146.0 2.7 %collective-permute-done.2.rec_ref = bf16[1024,1024]{1,0:T(8,128)(2,1)} collective-permute-done((bf16[1024,1024]{1,0:T(8,128)(2,1)}, bf16[1024,1024]{1,0:T(8,128)(2,1)}, u32[]{:S(2)}, u32[]{:S(2)}) %collective-permute-start.2) | collective-permute-done | bytes 2097184 | tf_op jit(solution)/shard_map/ppermute | solution.py:229
  148.7 4.8 %shard_map.133 = bf16[1024,1024]{1,0:T(8,128)(2,1)} custom-call(bf16[1024,1024]{1,0:T(8,128)(2,1)} %tok_ref.1, bf16[1024,1024]{1,0:T(8,128)(2,1)} %get-tuple-element.12.mine_ref, bf16[1024,1024]{1,0:T(8,128)(2,1)} %collective-permute-done.2.rec_ref), custom_call_target="tpu_custom_call" | custom-call | tf_op jit(solution)/shard_map/pallas_call | solution.py:206
  (15 shorter events, 0.2 us)
Async XLA Ops:
  7.2 12.2 %copy-start.3 = (s32[1,4]{1,0:T(1,128)S(1)}, s32[1,4]{1,0:T(1,128)}, u32[]{:S(2)}) copy-start(s32[1,4]{1,0:T(1,128)} %param.22) | copy-start | bytes 52
  7.2 12.2 %copy-start.1 = (bf16[1024,1024]{1,0:T(8,128)(2,1)S(1)}, bf16[1024,1024]{1,0:T(8,128)(2,1)}, u32[]{:S(2)}) copy-start(bf16[1024,1024]{1,0:T(8,128)(2,1)} %tok_ref.1) | copy-start | bytes 6291460
  7.2 15.3 %copy-start.4 = (bf16[2048]{0:T(1024)(128)(2,1)S(1)}, bf16[2048]{0:T(1024)(128)(2,1)}, u32[]{:S(2)}) copy-start(bf16[2048]{0:T(1024)(128)(2,1)} %param.13) | copy-start | bytes 12292
  7.2 15.5 %copy-start.6 = (s32[1,4]{1,0:T(1,128)S(1)}, s32[1,4]{1,0:T(1,128)}, u32[]{:S(2)}) copy-start(s32[1,4]{1,0:T(1,128)} %param.21) | copy-start | bytes 52
  7.2 87.4 %all-gather.2.cloned.1.call-start = ((), (), s32[]{:S(2)}) async-start(), calls=%async_computation | async-start | bytes 9052160 | tf_op jit(solution)/shard_map/all_gather | solution.py:255
  18.0 17.6 %collective-permute-start.1 = (bf16[2048,64]{1,0:T(8,128)(2,1)}, bf16[2048,64]{1,0:T(8,128)(2,1)}, u32[]{:S(2)}, u32[]{:S(2)}) collective-permute-start(bf16[2048,64]{1,0:T(8,128)(2,1)} %pad_maximum_fusion.1), channel_id=1, source_target_pairs={{0,1},{1,0},{2,3},{3,2},{4,5},{5,4},{6,7},{7,6},{8,9},{9,8},{10,11... | collective-permute-start | bytes 786440 | tf_op jit(solution)/shard_map/ppermute | solution.py:229
  19.4 11.9 %collective-permute-start = (bf16[1024,1024]{1,0:T(8,128)(2,1)S(1)}, bf16[1024,1024]{1,0:T(8,128)(2,1)}, u32[]{:S(2)}, u32[]{:S(2)}) collective-permute-start(bf16[1024,1024]{1,0:T(8,128)(2,1)S(1)} %copy-done.1), channel_id=1, source_target_pairs={{0,1},{1,0},{2,3},{3,2},{4,5},{5,4},{6,7},{7,6},{8,9},{9,8},{10,11... | collective-permute-start | bytes 6291464 | tf_op jit(solution)/shard_map/ppermute | solution.py:229
  24.0 4.9 %copy-start.5 = (bf16[512]{0:T(512)(128)(2,1)S(1)}, bf16[512]{0:T(512)(128)(2,1)}, u32[]{:S(2)}) copy-start(bf16[512]{0:T(512)(128)(2,1)} %param.16) | copy-start | bytes 3076
  35.5 3.4 %copy-start = (bf16[1024,2048]{1,0:T(8,128)(2,1)}, bf16[1024,2048]{1,0:T(8,128)(2,1)S(1)}, u32[]{:S(2)}) copy-start(bf16[1024,2048]{1,0:T(8,128)(2,1)S(1)} %fusion.2.x_ref) | copy-start | bytes 12582916
  114.3 30.3 %copy-start.2 = (bf16[1024,576]{1,0:T(8,128)(2,1)S(1)}, bf16[1024,576]{1,0:T(8,128)(2,1)}, u32[]{:S(2)}) copy-start(bf16[1024,576]{1,0:T(8,128)(2,1)} %get-tuple-element.19.cache_ref) | copy-start | bytes 3538948
  144.0 4.8 %collective-permute-start.2 = (bf16[1024,1024]{1,0:T(8,128)(2,1)}, bf16[1024,1024]{1,0:T(8,128)(2,1)}, u32[]{:S(2)}, u32[]{:S(2)}) collective-permute-start(bf16[1024,1024]{1,0:T(8,128)(2,1)} %get-tuple-element.13), channel_id=1, source_target_pairs={{0,1},{1,0},{2,3},{3,2},{4,5},{5,4},{6,7},{7,6},{8,9},{9,8},{10,11... | collective-permute-start | bytes 6291464 | tf_op jit(solution)/shard_map/ppermute | solution.py:229
Sparse Core Ops, SparseCore 0:
  10.8 83.7 all-gather.1

commit v11 on v9

--- a/solution.py
+++ b/solution.py
@@ -13,7 +13,7 @@
 LMAX = 512
 QBLOCK = 256
 WINDOW = QBLOCK + LMAX
-PBLOCK = 256
+PBLOCK = 512
 
 
 EPS = 1e-06

time: 160 us -> 161 us (level); the launches traced: 158 us -> 161 us
  Pallas kernels: 51.4 us -> 55.1 us
    pallas_call x1, Pallas kernels: 26.9 us -> 29.6 us  [attend(): pl.pallas_call(attention_kernel, grid_spec=grid_spec, out_shape=[jax.Shap...]
where the time goes in v11:
time: 161 us
  waiting for transfers between devices  57.5 us (36%)
  Pallas kernels  55.1 us (34%)
  between operations  19.3 us (12%)
  local copies, waits for them, and re-layouts  13.6 us (8%)
  other arithmetic  10.3 us (6%)
  matrix products  3.41 us (2%)
  starting transfers between devices  2.14 us (1%)
    all_gather x1, waiting for transfers between devices, body(): joined = lax.all_gather(joined, 'wide', axis=0, tiled=True)  54.7 us
    pallas_call x1, Pallas kernels, attend(): pl.pallas_call(attention_kernel, grid_spec=grid_spec, out_shape=[jax.Shap...  29.6 us
    pallas_call x1, Pallas kernels, project(): pl.pallas_call(project_kernel, grid=(rows // PBLOCK,), in_specs=[part(wid...  20.6 us
    pallas_call x1, Pallas kernels, finish(): pl.pallas_call(finish_kernel, grid=(rows // QBLOCK,), in_specs=[spec, spe...  4.83 us
    dot_general x1, matrix products, body(): jnp.dot(normed, chosen, preferred_element_type=jnp.float32)  3.41 us
  transfers between devices with their start and end apart: 4, of which 2 were waited for; matrix products, arithmetic and copies ran while one was open for 15% of the time, Pallas kernels for 0%

profile of v11, /device:TPU:1, one launch (start us, length us, event | category | flops | bytes accessed | tf_op | source)
XLA Modules:
  0.0 161.3 jit_solution(5392789015737039929)
XLA Ops:
  7.2 0.0 copy-start.3
  7.2 0.0 copy-start.1
  7.2 0.0 copy-start.4
  7.2 0.0 copy-start.6
  7.2 0.0 all-gather.2.cloned.1.call-start
  7.3 1.2 reshape.201
  8.4 0.1 fusion.11
  8.6 0.1 reshape.203
  8.7 0.1 reshape.204
  8.8 1.5 pad_maximum_fusion.4
  10.2 0.0 all-gather.2.cloned.1.call-update
  10.3 0.9 select_reduce_fusion.1
  11.1 0.6 fusion.13
  14.3 2.2 %constant_dynamic-slice_fusion.6 = (bf16[2048,16]{1,0:T(8,128)(2,1)S(1)}, bf16[2048,16]{1,0:T(8,128)(2,1)S(1)}, bf16[2048,16]{1,0:T(8,128)(2,1)S(1)}, bf16[2048,16]{1,0:T(8,128)(2,1)S(1)}) fusion(bf16[2048,512]{1,0:T(8,128)(2,1)} %param.19, s32[]{:T(128)S(6)} %select_n.57, s32[]{:T(128)S(6)} %select_n.58, s32[]{:T(128)S(6)} %select_n.60, s32[]{:T(128)S(6)} %select_n.59), kind=kLoop, calls=%fused_computation.37 | loop fusion | bytes 524304 | tf_op jit(solution)/shard_map/dynamic_slice | solution.py:277
  16.5 1.5 pad_maximum_fusion.1
  18.0 1.4 collective-permute-start.1
  19.4 0.0 copy-done.1
  19.4 0.0 collective-permute-start
  19.4 0.0 copy-done.3
  19.4 0.6 fusion.12
  22.5 0.0 copy-done.4
  22.6 0.1 broadcast_in_dim.16
  22.6 0.1 broadcast_in_dim.17
  22.7 0.0 copy-done.6
  22.7 0.2 reduce-window.4
  22.9 0.9 constant_dynamic-slice_fusion.2
  23.8 0.2 reshape.206
  24.1 0.0 copy-start.5
  24.1 0.1 fusion.10
  24.2 0.1 copy.34
  24.3 0.1 copy.27
  24.4 0.1 copy.35
  24.6 0.1 copy.28
  24.7 0.1 convert_reduce_fusion
  24.8 0.1 select_reduce_fusion
  24.9 0.6 slice.49.first_ref
  25.5 0.5 multiply_sine_fusion
  26.1 0.1 tile.8
  26.2 1.3 copy.30.cos_ref
  27.5 0.1 tile.20
  27.6 1.3 copy.31.sin_ref
  28.9 0.0 copy-done.5
  28.9 0.6 broadcast_in_dim.21
  29.5 1.0 copy.32.kst_ref
  30.5 0.7 pad_maximum_fusion.3.up_ref
  31.2 0.0 collective-permute-done
  31.3 1.9 %broadcast_select_fusion.1 = (bf16[1024,1024]{1,0:T(8,128)(2,1)S(1)}, bf16[1024,1024]{1,0:T(8,128)(2,1)S(1)}) fusion(bf16[1024,1024]{1,0:T(8,128)(2,1)S(1)} %copy-done.1, bf16[1024,1024]{1,0:T(8,128)(2,1)} %collective-permute-done, pred[]{:T(512)S(6)} %eq.56), kind=kLoop, calls=%fused_computation.7 | loop fusion | flops 2097152 | bytes 8388609 | tf_op jit(solution)/shard_map/jit(_where)/select_n | solution.py:266
  33.1 1.0 fusion
  34.1 1.4 fusion.2.x_ref
  35.5 0.0 copy-start
  35.5 0.0 collective-permute-done.1
  35.6 3.4 %fusion.3 = f32[1024,64]{0,1:T(8,128)S(1)} fusion(bf16[1024,2048]{1,0:T(8,128)(2,1)S(1)} %fusion.2.x_ref, bf16[2048,64]{1,0:T(8,128)(2,1)} %pad_maximum_fusion.1, bf16[2048,64]{1,0:T(8,128)(2,1)} %collective-permute-done.1, pred[64]{0:T(512)(128)(4,1)S(1)} %broadcast_in_dim.17), kind=kOutput, calls=%fused_computation.9 | convolution fusion | flops 268566528 | bytes 4980800 | tf_op jit(solution)/shard_map/dot_general | solution.py:292
  39.0 0.0 copy-done
  39.0 0.8 copy.29.sp_ref
  39.9 54.7 %all-gather.2.cloned.1.call-done.w_ref = bf16[2048,2112]{1,0:T(8,128)(2,1)} async-done(((bf16[32,2112]{1,0:T(8,128)(2,1)}), bf16[2048,2112]{1,0:T(8,128)(2,1)}) %all-gather.2.cloned.1.call-update) | async-done | bytes 8650768 | tf_op jit(solution)/shard_map/all_gather | solution.py:262
  94.6 20.6 %shard_map.131 = (bf16[1024,1024]{1,0:T(8,128)(2,1)}, bf16[8,1024,64]{2,1,0:T(8,128)(2,1)}, bf16[1024,576]{1,0:T(8,128)(2,1)}, bf16[1024,2048]{1,0:T(8,128)(2,1)}) custom-call(bf16[1024,2048]{1,0:T(8,128)(2,1)} %copy-done, bf16[2048,2112]{1,0:T(8,128)(2,1)} %all-gather.2.cloned.1.call-done.w_ref, bf16[1024,64]{1,0:T(8,128)(2,1)} %copy.29.sp_ref, ...), custom_call_target="tpu_custom_call" | custom-call | tf_op jit(solution)/shard_map/pallas_call | solution.py:102
  115.2 0.0 copy-start.2
  115.2 29.6 %shard_map.132 = (bf16[1024,1024]{1,0:T(8,128)(2,1)}, bf16[1024,1024]{1,0:T(8,128)(2,1)}) custom-call(s32[1]{0:T(128)} %bitcast.me_ref, s32[4]{0:T(128)} %slice.49.first_ref, bf16[1024,1024]{1,0:T(8,128)(2,1)} %get-tuple-element.8.q_nope_ref, bf16[8,1024,64]{2,1,0:T(8,128)(2,1)} %get-tuple-element.9.qr_ref, bf16[1024,2048]{1,0:T(8,128)(2,1)} %get-tuple-element.10.kv_ref, ...), custom_call_target="tpu_custom_call" | custom-call | tf_op jit(solution)/shard_map/pallas_call | solution.py:195
  144.9 0.7 collective-permute-start.2
  145.5 0.0 copy-done.2
  145.5 1.4 copy.33
  147.0 2.7 %collective-permute-done.2.rec_ref = bf16[1024,1024]{1,0:T(8,128)(2,1)} collective-permute-done((bf16[1024,1024]{1,0:T(8,128)(2,1)}, bf16[1024,1024]{1,0:T(8,128)(2,1)}, u32[]{:S(2)}, u32[]{:S(2)}) %collective-permute-start.2) | collective-permute-done | bytes 2097184 | tf_op jit(solution)/shard_map/ppermute | solution.py:236
  149.7 4.8 %shard_map.133 = bf16[1024,1024]{1,0:T(8,128)(2,1)} custom-call(bf16[1024,1024]{1,0:T(8,128)(2,1)} %tok_ref.1, bf16[1024,1024]{1,0:T(8,128)(2,1)} %get-tuple-element.12.mine_ref, bf16[1024,1024]{1,0:T(8,128)(2,1)} %collective-permute-done.2.rec_ref), custom_call_target="tpu_custom_call" | custom-call | tf_op jit(solution)/shard_map/pallas_call | solution.py:213
  (15 shorter events, 0.2 us)
Async XLA Ops:
  7.2 12.2 %copy-start.3 = (s32[1,4]{1,0:T(1,128)S(1)}, s32[1,4]{1,0:T(1,128)}, u32[]{:S(2)}) copy-start(s32[1,4]{1,0:T(1,128)} %param.22) | copy-start | bytes 52
  7.2 12.2 %copy-start.1 = (bf16[1024,1024]{1,0:T(8,128)(2,1)S(1)}, bf16[1024,1024]{1,0:T(8,128)(2,1)}, u32[]{:S(2)}) copy-start(bf16[1024,1024]{1,0:T(8,128)(2,1)} %tok_ref.1) | copy-start | bytes 6291460
  7.2 15.3 %copy-start.4 = (bf16[2048]{0:T(1024)(128)(2,1)S(1)}, bf16[2048]{0:T(1024)(128)(2,1)}, u32[]{:S(2)}) copy-start(bf16[2048]{0:T(1024)(128)(2,1)} %param.13) | copy-start | bytes 12292
  7.2 15.5 %copy-start.6 = (s32[1,4]{1,0:T(1,128)S(1)}, s32[1,4]{1,0:T(1,128)}, u32[]{:S(2)}) copy-start(s32[1,4]{1,0:T(1,128)} %param.21) | copy-start | bytes 52
  7.2 87.4 %all-gather.2.cloned.1.call-start = ((), (), s32[]{:S(2)}) async-start(), calls=%async_computation | async-start | bytes 9052160 | tf_op jit(solution)/shard_map/all_gather | solution.py:262
  18.0 17.6 %collective-permute-start.1 = (bf16[2048,64]{1,0:T(8,128)(2,1)}, bf16[2048,64]{1,0:T(8,128)(2,1)}, u32[]{:S(2)}, u32[]{:S(2)}) collective-permute-start(bf16[2048,64]{1,0:T(8,128)(2,1)} %pad_maximum_fusion.1), channel_id=1, source_target_pairs={{0,1},{1,0},{2,3},{3,2},{4,5},{5,4},{6,7},{7,6},{8,9},{9,8},{10,11... | collective-permute-start | bytes 786440 | tf_op jit(solution)/shard_map/ppermute | solution.py:236
  19.4 11.9 %collective-permute-start = (bf16[1024,1024]{1,0:T(8,128)(2,1)S(1)}, bf16[1024,1024]{1,0:T(8,128)(2,1)}, u32[]{:S(2)}, u32[]{:S(2)}) collective-permute-start(bf16[1024,1024]{1,0:T(8,128)(2,1)S(1)} %copy-done.1), channel_id=1, source_target_pairs={{0,1},{1,0},{2,3},{3,2},{4,5},{5,4},{6,7},{7,6},{8,9},{9,8},{10,11... | collective-permute-start | bytes 6291464 | tf_op jit(solution)/shard_map/ppermute | solution.py:236
  24.1 4.9 %copy-start.5 = (bf16[512]{0:T(512)(128)(2,1)S(1)}, bf16[512]{0:T(512)(128)(2,1)}, u32[]{:S(2)}) copy-start(bf16[512]{0:T(512)(128)(2,1)} %param.16) | copy-start | bytes 3076
  35.5 3.4 %copy-start = (bf16[1024,2048]{1,0:T(8,128)(2,1)}, bf16[1024,2048]{1,0:T(8,128)(2,1)S(1)}, u32[]{:S(2)}) copy-start(bf16[1024,2048]{1,0:T(8,128)(2,1)S(1)} %fusion.2.x_ref) | copy-start | bytes 12582916
  115.2 30.3 %copy-start.2 = (bf16[1024,576]{1,0:T(8,128)(2,1)S(1)}, bf16[1024,576]{1,0:T(8,128)(2,1)}, u32[]{:S(2)}) copy-start(bf16[1024,576]{1,0:T(8,128)(2,1)} %get-tuple-element.19.cache_ref) | copy-start | bytes 3538948
  144.9 4.8 %collective-permute-start.2 = (bf16[1024,1024]{1,0:T(8,128)(2,1)}, bf16[1024,1024]{1,0:T(8,128)(2,1)}, u32[]{:S(2)}, u32[]{:S(2)}) collective-permute-start(bf16[1024,1024]{1,0:T(8,128)(2,1)} %get-tuple-element.13), channel_id=1, source_target_pairs={{0,1},{1,0},{2,3},{3,2},{4,5},{5,4},{6,7},{7,6},{8,9},{9,8},{10,11... | collective-permute-start | bytes 6291464 | tf_op jit(solution)/shard_map/ppermute | solution.py:236
Sparse Core Ops, SparseCore 0:
  10.8 83.7 all-gather.1

commit v12 on v9

--- a/solution.py
+++ b/solution.py
@@ -209,10 +209,11 @@
 
 def finish(tokens, mine, received):
     rows, cols = tokens.shape
-    spec = pl.BlockSpec((QBLOCK, cols), lambda i: (i, 0))
+    block = 128
+    spec = pl.BlockSpec((block, cols), lambda i: (i, 0))
     return pl.pallas_call(
         finish_kernel,
-        grid=(rows // QBLOCK,),
+        grid=(rows // block,),
         in_specs=[spec, spec, spec],
         out_specs=spec,
         out_shape=jax.ShapeDtypeStruct((rows, cols), tokens.dtype),

time: 160 us -> 163 us (1.019)
  Pallas kernels: 51.4 us -> 56 us
    pallas_call x1, Pallas kernels: 26.9 us -> 29.6 us  [attend(): pl.pallas_call(attention_kernel, grid_spec=grid_spec, out_shape=[jax.Shap...]
    pallas_call x1, Pallas kernels: 4.83 us -> 6.67 us  [finish(): pl.pallas_call(finish_kernel, grid=(rows // block,), in_specs=[spec, spec...]
where the time goes in v12:
time: 163 us; the launch traced here: 162 us
  waiting for transfers between devices  57.5 us (35%)
  Pallas kernels  56 us (34%)
  between operations  19.3 us (12%)
  local copies, waits for them, and re-layouts  13.6 us (8%)
  other arithmetic  10.3 us (6%)
  matrix products  3.41 us (2%)
  starting transfers between devices  2.14 us (1%)
    all_gather x1, waiting for transfers between devices, body(): joined = lax.all_gather(joined, 'wide', axis=0, tiled=True)  54.7 us
    pallas_call x1, Pallas kernels, attend(): pl.pallas_call(attention_kernel, grid_spec=grid_spec, out_shape=[jax.Shap...  29.6 us
    pallas_call x1, Pallas kernels, project(): pl.pallas_call(project_kernel, grid=(rows // PBLOCK,), in_specs=[part(wid...  19.7 us
    pallas_call x1, Pallas kernels, finish(): pl.pallas_call(finish_kernel, grid=(rows // block,), in_specs=[spec, spec...  6.67 us
    dot_general x1, matrix products, body(): jnp.dot(normed, chosen, preferred_element_type=jnp.float32)  3.41 us
  transfers between devices with their start and end apart: 4, of which 2 were waited for; matrix products, arithmetic and copies ran while one was open for 15% of the time, Pallas kernels for 0%

profile of v12, /device:TPU:1, one launch (start us, length us, event | category | flops | bytes accessed | tf_op | source)
XLA Modules:
  0.0 162.2 jit_solution(731615110292321934)
XLA Ops:
  7.2 0.0 copy-start.3
  7.2 0.0 copy-start.1
  7.2 0.0 copy-start.4
  7.2 0.0 copy-start.6
  7.2 0.0 all-gather.2.cloned.1.call-start
  7.3 1.2 reshape.201
  8.4 0.1 fusion.11
  8.6 0.1 reshape.203
  8.7 0.1 reshape.204
  8.8 1.5 pad_maximum_fusion.4
  10.2 0.0 all-gather.2.cloned.1.call-update
  10.3 0.9 select_reduce_fusion.1
  11.1 0.6 fusion.13
  14.3 2.2 %constant_dynamic-slice_fusion.6 = (bf16[2048,16]{1,0:T(8,128)(2,1)S(1)}, bf16[2048,16]{1,0:T(8,128)(2,1)S(1)}, bf16[2048,16]{1,0:T(8,128)(2,1)S(1)}, bf16[2048,16]{1,0:T(8,128)(2,1)S(1)}) fusion(bf16[2048,512]{1,0:T(8,128)(2,1)} %param.19, s32[]{:T(128)S(6)} %select_n.57, s32[]{:T(128)S(6)} %select_n.58, s32[]{:T(128)S(6)} %select_n.60, s32[]{:T(128)S(6)} %select_n.59), kind=kLoop, calls=%fused_computation.37 | loop fusion | bytes 524304 | tf_op jit(solution)/shard_map/dynamic_slice | solution.py:278
  16.5 1.5 pad_maximum_fusion.1
  18.0 1.4 collective-permute-start.1
  19.4 0.0 copy-done.1
  19.4 0.0 collective-permute-start
  19.4 0.0 copy-done.3
  19.4 0.6 fusion.12
  22.5 0.0 copy-done.4
  22.6 0.1 broadcast_in_dim.16
  22.6 0.1 broadcast_in_dim.17
  22.7 0.0 copy-done.6
  22.7 0.2 reduce-window.4
  22.9 0.9 constant_dynamic-slice_fusion.2
  23.8 0.2 reshape.206
  24.0 0.0 copy-start.5
  24.1 0.1 fusion.10
  24.2 0.1 copy.34
  24.3 0.1 copy.27
  24.4 0.1 copy.35
  24.6 0.1 copy.28
  24.7 0.1 convert_reduce_fusion
  24.8 0.1 select_reduce_fusion
  24.9 0.6 slice.49.first_ref
  25.5 0.5 multiply_sine_fusion
  26.0 0.1 tile.8
  26.2 1.3 copy.30.cos_ref
  27.5 0.1 tile.20
  27.6 1.3 copy.31.sin_ref
  28.9 0.0 copy-done.5
  28.9 0.6 broadcast_in_dim.21
  29.5 1.0 copy.32.kst_ref
  30.5 0.7 pad_maximum_fusion.3.up_ref
  31.2 0.0 collective-permute-done
  31.2 1.9 %broadcast_select_fusion.1 = (bf16[1024,1024]{1,0:T(8,128)(2,1)S(1)}, bf16[1024,1024]{1,0:T(8,128)(2,1)S(1)}) fusion(bf16[1024,1024]{1,0:T(8,128)(2,1)S(1)} %copy-done.1, bf16[1024,1024]{1,0:T(8,128)(2,1)} %collective-permute-done, pred[]{:T(512)S(6)} %eq.56), kind=kLoop, calls=%fused_computation.7 | loop fusion | flops 2097152 | bytes 8388609 | tf_op jit(solution)/shard_map/jit(_where)/select_n | solution.py:267
  33.1 1.0 fusion
  34.1 1.4 fusion.2.x_ref
  35.5 0.0 copy-start
  35.5 0.0 collective-permute-done.1
  35.5 3.4 %fusion.3 = f32[1024,64]{0,1:T(8,128)S(1)} fusion(bf16[1024,2048]{1,0:T(8,128)(2,1)S(1)} %fusion.2.x_ref, bf16[2048,64]{1,0:T(8,128)(2,1)} %pad_maximum_fusion.1, bf16[2048,64]{1,0:T(8,128)(2,1)} %collective-permute-done.1, pred[64]{0:T(512)(128)(4,1)S(1)} %broadcast_in_dim.17), kind=kOutput, calls=%fused_computation.9 | convolution fusion | flops 268566528 | bytes 4980800 | tf_op jit(solution)/shard_map/dot_general | solution.py:293
  39.0 0.0 copy-done
  39.0 0.8 copy.29.sp_ref
  39.9 54.7 %all-gather.2.cloned.1.call-done.w_ref = bf16[2048,2112]{1,0:T(8,128)(2,1)} async-done(((bf16[32,2112]{1,0:T(8,128)(2,1)}), bf16[2048,2112]{1,0:T(8,128)(2,1)}) %all-gather.2.cloned.1.call-update) | async-done | bytes 8650768 | tf_op jit(solution)/shard_map/all_gather | solution.py:263
  94.6 19.7 %shard_map.131 = (bf16[1024,1024]{1,0:T(8,128)(2,1)}, bf16[8,1024,64]{2,1,0:T(8,128)(2,1)}, bf16[1024,576]{1,0:T(8,128)(2,1)}, bf16[1024,2048]{1,0:T(8,128)(2,1)}) custom-call(bf16[1024,2048]{1,0:T(8,128)(2,1)} %copy-done, bf16[2048,2112]{1,0:T(8,128)(2,1)} %all-gather.2.cloned.1.call-done.w_ref, bf16[1024,64]{1,0:T(8,128)(2,1)} %copy.29.sp_ref, ...), custom_call_target="tpu_custom_call" | custom-call | tf_op jit(solution)/shard_map/pallas_call | solution.py:102
  114.3 0.0 copy-start.2
  114.3 29.6 %shard_map.132 = (bf16[1024,1024]{1,0:T(8,128)(2,1)}, bf16[1024,1024]{1,0:T(8,128)(2,1)}) custom-call(s32[1]{0:T(128)} %bitcast.me_ref, s32[4]{0:T(128)} %slice.49.first_ref, bf16[1024,1024]{1,0:T(8,128)(2,1)} %get-tuple-element.8.q_nope_ref, bf16[8,1024,64]{2,1,0:T(8,128)(2,1)} %get-tuple-element.9.qr_ref, bf16[1024,2048]{1,0:T(8,128)(2,1)} %get-tuple-element.10.kv_ref, ...), custom_call_target="tpu_custom_call" | custom-call | tf_op jit(solution)/shard_map/pallas_call | solution.py:195
  143.9 0.7 collective-permute-start.2
  144.6 0.0 copy-done.2
  144.6 1.4 copy.33
  146.0 2.7 %collective-permute-done.2.rec_ref = bf16[1024,1024]{1,0:T(8,128)(2,1)} collective-permute-done((bf16[1024,1024]{1,0:T(8,128)(2,1)}, bf16[1024,1024]{1,0:T(8,128)(2,1)}, u32[]{:S(2)}, u32[]{:S(2)}) %collective-permute-start.2) | collective-permute-done | bytes 2097184 | tf_op jit(solution)/shard_map/ppermute | solution.py:237
  148.7 6.7 %shard_map.133 = bf16[1024,1024]{1,0:T(8,128)(2,1)} custom-call(bf16[1024,1024]{1,0:T(8,128)(2,1)} %tok_ref.1, bf16[1024,1024]{1,0:T(8,128)(2,1)} %get-tuple-element.12.mine_ref, bf16[1024,1024]{1,0:T(8,128)(2,1)} %collective-permute-done.2.rec_ref), custom_call_target="tpu_custom_call" | custom-call | tf_op jit(solution)/shard_map/pallas_call | solution.py:214
  (15 shorter events, 0.2 us)
Async XLA Ops:
  7.2 12.2 %copy-start.3 = (s32[1,4]{1,0:T(1,128)S(1)}, s32[1,4]{1,0:T(1,128)}, u32[]{:S(2)}) copy-start(s32[1,4]{1,0:T(1,128)} %param.22) | copy-start | bytes 52
  7.2 12.2 %copy-start.1 = (bf16[1024,1024]{1,0:T(8,128)(2,1)S(1)}, bf16[1024,1024]{1,0:T(8,128)(2,1)}, u32[]{:S(2)}) copy-start(bf16[1024,1024]{1,0:T(8,128)(2,1)} %tok_ref.1) | copy-start | bytes 6291460
  7.2 15.3 %copy-start.4 = (bf16[2048]{0:T(1024)(128)(2,1)S(1)}, bf16[2048]{0:T(1024)(128)(2,1)}, u32[]{:S(2)}) copy-start(bf16[2048]{0:T(1024)(128)(2,1)} %param.13) | copy-start | bytes 12292
  7.2 15.5 %copy-start.6 = (s32[1,4]{1,0:T(1,128)S(1)}, s32[1,4]{1,0:T(1,128)}, u32[]{:S(2)}) copy-start(s32[1,4]{1,0:T(1,128)} %param.21) | copy-start | bytes 52
  7.2 87.4 %all-gather.2.cloned.1.call-start = ((), (), s32[]{:S(2)}) async-start(), calls=%async_computation | async-start | bytes 9052160 | tf_op jit(solution)/shard_map/all_gather | solution.py:263
  18.0 17.6 %collective-permute-start.1 = (bf16[2048,64]{1,0:T(8,128)(2,1)}, bf16[2048,64]{1,0:T(8,128)(2,1)}, u32[]{:S(2)}, u32[]{:S(2)}) collective-permute-start(bf16[2048,64]{1,0:T(8,128)(2,1)} %pad_maximum_fusion.1), channel_id=1, source_target_pairs={{0,1},{1,0},{2,3},{3,2},{4,5},{5,4},{6,7},{7,6},{8,9},{9,8},{10,11... | collective-permute-start | bytes 786440 | tf_op jit(solution)/shard_map/ppermute | solution.py:237
  19.4 11.9 %collective-permute-start = (bf16[1024,1024]{1,0:T(8,128)(2,1)S(1)}, bf16[1024,1024]{1,0:T(8,128)(2,1)}, u32[]{:S(2)}, u32[]{:S(2)}) collective-permute-start(bf16[1024,1024]{1,0:T(8,128)(2,1)S(1)} %copy-done.1), channel_id=1, source_target_pairs={{0,1},{1,0},{2,3},{3,2},{4,5},{5,4},{6,7},{7,6},{8,9},{9,8},{10,11... | collective-permute-start | bytes 6291464 | tf_op jit(solution)/shard_map/ppermute | solution.py:237
  24.0 4.9 %copy-start.5 = (bf16[512]{0:T(512)(128)(2,1)S(1)}, bf16[512]{0:T(512)(128)(2,1)}, u32[]{:S(2)}) copy-start(bf16[512]{0:T(512)(128)(2,1)} %param.16) | copy-start | bytes 3076
  35.5 3.4 %copy-start = (bf16[1024,2048]{1,0:T(8,128)(2,1)}, bf16[1024,2048]{1,0:T(8,128)(2,1)S(1)}, u32[]{:S(2)}) copy-start(bf16[1024,2048]{1,0:T(8,128)(2,1)S(1)} %fusion.2.x_ref) | copy-start | bytes 12582916
  114.3 30.3 %copy-start.2 = (bf16[1024,576]{1,0:T(8,128)(2,1)S(1)}, bf16[1024,576]{1,0:T(8,128)(2,1)}, u32[]{:S(2)}) copy-start(bf16[1024,576]{1,0:T(8,128)(2,1)} %get-tuple-element.19.cache_ref) | copy-start | bytes 3538948
  143.9 4.8 %collective-permute-start.2 = (bf16[1024,1024]{1,0:T(8,128)(2,1)}, bf16[1024,1024]{1,0:T(8,128)(2,1)}, u32[]{:S(2)}, u32[]{:S(2)}) collective-permute-start(bf16[1024,1024]{1,0:T(8,128)(2,1)} %get-tuple-element.13), channel_id=1, source_target_pairs={{0,1},{1,0},{2,3},{3,2},{4,5},{5,4},{6,7},{7,6},{8,9},{9,8},{10,11... | collective-permute-start | bytes 6291464 | tf_op jit(solution)/shard_map/ppermute | solution.py:237
Sparse Core Ops, SparseCore 0:
  10.8 83.7 all-gather.1

commit v13 on v12

--- a/solution.py
+++ b/solution.py
@@ -209,7 +209,7 @@
 
 def finish(tokens, mine, received):
     rows, cols = tokens.shape
-    block = 128
+    block = 512
     spec = pl.BlockSpec((block, cols), lambda i: (i, 0))
     return pl.pallas_call(
         finish_kernel,

time: 163 us -> 159 us (0.975)
  Pallas kernels: 56 us -> 50.8 us
    pallas_call x1, Pallas kernels: 29.6 us -> 26.9 us  [attend(): pl.pallas_call(attention_kernel, grid_spec=grid_spec, out_shape=[jax.Shap...]
    pallas_call x1, Pallas kernels: 6.67 us -> 4.15 us  [finish(): pl.pallas_call(finish_kernel, grid=(rows // block,), in_specs=[spec, spec...]
  transfers between devices with their start and end apart: 4 -> 4, of which waited for: 2 -> 2; matrix products, arithmetic and copies ran while one was open for 15% -> 16% of each run, Pallas kernels for 0% -> 0%
where the time goes in v13:
time: 159 us; the launch traced here: 157 us
  waiting for transfers between devices  57.4 us (36%)
  Pallas kernels  50.8 us (32%)
  between operations  19.3 us (12%)
  local copies, waits for them, and re-layouts  13.7 us (9%)
  other arithmetic  10.3 us (6%)
  matrix products  3.41 us (2%)
  starting transfers between devices  2.11 us (1%)
    all_gather x1, waiting for transfers between devices, body(): joined = lax.all_gather(joined, 'wide', axis=0, tiled=True)  54.6 us
    pallas_call x1, Pallas kernels, attend(): pl.pallas_call(attention_kernel, grid_spec=grid_spec, out_shape=[jax.Shap...  26.9 us
    pallas_call x1, Pallas kernels, project(): pl.pallas_call(project_kernel, grid=(rows // PBLOCK,), in_specs=[part(wid...  19.7 us
    pallas_call x1, Pallas kernels, finish(): pl.pallas_call(finish_kernel, grid=(rows // block,), in_specs=[spec, spec...  4.15 us
    dot_general x1, matrix products, body(): jnp.dot(normed, chosen, preferred_element_type=jnp.float32)  3.41 us
  transfers between devices with their start and end apart: 4, of which 2 were waited for; matrix products, arithmetic and copies ran while one was open for 16% of the time, Pallas kernels for 0%

profile of v13, /device:TPU:1, one launch (start us, length us, event | category | flops | bytes accessed | tf_op | source)
XLA Modules:
  0.0 156.9 jit_solution(2190986986072504567)
XLA Ops:
  7.2 0.0 copy-start.3
  7.2 0.0 copy-start.1
  7.2 0.0 copy-start.4
  7.2 0.0 copy-start.6
  7.2 0.0 all-gather.2.cloned.1.call-start
  7.3 1.2 reshape.201
  8.4 0.1 fusion.11
  8.6 0.1 reshape.203
  8.7 0.1 reshape.204
  8.8 1.5 pad_maximum_fusion.4
  10.2 0.0 all-gather.2.cloned.1.call-update
  10.3 0.9 select_reduce_fusion.1
  11.1 0.6 fusion.13
  14.3 2.3 %constant_dynamic-slice_fusion.6 = (bf16[2048,16]{1,0:T(8,128)(2,1)S(1)}, bf16[2048,16]{1,0:T(8,128)(2,1)S(1)}, bf16[2048,16]{1,0:T(8,128)(2,1)S(1)}, bf16[2048,16]{1,0:T(8,128)(2,1)S(1)}) fusion(bf16[2048,512]{1,0:T(8,128)(2,1)} %param.19, s32[]{:T(128)S(6)} %select_n.57, s32[]{:T(128)S(6)} %select_n.58, s32[]{:T(128)S(6)} %select_n.60, s32[]{:T(128)S(6)} %select_n.59), kind=kLoop, calls=%fused_computation.37 | loop fusion | bytes 524304 | tf_op jit(solution)/shard_map/dynamic_slice | solution.py:278
  16.5 1.5 pad_maximum_fusion.1
  18.0 1.4 collective-permute-start.1
  19.4 0.0 copy-done.1
  19.4 0.0 collective-permute-start
  19.4 0.0 copy-done.3
  19.4 0.6 fusion.12
  22.6 0.0 copy-done.4
  22.6 0.1 broadcast_in_dim.16
  22.7 0.1 broadcast_in_dim.17
  22.8 0.0 copy-done.6
  22.8 0.2 reduce-window.4
  22.9 0.9 constant_dynamic-slice_fusion.2
  23.9 0.2 reshape.206
  24.1 0.0 copy-start.5
  24.1 0.1 fusion.10
  24.2 0.1 copy.34
  24.4 0.1 copy.27
  24.5 0.1 copy.35
  24.6 0.1 copy.28
  24.7 0.1 convert_reduce_fusion
  24.8 0.1 select_reduce_fusion
  24.9 0.6 slice.49.first_ref
  25.6 0.5 multiply_sine_fusion
  26.1 0.1 tile.8
  26.2 1.3 copy.30.cos_ref
  27.5 0.1 tile.20
  27.6 1.3 copy.31.sin_ref
  29.0 0.0 copy-done.5
  29.0 0.6 broadcast_in_dim.21
  29.6 1.0 copy.32.kst_ref
  30.6 0.7 pad_maximum_fusion.3.up_ref
  31.3 0.0 collective-permute-done
  31.3 1.9 %broadcast_select_fusion.1 = (bf16[1024,1024]{1,0:T(8,128)(2,1)S(1)}, bf16[1024,1024]{1,0:T(8,128)(2,1)S(1)}) fusion(bf16[1024,1024]{1,0:T(8,128)(2,1)S(1)} %copy-done.1, bf16[1024,1024]{1,0:T(8,128)(2,1)} %collective-permute-done, pred[]{:T(512)S(6)} %eq.56), kind=kLoop, calls=%fused_computation.7 | loop fusion | flops 2097152 | bytes 8388609 | tf_op jit(solution)/shard_map/jit(_where)/select_n | solution.py:267
  33.2 1.0 fusion
  34.2 1.4 fusion.2.x_ref
  35.6 0.0 copy-start
  35.6 0.0 collective-permute-done.1
  35.6 3.4 %fusion.3 = f32[1024,64]{0,1:T(8,128)S(1)} fusion(bf16[1024,2048]{1,0:T(8,128)(2,1)S(1)} %fusion.2.x_ref, bf16[2048,64]{1,0:T(8,128)(2,1)} %pad_maximum_fusion.1, bf16[2048,64]{1,0:T(8,128)(2,1)} %collective-permute-done.1, pred[64]{0:T(512)(128)(4,1)S(1)} %broadcast_in_dim.17), kind=kOutput, calls=%fused_computation.9 | convolution fusion | flops 268566528 | bytes 4980800 | tf_op jit(solution)/shard_map/dot_general | solution.py:293
  39.0 0.0 copy-done
  39.1 0.8 copy.29.sp_ref
  39.9 54.6 %all-gather.2.cloned.1.call-done.w_ref = bf16[2048,2112]{1,0:T(8,128)(2,1)} async-done(((bf16[32,2112]{1,0:T(8,128)(2,1)}), bf16[2048,2112]{1,0:T(8,128)(2,1)}) %all-gather.2.cloned.1.call-update) | async-done | bytes 8650768 | tf_op jit(solution)/shard_map/all_gather | solution.py:263
  94.5 19.7 %shard_map.131 = (bf16[1024,1024]{1,0:T(8,128)(2,1)}, bf16[8,1024,64]{2,1,0:T(8,128)(2,1)}, bf16[1024,576]{1,0:T(8,128)(2,1)}, bf16[1024,2048]{1,0:T(8,128)(2,1)}) custom-call(bf16[1024,2048]{1,0:T(8,128)(2,1)} %copy-done, bf16[2048,2112]{1,0:T(8,128)(2,1)} %all-gather.2.cloned.1.call-done.w_ref, bf16[1024,64]{1,0:T(8,128)(2,1)} %copy.29.sp_ref, ...), custom_call_target="tpu_custom_call" | custom-call | tf_op jit(solution)/shard_map/pallas_call | solution.py:102
  114.3 0.0 copy-start.2
  114.3 26.9 %shard_map.132 = (bf16[1024,1024]{1,0:T(8,128)(2,1)}, bf16[1024,1024]{1,0:T(8,128)(2,1)}) custom-call(s32[1]{0:T(128)} %bitcast.me_ref, s32[4]{0:T(128)} %slice.49.first_ref, bf16[1024,1024]{1,0:T(8,128)(2,1)} %get-tuple-element.8.q_nope_ref, bf16[8,1024,64]{2,1,0:T(8,128)(2,1)} %get-tuple-element.9.qr_ref, bf16[1024,2048]{1,0:T(8,128)(2,1)} %get-tuple-element.10.kv_ref, ...), custom_call_target="tpu_custom_call" | custom-call | tf_op jit(solution)/shard_map/pallas_call | solution.py:195
  141.2 0.6 collective-permute-start.2
  141.8 0.0 copy-done.2
  141.8 1.4 copy.33
  143.2 2.7 %collective-permute-done.2.rec_ref = bf16[1024,1024]{1,0:T(8,128)(2,1)} collective-permute-done((bf16[1024,1024]{1,0:T(8,128)(2,1)}, bf16[1024,1024]{1,0:T(8,128)(2,1)}, u32[]{:S(2)}, u32[]{:S(2)}) %collective-permute-start.2) | collective-permute-done | bytes 2097184 | tf_op jit(solution)/shard_map/ppermute | solution.py:237
  145.9 4.1 %shard_map.133 = bf16[1024,1024]{1,0:T(8,128)(2,1)} custom-call(bf16[1024,1024]{1,0:T(8,128)(2,1)} %tok_ref.1, bf16[1024,1024]{1,0:T(8,128)(2,1)} %get-tuple-element.12.mine_ref, bf16[1024,1024]{1,0:T(8,128)(2,1)} %collective-permute-done.2.rec_ref), custom_call_target="tpu_custom_call" | custom-call | tf_op jit(solution)/shard_map/pallas_call | solution.py:214
  (15 shorter events, 0.2 us)
Async XLA Ops:
  7.2 12.3 %copy-start.3 = (s32[1,4]{1,0:T(1,128)S(1)}, s32[1,4]{1,0:T(1,128)}, u32[]{:S(2)}) copy-start(s32[1,4]{1,0:T(1,128)} %param.22) | copy-start | bytes 52
  7.2 12.3 %copy-start.1 = (bf16[1024,1024]{1,0:T(8,128)(2,1)S(1)}, bf16[1024,1024]{1,0:T(8,128)(2,1)}, u32[]{:S(2)}) copy-start(bf16[1024,1024]{1,0:T(8,128)(2,1)} %tok_ref.1) | copy-start | bytes 6291460
  7.2 15.4 %copy-start.4 = (bf16[2048]{0:T(1024)(128)(2,1)S(1)}, bf16[2048]{0:T(1024)(128)(2,1)}, u32[]{:S(2)}) copy-start(bf16[2048]{0:T(1024)(128)(2,1)} %param.13) | copy-start | bytes 12292
  7.2 15.6 %copy-start.6 = (s32[1,4]{1,0:T(1,128)S(1)}, s32[1,4]{1,0:T(1,128)}, u32[]{:S(2)}) copy-start(s32[1,4]{1,0:T(1,128)} %param.21) | copy-start | bytes 52
  7.2 87.3 %all-gather.2.cloned.1.call-start = ((), (), s32[]{:S(2)}) async-start(), calls=%async_computation | async-start | bytes 9052160 | tf_op jit(solution)/shard_map/all_gather | solution.py:263
  18.0 17.6 %collective-permute-start.1 = (bf16[2048,64]{1,0:T(8,128)(2,1)}, bf16[2048,64]{1,0:T(8,128)(2,1)}, u32[]{:S(2)}, u32[]{:S(2)}) collective-permute-start(bf16[2048,64]{1,0:T(8,128)(2,1)} %pad_maximum_fusion.1), channel_id=1, source_target_pairs={{0,1},{1,0},{2,3},{3,2},{4,5},{5,4},{6,7},{7,6},{8,9},{9,8},{10,11... | collective-permute-start | bytes 786440 | tf_op jit(solution)/shard_map/ppermute | solution.py:237
  19.4 11.9 %collective-permute-start = (bf16[1024,1024]{1,0:T(8,128)(2,1)S(1)}, bf16[1024,1024]{1,0:T(8,128)(2,1)}, u32[]{:S(2)}, u32[]{:S(2)}) collective-permute-start(bf16[1024,1024]{1,0:T(8,128)(2,1)S(1)} %copy-done.1), channel_id=1, source_target_pairs={{0,1},{1,0},{2,3},{3,2},{4,5},{5,4},{6,7},{7,6},{8,9},{9,8},{10,11... | collective-permute-start | bytes 6291464 | tf_op jit(solution)/shard_map/ppermute | solution.py:237
  24.1 4.9 %copy-start.5 = (bf16[512]{0:T(512)(128)(2,1)S(1)}, bf16[512]{0:T(512)(128)(2,1)}, u32[]{:S(2)}) copy-start(bf16[512]{0:T(512)(128)(2,1)} %param.16) | copy-start | bytes 3076
  35.6 3.4 %copy-start = (bf16[1024,2048]{1,0:T(8,128)(2,1)}, bf16[1024,2048]{1,0:T(8,128)(2,1)S(1)}, u32[]{:S(2)}) copy-start(bf16[1024,2048]{1,0:T(8,128)(2,1)S(1)} %fusion.2.x_ref) | copy-start | bytes 12582916
  114.3 27.5 %copy-start.2 = (bf16[1024,576]{1,0:T(8,128)(2,1)S(1)}, bf16[1024,576]{1,0:T(8,128)(2,1)}, u32[]{:S(2)}) copy-start(bf16[1024,576]{1,0:T(8,128)(2,1)} %get-tuple-element.19.cache_ref) | copy-start | bytes 3538948
  141.2 4.8 %collective-permute-start.2 = (bf16[1024,1024]{1,0:T(8,128)(2,1)}, bf16[1024,1024]{1,0:T(8,128)(2,1)}, u32[]{:S(2)}, u32[]{:S(2)}) collective-permute-start(bf16[1024,1024]{1,0:T(8,128)(2,1)} %get-tuple-element.13), channel_id=1, source_target_pairs={{0,1},{1,0},{2,3},{3,2},{4,5},{5,4},{6,7},{7,6},{8,9},{9,8},{10,11... | collective-permute-start | bytes 6291464 | tf_op jit(solution)/shard_map/ppermute | solution.py:237
Sparse Core Ops, SparseCore 0:
  10.8 83.6 all-gather.1
